TPU v7x, 512 devices: a whole 4x4x16 slice. The times are simulated.
512 devices in a mesh: az: 128 (over x, z_lo, y), rad: 4 (over z_hi, core).
Axes of the slice: x: 4, y: 4, z: 16 (z_hi: 2, z_lo: 8; z = z_hi * 8 + z_lo), core: 2. Of those that a mesh axis runs over, the one named last changes fastest.
Arguments:
- block_mass: float32 [128, 4, 512, 128], P('az', 'rad'), may hold values from 0.5 to 4
- block_flux: float32 [128, 4, 512, 9, 128], P('az', 'rad'), may hold values from -6 to 6
- block_dest: int32 [128, 4, 512], P('az', 'rad'), may hold values from 0 to 32767, as said below
- block_count: int32 [128, 4], P('az', 'rad'), may hold values from 128 to 512, as said below
Outputs:
- smoothed: float32 [10, 1024, 32, 512], P(None, 'az', None, 'rad')
- force: float32 [3, 1024, 32, 512], P(None, 'az', None, 'rad')
- strain: float32 [6, 1024, 32, 512], P(None, 'az', None, 'rad')
Inputs may be any that keep to these rules, and one draw needn't show every extreme that they name: `block_dest`: the azimuthal row of a block of device (a, b) lies from 2 rows before to 2 rows after the rows a * 8 to a * 8 + 7, cyclically over 1024 rows. `block_count`: some device is full in every draw.
All inputs are finite; a program needn't handle non-finite values.
Results may differ from a plain program's by a relative error of at most 0.000076.
Values sent between devices are 32-bit elements; how exact they have to be, the bound alone decides.
No kernel may reach another device: no remote copies, remote signals or barrier semaphores. Data moves between devices by JAX's collectives and lax.ppermute only.
A program may use at most 64 MiB of HBM per device.

v0:
```python
import math

import jax
import jax.numpy as jnp
from jax import lax
from jax.sharding import PartitionSpec as P

CA = 8
H = 32


density_base = 0.5


def passed_along(value, axis, steps):
    count = lax.axis_size(axis)
    pairs = [(source, (source + steps) % count) for source in range(count)]
    return lax.ppermute(value, axis, pairs)


def padded_2(cells, sides, width):
    for axis, dim in sides:
        count = lax.axis_size(axis)
        head = lax.slice_in_dim(cells, 0, width, axis=dim)
        tail = lax.slice_in_dim(cells, cells.shape[dim] - width, cells.shape[dim], axis=dim)
        cells = jnp.concatenate(
            [
                lax.ppermute(tail, axis, [(i, (i + 1) % count) for i in range(count)]),
                cells,
                lax.ppermute(head, axis, [((i + 1) % count, i) for i in range(count)]),
            ],
            axis=dim,
        )
    return cells


def smooth_block(extended):
    fields = 0.25 * extended[:, :-2] + 0.5 * extended[:, 1:-1] + 0.25 * extended[:, 2:]
    fields = 0.25 * fields[..., :-2] + 0.5 * fields[..., 1:-1] + 0.25 * fields[..., 2:]
    padded = jnp.pad(fields, ((0, 0), (0, 0), (1, 1), (0, 0)))
    return 0.25 * padded[:, :, :-2] + 0.5 * padded[:, :, 1:-1] + 0.25 * padded[:, :, 2:]


def radial_mask(extended, depth, band_index, width, n_rad):
    columns = band_index * width - depth + jnp.arange(width + 2 * depth, dtype=jnp.int32)
    inside = (columns >= 0) & (columns < width * n_rad)
    return extended * inside.astype(jnp.float32)


def gradients(extended, scale_az):
    center = extended[:, 1:-1, :, 1:-1]
    grad_az = (extended[:, 2:, :, 1:-1] - extended[:, :-2, :, 1:-1]) * scale_az
    grad_rad = (extended[:, 1:-1, :, 2:] - extended[:, 1:-1, :, :-2]) * 0.5
    padded = jnp.pad(center, ((0, 0), (0, 0), (1, 1), (0, 0)))
    grad_height = (padded[:, :, 2:] - padded[:, :, :-2]) * 0.5
    return (grad_az, grad_height, grad_rad, center)


def assemble(grad_az, grad_height, grad_rad, center, recip):
    force = jnp.stack(
        [
            grad_az[3] + grad_height[6] + grad_rad[7] + 2.0 * center[7] * recip,
            grad_az[6] + grad_height[4] + grad_rad[8],
            grad_az[7] + grad_height[8] + grad_rad[5] + (center[5] - center[3]) * recip,
        ]
    )
    strain = jnp.stack(
        [
            grad_az[0] + center[2] * recip,
            grad_height[1],
            grad_rad[2],
            0.5 * (grad_height[0] + grad_az[1]),
            0.5 * (grad_rad[0] + grad_az[2] - center[0] * recip),
            0.5 * (grad_rad[1] + grad_height[2]),
        ]
    )
    return (force, strain)


def deposit(onehot, values):
    return jnp.einsum("ls,scn->cln", onehot, values, precision=lax.Precision.HIGHEST)


def local_rows(values, dest, live, start, total_rows, width):
    local_row = jnp.mod(dest // H - start + 2, total_rows)
    line = local_row * H + dest % H
    onehot = (
        (jnp.arange((CA + 4) * H, dtype=jnp.int32)[:, None] == line[None, :]) & live[None, :]
    ).astype(jnp.float32)
    return deposit(onehot, values).reshape(10, CA + 4, H, width)


def local(block_mass, block_flux, block_dest, block_count):
    sector = lax.axis_index("az")
    band_index = lax.axis_index("rad")
    n_az = lax.axis_size("az")
    n_rad = lax.axis_size("rad")
    slots = block_mass.shape[2]
    width = block_mass.shape[3]
    total_rows = CA * n_az
    start = sector * CA
    values = jnp.concatenate([block_mass[0, 0][:, None, :], block_flux[0, 0]], axis=1)
    dest = block_dest[0, 0]
    slot_index = jnp.arange(slots, dtype=jnp.int32)
    live = slot_index < block_count[0, 0]
    extended = local_rows(values, dest, live, start, total_rows, width)
    from_left = passed_along(extended[:, CA + 2 :], "az", 1)
    from_right = passed_along(extended[:, :2], "az", -1)
    fields = extended[:, 2 : CA + 2]
    fields = fields.at[:, :2].add(from_left)
    fields = fields.at[:, CA - 2 :].add(from_right)
    glob_cells = (band_index * width + jnp.arange(width, dtype=jnp.int32)).astype(jnp.float32)
    radius = width * n_rad + glob_cells + 0.5
    dtheta = 2.0 * math.pi / total_rows
    scale_az = 0.5 / (radius * dtheta)
    recip = 1.0 / radius
    extended = padded_2(fields, (("az", 1), ("rad", 3)), 1)
    extended = radial_mask(extended, 1, band_index, width, n_rad)
    smoothed = smooth_block(extended)
    velocity = smoothed[1:4] / (smoothed[0:1] + density_base)
    combined = jnp.concatenate([velocity, smoothed[4:]], axis=0)
    outer = padded_2(combined, (("az", 1), ("rad", 3)), 1)
    outer = radial_mask(outer, 1, band_index, width, n_rad)
    grad_az, grad_height, grad_rad, center = gradients(outer, scale_az)
    force, strain = assemble(grad_az, grad_height, grad_rad, center, recip)
    return (smoothed, force, strain)


def solution(mesh):
    return jax.shard_map(
        local,
        mesh=mesh,
        in_specs=(
            P("az", "rad", None, None),
            P("az", "rad", None, None, None),
            P("az", "rad", None),
            P("az", "rad"),
        ),
        out_specs=(
            P(None, "az", None, "rad"),
            P(None, "az", None, "rad"),
            P(None, "az", None, "rad"),
        ),
        check_vma=False,
    )
```

profile of v0, /device:TPU:254, one launch (start us, length us, event | category | flops | bytes accessed | tf_op | source)
XLA Modules:
  0.0 153.4 jit_solution(9077222845982300074)
XLA Ops:
  1.3 1.1 copy.16
  2.4 2.1 %copy.17 = f32[1,1,512,9,128]{2,4,3,1,0:T(8,128)S(1)} copy(f32[1,1,512,9,128]{4,2,3,1,0:T(8,128)} %param.9) | data formatting | bytes 4718592 | tf_op args[1]
  4.5 3.5 %fusion.6 = f32[10,384,128]{1,2,0:T(8,128)} fusion(f32[512,9,128]{0,2,1:T(8,128)S(1)} %bitcast.13, f32[512,1,128]{0,2,1:T(8,128)S(1)} %bitcast.17, s32[512]{0:T(512)S(1)} %fusion.42, pred[512]{0:T(512)(128)(4,1)S(1)} %iota_compare_fusion.1), kind=kOutput, calls=%fused_computation.14 | convolution fusion | flops 3020947456 | bytes 4590080 | tf_op jit(solution)/shard_map/ls,scn->cln/dot_general | solution.py:81
  8.0 1.9 %copy.18 = f32[10,384,128]{2,1,0:T(8,128)S(1)} copy(f32[10,384,128]{1,2,0:T(8,128)} %fusion.6) | data formatting | bytes 3932160 | tf_op jit(solution)/shard_map/ls,scn->cln/transpose | solution.py:81
  10.0 4.2 %collective-permute-start = (f32[10,2,32,128]{3,2,1,0:T(8,128)S(1)}, f32[10,2,32,128]{3,2,1,0:T(8,128)S(1)}, u32[]{:S(2)}, u32[]{:S(2)}) collective-permute-start(f32[10,2,32,128]{3,2,1,0:T(8,128)S(1)} %get-tuple-element.37), channel_id=1, source_target_pairs={{0,4},{4,8},{8,12},{12,16},{16,20},{20,24},{24,28},{28,32},{32,36}... | collective-permute-start | bytes 983048 | tf_op jit(solution)/shard_map/ppermute | solution.py:18
  14.2 1.9 %collective-permute-start.1 = (f32[10,2,32,128]{3,2,1,0:T(8,128)S(1)}, f32[10,2,32,128]{3,2,1,0:T(8,128)S(1)}, u32[]{:S(2)}, u32[]{:S(2)}) collective-permute-start(f32[10,2,32,128]{3,2,1,0:T(8,128)S(1)} %get-tuple-element.36), channel_id=1, source_target_pairs={{0,508},{4,0},{8,4},{12,8},{16,12},{20,16},{24,20},{28,24},{32,28}... | collective-permute-start | bytes 983048 | tf_op jit(solution)/shard_map/ppermute | solution.py:18
  16.1 0.1 slice.276
  16.2 5.1 %collective-permute-done = f32[10,2,32,128]{3,2,1,0:T(8,128)S(1)} collective-permute-done((f32[10,2,32,128]{3,2,1,0:T(8,128)S(1)}, f32[10,2,32,128]{3,2,1,0:T(8,128)S(1)}, u32[]{:S(2)}, u32[]{:S(2)}) %collective-permute-start) | collective-permute-done | bytes 327712 | tf_op jit(solution)/shard_map/ppermute | solution.py:18
  21.4 12.7 %collective-permute-done.1 = f32[10,2,32,128]{3,2,1,0:T(8,128)S(1)} collective-permute-done((f32[10,2,32,128]{3,2,1,0:T(8,128)S(1)}, f32[10,2,32,128]{3,2,1,0:T(8,128)S(1)}, u32[]{:S(2)}, u32[]{:S(2)}) %collective-permute-start.1) | collective-permute-done | bytes 327712 | tf_op jit(solution)/shard_map/ppermute | solution.py:18
  34.1 0.1 constant_dynamic-update-slice_fusion
  34.2 1.9 %collective-permute-start.3 = (f32[10,1,32,128]{3,2,1,0:T(8,128)S(1)}, f32[10,1,32,128]{3,2,1,0:T(8,128)S(1)}, u32[]{:S(2)}, u32[]{:S(2)}) collective-permute-start(f32[10,1,32,128]{3,2,1,0:T(8,128)S(1)} %slice.282), channel_id=1, source_target_pairs={{4,0},{8,4},{12,8},{16,12},{20,16},{24,20},{28,24},{32,28},{36,32}... | collective-permute-start | bytes 491528 | tf_op jit(solution)/shard_map/ppermute | solution.py:30
  36.2 14.7 %collective-permute-start.2 = (f32[10,1,32,128]{3,2,1,0:T(8,128)S(1)}, f32[10,1,32,128]{3,2,1,0:T(8,128)S(1)}, u32[]{:S(2)}, u32[]{:S(2)}) collective-permute-start(f32[10,1,32,128]{3,2,1,0:T(8,128)S(1)} %slice.281), channel_id=1, source_target_pairs={{0,4},{4,8},{8,12},{12,16},{16,20},{20,24},{24,28},{28,32},{32,36}... | collective-permute-start | bytes 491528 | tf_op jit(solution)/shard_map/ppermute | solution.py:28
  50.9 1.3 collective-permute-done.3
  52.3 1.5 collective-permute-done.2
  53.7 0.2 pad_maximum_fusion
  53.9 1.8 %fusion.47 = (f32[10,10,32,1]{3,2,1,0:T(8,128)}, f32[10,10,32,1]{3,2,1,0:T(8,128)S(1)}) fusion(f32[10,10,32,128]{3,2,1,0:T(8,128)S(1)} %pad_maximum_fusion), kind=kLoop, calls=%fused_computation.98 | loop fusion | bytes 51200 | tf_op jit(solution)/shard_map/slice | solution.py:25
  55.7 2.1 %copy.19 = f32[10,10,32,1]{2,3,1,0:T(1,128)S(1)} copy(f32[10,10,32,1]{3,2,1,0:T(8,128)} %get-tuple-element.38) | data formatting | bytes 25600 | tf_op jit(solution)/shard_map/slice | solution.py:25
  57.7 0.7 copy.20
  58.4 11.2 %collective-permute-start.5 = (f32[10,10,32,1]{2,3,1,0:T(1,128)S(1)}, f32[10,10,32,1]{2,3,1,0:T(1,128)S(1)}, u32[]{:S(2)}, u32[]{:S(2)}) collective-permute-start(f32[10,10,32,1]{2,3,1,0:T(1,128)S(1)} %copy.20), channel_id=1, source_target_pairs={{1,0},{2,1},{3,2},{0,3},{5,4},{6,5},{7,6},{4,7},{9,8},{10,9},{11,1... | collective-permute-start | bytes 38408 | tf_op jit(solution)/shard_map/ppermute | solution.py:30
  69.6 1.9 %collective-permute-start.4 = (f32[10,10,32,1]{2,3,1,0:T(1,128)S(1)}, f32[10,10,32,1]{2,3,1,0:T(1,128)S(1)}, u32[]{:S(2)}, u32[]{:S(2)}) collective-permute-start(f32[10,10,32,1]{2,3,1,0:T(1,128)S(1)} %copy.19), channel_id=1, source_target_pairs={{0,1},{1,2},{2,3},{3,0},{4,5},{5,6},{6,7},{7,4},{8,9},{9,10},{10,1... | collective-permute-start | bytes 38408 | tf_op jit(solution)/shard_map/ppermute | solution.py:28
  71.5 12.2 %collective-permute-done.4 = f32[10,10,32,1]{2,3,1,0:T(1,128)S(1)} collective-permute-done((f32[10,10,32,1]{2,3,1,0:T(1,128)S(1)}, f32[10,10,32,1]{2,3,1,0:T(1,128)S(1)}, u32[]{:S(2)}, u32[]{:S(2)}) %collective-permute-start.4) | collective-permute-done | bytes 12832 | tf_op jit(solution)/shard_map/ppermute | solution.py:28
  83.7 0.7 copy.21
  84.4 1.8 %copy.22 = f32[10,10,32,1]{3,2,1,0:T(8,128)} copy(f32[10,10,32,1]{2,3,1,0:T(1,128)S(1)} %collective-permute-done.5) | data formatting | bytes 25600 | tf_op jit(solution)/shard_map/ppermute | solution.py:30
  86.2 2.8 %maximum_multiply_fusion = f32[10,10,32,130]{3,2,1,0:T(8,128)S(1)} fusion(f32[10,10,32,1]{3,2,1,0:T(8,128)} %copy.22, f32[10,1,32,128]{3,2,1,0:T(8,128)S(1)} %collective-permute-done.3, f32[10,8,32,128]{3,2,1,0:T(8,128)S(1)} %get-tuple-element.27, f32[10,1,32,128]{3,2,1,0:T(8,128)S(1)} %collective-permute-done.2, f32[10,10,32,1]{3,2,1,0:T(8,128)S(1)} %copy.21, ...), kind=kLoop, calls=%fused_computation | loop fusion | flops 2080000 | bytes 3328520 | tf_op jit(solution)/shard_map/mul | solution.py:47
  89.0 0.6 fusion
  89.6 0.7 fusion.13
  90.4 0.4 fusion.11
  91.0 0.9 copy-done
  91.8 15.4 %collective-permute-start.6 = (f32[9,1,32,128]{3,2,1,0:T(8,128)S(1)}, f32[9,1,32,128]{3,2,1,0:T(8,128)S(1)}, u32[]{:S(2)}, u32[]{:S(2)}) collective-permute-start(f32[9,1,32,128]{3,2,1,0:T(8,128)S(1)} %get-tuple-element.42), channel_id=1, source_target_pairs={{0,4},{4,8},{8,12},{12,16},{16,20},{20,24},{24,28},{28,32},{32,36}... | collective-permute-start | bytes 442376 | tf_op jit(solution)/shard_map/ppermute | solution.py:28
  107.2 1.9 %collective-permute-start.7 = (f32[9,1,32,128]{3,2,1,0:T(8,128)S(1)}, f32[9,1,32,128]{3,2,1,0:T(8,128)S(1)}, u32[]{:S(2)}, u32[]{:S(2)}) collective-permute-start(f32[9,1,32,128]{3,2,1,0:T(8,128)S(1)} %get-tuple-element.43), channel_id=1, source_target_pairs={{4,0},{8,4},{12,8},{16,12},{20,16},{24,20},{28,24},{32,28},{36,32}... | collective-permute-start | bytes 442376 | tf_op jit(solution)/shard_map/ppermute | solution.py:30
  109.2 0.7 collective-permute-done.6
  109.9 15.2 %collective-permute-done.7 = f32[9,1,32,128]{3,2,1,0:T(8,128)S(1)} collective-permute-done((f32[9,1,32,128]{3,2,1,0:T(8,128)S(1)}, f32[9,1,32,128]{3,2,1,0:T(8,128)S(1)}, u32[]{:S(2)}, u32[]{:S(2)}) %collective-permute-start.7) | collective-permute-done | bytes 147488 | tf_op jit(solution)/shard_map/ppermute | solution.py:30
  125.1 0.1 pad_maximum_fusion.1
  125.2 1.7 %fusion.48 = (f32[9,10,32,1]{3,2,1,0:T(8,128)}, f32[9,10,32,1]{3,2,1,0:T(8,128)S(1)}) fusion(f32[9,10,32,128]{3,2,1,0:T(8,128)S(1)} %pad_maximum_fusion.1), kind=kLoop, calls=%fused_computation.99 | loop fusion | bytes 46080 | tf_op jit(solution)/shard_map/slice | solution.py:25
  126.9 2.0 %copy.23 = f32[9,10,32,1]{2,3,1,0:T(1,128)S(1)} copy(f32[9,10,32,1]{3,2,1,0:T(8,128)} %get-tuple-element.40) | data formatting | bytes 23040 | tf_op jit(solution)/shard_map/slice | solution.py:25
  128.8 0.6 copy.24
  129.4 1.9 %collective-permute-start.9 = (f32[9,10,32,1]{2,3,1,0:T(1,128)S(1)}, f32[9,10,32,1]{2,3,1,0:T(1,128)S(1)}, u32[]{:S(2)}, u32[]{:S(2)}) collective-permute-start(f32[9,10,32,1]{2,3,1,0:T(1,128)S(1)} %copy.24), channel_id=1, source_target_pairs={{1,0},{2,1},{3,2},{0,3},{5,4},{6,5},{7,6},{4,7},{9,8},{10,9},{11,1... | collective-permute-start | bytes 34568 | tf_op jit(solution)/shard_map/ppermute | solution.py:30
  131.4 2.6 %collective-permute-start.8 = (f32[9,10,32,1]{2,3,1,0:T(1,128)S(1)}, f32[9,10,32,1]{2,3,1,0:T(1,128)S(1)}, u32[]{:S(2)}, u32[]{:S(2)}) collective-permute-start(f32[9,10,32,1]{2,3,1,0:T(1,128)S(1)} %copy.23), channel_id=1, source_target_pairs={{0,1},{1,2},{2,3},{3,0},{4,5},{5,6},{6,7},{7,4},{8,9},{9,10},{10,1... | collective-permute-start | bytes 34568 | tf_op jit(solution)/shard_map/ppermute | solution.py:28
  134.0 11.5 %collective-permute-done.8 = f32[9,10,32,1]{2,3,1,0:T(1,128)S(1)} collective-permute-done((f32[9,10,32,1]{2,3,1,0:T(1,128)S(1)}, f32[9,10,32,1]{2,3,1,0:T(1,128)S(1)}, u32[]{:S(2)}, u32[]{:S(2)}) %collective-permute-start.8) | collective-permute-done | bytes 11552 | tf_op jit(solution)/shard_map/ppermute | solution.py:28
  145.4 0.6 copy.25
  146.1 1.7 %copy.26 = f32[9,10,32,1]{3,2,1,0:T(8,128)} copy(f32[9,10,32,1]{2,3,1,0:T(1,128)S(1)} %collective-permute-done.9) | data formatting | bytes 23040 | tf_op jit(solution)/shard_map/ppermute | solution.py:30
  147.8 2.6 %maximum_multiply_fusion.1 = f32[9,10,32,130]{3,2,1,0:T(8,128)S(1)} fusion(f32[9,10,32,1]{3,2,1,0:T(8,128)} %copy.26, f32[9,1,32,128]{3,2,1,0:T(8,128)S(1)} %collective-permute-done.7, f32[6,8,32,128]{3,2,1,0:T(8,128)S(1)} %slice.293, f32[3,8,32,128]{3,2,1,0:T(8,128)S(1)} %slice_divide_fusion, f32[9,1,32,128]{3,2,1,0:T(8,128)S(1)} %collective-permute-done.6, ...), kind=kLoop, calls=%fused_computation.1 | loop fusion | flops 2246400 | bytes 2995720 | tf_op jit(solution)/shard_map/mul | solution.py:47
  150.4 1.3 fusion.18
  151.7 0.3 fusion.16
  151.9 0.1 fusion.33
  152.1 0.2 fusion.36
  152.4 0.8 pad_maximum_fusion.2
  153.2 0.2 copy-done.1
  (23 shorter events, 0.4 us)
Async XLA Ops:
  2.4 2.1 %copy-start.2 = (s32[1,1,512]{2,1,0:T(1,128)S(1)}, s32[1,1,512]{2,1,0:T(1,128)}, u32[]{:S(2)}) copy-start(s32[1,1,512]{2,1,0:T(1,128)} %param.10) | copy-start | bytes 6148
  10.0 11.3 %collective-permute-start = (f32[10,2,32,128]{3,2,1,0:T(8,128)S(1)}, f32[10,2,32,128]{3,2,1,0:T(8,128)S(1)}, u32[]{:S(2)}, u32[]{:S(2)}) collective-permute-start(f32[10,2,32,128]{3,2,1,0:T(8,128)S(1)} %get-tuple-element.37), channel_id=1, source_target_pairs={{0,4},{4,8},{8,12},{12,16},{16,20},{20,24},{24,28},{28,32},{32,36}... | collective-permute-start | bytes 983048 | tf_op jit(solution)/shard_map/ppermute | solution.py:18
  14.2 19.9 %collective-permute-start.1 = (f32[10,2,32,128]{3,2,1,0:T(8,128)S(1)}, f32[10,2,32,128]{3,2,1,0:T(8,128)S(1)}, u32[]{:S(2)}, u32[]{:S(2)}) collective-permute-start(f32[10,2,32,128]{3,2,1,0:T(8,128)S(1)} %get-tuple-element.36), channel_id=1, source_target_pairs={{0,508},{4,0},{8,4},{12,8},{16,12},{20,16},{24,20},{28,24},{32,28}... | collective-permute-start | bytes 983048 | tf_op jit(solution)/shard_map/ppermute | solution.py:18
  34.2 18.0 %collective-permute-start.3 = (f32[10,1,32,128]{3,2,1,0:T(8,128)S(1)}, f32[10,1,32,128]{3,2,1,0:T(8,128)S(1)}, u32[]{:S(2)}, u32[]{:S(2)}) collective-permute-start(f32[10,1,32,128]{3,2,1,0:T(8,128)S(1)} %slice.282), channel_id=1, source_target_pairs={{4,0},{8,4},{12,8},{16,12},{20,16},{24,20},{28,24},{32,28},{36,32}... | collective-permute-start | bytes 491528 | tf_op jit(solution)/shard_map/ppermute | solution.py:30
  36.2 17.6 %collective-permute-start.2 = (f32[10,1,32,128]{3,2,1,0:T(8,128)S(1)}, f32[10,1,32,128]{3,2,1,0:T(8,128)S(1)}, u32[]{:S(2)}, u32[]{:S(2)}) collective-permute-start(f32[10,1,32,128]{3,2,1,0:T(8,128)S(1)} %slice.281), channel_id=1, source_target_pairs={{0,4},{4,8},{8,12},{12,16},{16,20},{20,24},{24,28},{28,32},{32,36}... | collective-permute-start | bytes 491528 | tf_op jit(solution)/shard_map/ppermute | solution.py:28
  58.4 26.0 %collective-permute-start.5 = (f32[10,10,32,1]{2,3,1,0:T(1,128)S(1)}, f32[10,10,32,1]{2,3,1,0:T(1,128)S(1)}, u32[]{:S(2)}, u32[]{:S(2)}) collective-permute-start(f32[10,10,32,1]{2,3,1,0:T(1,128)S(1)} %copy.20), channel_id=1, source_target_pairs={{1,0},{2,1},{3,2},{0,3},{5,4},{6,5},{7,6},{4,7},{9,8},{10,9},{11,1... | collective-permute-start | bytes 38408 | tf_op jit(solution)/shard_map/ppermute | solution.py:30
  69.6 14.1 %collective-permute-start.4 = (f32[10,10,32,1]{2,3,1,0:T(1,128)S(1)}, f32[10,10,32,1]{2,3,1,0:T(1,128)S(1)}, u32[]{:S(2)}, u32[]{:S(2)}) collective-permute-start(f32[10,10,32,1]{2,3,1,0:T(1,128)S(1)} %copy.19), channel_id=1, source_target_pairs={{0,1},{1,2},{2,3},{3,0},{4,5},{5,6},{6,7},{7,4},{8,9},{9,10},{10,1... | collective-permute-start | bytes 38408 | tf_op jit(solution)/shard_map/ppermute | solution.py:28
  90.8 1.1 copy-start
  91.8 18.0 %collective-permute-start.6 = (f32[9,1,32,128]{3,2,1,0:T(8,128)S(1)}, f32[9,1,32,128]{3,2,1,0:T(8,128)S(1)}, u32[]{:S(2)}, u32[]{:S(2)}) collective-permute-start(f32[9,1,32,128]{3,2,1,0:T(8,128)S(1)} %get-tuple-element.42), channel_id=1, source_target_pairs={{0,4},{4,8},{8,12},{12,16},{16,20},{20,24},{24,28},{28,32},{32,36}... | collective-permute-start | bytes 442376 | tf_op jit(solution)/shard_map/ppermute | solution.py:28
  107.2 17.9 %collective-permute-start.7 = (f32[9,1,32,128]{3,2,1,0:T(8,128)S(1)}, f32[9,1,32,128]{3,2,1,0:T(8,128)S(1)}, u32[]{:S(2)}, u32[]{:S(2)}) collective-permute-start(f32[9,1,32,128]{3,2,1,0:T(8,128)S(1)} %get-tuple-element.43), channel_id=1, source_target_pairs={{4,0},{8,4},{12,8},{16,12},{20,16},{24,20},{28,24},{32,28},{36,32}... | collective-permute-start | bytes 442376 | tf_op jit(solution)/shard_map/ppermute | solution.py:30
  129.4 16.6 %collective-permute-start.9 = (f32[9,10,32,1]{2,3,1,0:T(1,128)S(1)}, f32[9,10,32,1]{2,3,1,0:T(1,128)S(1)}, u32[]{:S(2)}, u32[]{:S(2)}) collective-permute-start(f32[9,10,32,1]{2,3,1,0:T(1,128)S(1)} %copy.24), channel_id=1, source_target_pairs={{1,0},{2,1},{3,2},{0,3},{5,4},{6,5},{7,6},{4,7},{9,8},{10,9},{11,1... | collective-permute-start | bytes 34568 | tf_op jit(solution)/shard_map/ppermute | solution.py:30
  131.4 14.1 %collective-permute-start.8 = (f32[9,10,32,1]{2,3,1,0:T(1,128)S(1)}, f32[9,10,32,1]{2,3,1,0:T(1,128)S(1)}, u32[]{:S(2)}, u32[]{:S(2)}) collective-permute-start(f32[9,10,32,1]{2,3,1,0:T(1,128)S(1)} %copy.23), channel_id=1, source_target_pairs={{0,1},{1,2},{2,3},{3,0},{4,5},{5,6},{6,7},{7,4},{8,9},{9,10},{10,1... | collective-permute-start | bytes 34568 | tf_op jit(solution)/shard_map/ppermute | solution.py:28
  152.4 1.0 copy-start.1
where the time goes:
time: 154 us; the launch traced here: 153 us
  waiting for transfers between devices  60.2 us (39%)
  starting transfers between devices  57.7 us (37%)
  local copies, waits for them, and re-layouts  19.9 us (13%)
  other arithmetic  10.4 us (7%)
  matrix products  3.53 us (2%)
  between operations  1.62 us (1%)
    ppermute x4, starting transfers between devices, padded_2(): lax.ppermute(tail, axis, [(i, (i + 1) % count) for i in range(count)])  34.6 us
    ppermute x4, waiting for transfers between devices, padded_2(): lax.ppermute(tail, axis, [(i, (i + 1) % count) for i in range(count)])  25.9 us
    ppermute x2, waiting for transfers between devices, passed_along(): return lax.ppermute(value, axis, pairs)  17.8 us
    ppermute x4, starting transfers between devices, padded_2(): lax.ppermute(head, axis, [((i + 1) % count, i) for i in range(count)])  16.9 us
    ppermute x4, waiting for transfers between devices, padded_2(): lax.ppermute(head, axis, [((i + 1) % count, i) for i in range(count)])  16.6 us
    slice x5, local copies, waits for them, and re-layouts, padded_2(): lax.slice_in_dim(cells, cells.shape[dim] - width, cells.shape[dim], axis=...  7.45 us
    ppermute x2, starting transfers between devices, passed_along(): return lax.ppermute(value, axis, pairs)  6.13 us
    mul x2, other arithmetic, radial_mask(): return extended * inside.astype(jnp.float32)  5.34 us
  transfers between devices with their start and end apart: 10, of which 8 were waited for; matrix products, arithmetic and copies ran while one was open for 1% of the time, Pallas kernels for 0%

commit v1 on v0

--- a/solution.py
+++ b/solution.py
@@ -7,31 +7,63 @@
 
 CA = 8
 H = 32
+HALO = 2
 
 
 density_base = 0.5
 
 
-def passed_along(value, axis, steps):
-    count = lax.axis_size(axis)
-    pairs = [(source, (source + steps) % count) for source in range(count)]
-    return lax.ppermute(value, axis, pairs)
+def shifted(value, da, db):
+    n_az = lax.axis_size("az")
+    n_rad = lax.axis_size("rad")
+    pairs = []
+    for a in range(n_az):
+        for b in range(n_rad):
+            tb = b + db
+            if 0 <= tb < n_rad:
+                pairs.append((a * n_rad + b, ((a + da) % n_az) * n_rad + tb))
+    return lax.ppermute(value, ("az", "rad"), pairs)
 
 
-def padded_2(cells, sides, width):
-    for axis, dim in sides:
-        count = lax.axis_size(axis)
-        head = lax.slice_in_dim(cells, 0, width, axis=dim)
-        tail = lax.slice_in_dim(cells, cells.shape[dim] - width, cells.shape[dim], axis=dim)
-        cells = jnp.concatenate(
-            [
-                lax.ppermute(tail, axis, [(i, (i + 1) % count) for i in range(count)]),
-                cells,
-                lax.ppermute(head, axis, [((i + 1) % count, i) for i in range(count)]),
-            ],
-            axis=dim,
-        )
-    return cells
+def deposit(onehot, values):
+    return jnp.einsum("ls,scn->cln", onehot, values, precision=lax.Precision.HIGHEST)
+
+
+def local_rows(values, dest, live, start, total_rows, width):
+    local_row = jnp.mod(dest // H - start + HALO, total_rows)
+    line = local_row * H + dest % H
+    onehot = (
+        (jnp.arange((CA + 2 * HALO) * H, dtype=jnp.int32)[:, None] == line[None, :]) & live[None, :]
+    ).astype(jnp.float32)
+    return deposit(onehot, values).reshape(10, CA + 2 * HALO, H, width)
+
+
+def add_rows(base, head, tail):
+    k = head.shape[1]
+    rows = base.shape[1]
+    return jnp.concatenate(
+        [base[:, :k] + head, base[:, k : rows - k], base[:, rows - k :] + tail], axis=1
+    )
+
+
+def window(raw):
+    k = 2 * HALO
+    top = raw[:, :k]
+    bottom = raw[:, -k:]
+    center = add_rows(raw, shifted(bottom, 1, 0), shifted(top, -1, 0))
+    lo = slice(0, HALO)
+    hi = slice(raw.shape[3] - HALO, raw.shape[3])
+    right = add_rows(
+        shifted(raw[..., lo], 0, -1),
+        shifted(bottom[..., lo], 1, -1),
+        shifted(top[..., lo], -1, -1),
+    )
+    left = add_rows(
+        shifted(raw[..., hi], 0, 1),
+        shifted(bottom[..., hi], 1, 1),
+        shifted(top[..., hi], -1, 1),
+    )
+    return jnp.concatenate([left, center, right], axis=3)
 
 
 def smooth_block(extended):
@@ -77,19 +109,6 @@
     return (force, strain)
 
 
-def deposit(onehot, values):
-    return jnp.einsum("ls,scn->cln", onehot, values, precision=lax.Precision.HIGHEST)
-
-
-def local_rows(values, dest, live, start, total_rows, width):
-    local_row = jnp.mod(dest // H - start + 2, total_rows)
-    line = local_row * H + dest % H
-    onehot = (
-        (jnp.arange((CA + 4) * H, dtype=jnp.int32)[:, None] == line[None, :]) & live[None, :]
-    ).astype(jnp.float32)
-    return deposit(onehot, values).reshape(10, CA + 4, H, width)
-
-
 def local(block_mass, block_flux, block_dest, block_count):
     sector = lax.axis_index("az")
     band_index = lax.axis_index("rad")
@@ -103,25 +122,19 @@
     dest = block_dest[0, 0]
     slot_index = jnp.arange(slots, dtype=jnp.int32)
     live = slot_index < block_count[0, 0]
-    extended = local_rows(values, dest, live, start, total_rows, width)
-    from_left = passed_along(extended[:, CA + 2 :], "az", 1)
-    from_right = passed_along(extended[:, :2], "az", -1)
-    fields = extended[:, 2 : CA + 2]
-    fields = fields.at[:, :2].add(from_left)
-    fields = fields.at[:, CA - 2 :].add(from_right)
+    raw = local_rows(values, dest, live, start, total_rows, width)
+    extended = window(raw)
     glob_cells = (band_index * width + jnp.arange(width, dtype=jnp.int32)).astype(jnp.float32)
     radius = width * n_rad + glob_cells + 0.5
     dtheta = 2.0 * math.pi / total_rows
     scale_az = 0.5 / (radius * dtheta)
     recip = 1.0 / radius
-    extended = padded_2(fields, (("az", 1), ("rad", 3)), 1)
-    extended = radial_mask(extended, 1, band_index, width, n_rad)
-    smoothed = smooth_block(extended)
-    velocity = smoothed[1:4] / (smoothed[0:1] + density_base)
-    combined = jnp.concatenate([velocity, smoothed[4:]], axis=0)
-    outer = padded_2(combined, (("az", 1), ("rad", 3)), 1)
-    outer = radial_mask(outer, 1, band_index, width, n_rad)
-    grad_az, grad_height, grad_rad, center = gradients(outer, scale_az)
+    smoothed_ext = smooth_block(extended)
+    smoothed = smoothed_ext[:, 1:-1, :, 1:-1]
+    velocity = smoothed_ext[1:4] / (smoothed_ext[0:1] + density_base)
+    combined = jnp.concatenate([velocity, smoothed_ext[4:]], axis=0)
+    combined = radial_mask(combined, 1, band_index, width, n_rad)
+    grad_az, grad_height, grad_rad, center = gradients(combined, scale_az)
     force, strain = assemble(grad_az, grad_height, grad_rad, center, recip)
     return (smoothed, force, strain)
 

time: 154 us -> 103 us (0.67)
  the two profiles are of different devices: /device:TPU:254 before, /device:TPU:1 now
where the time goes in v1:
time: 103 us
  starting transfers between devices  47.5 us (46%)
  local copies, waits for them, and re-layouts  26.9 us (26%)
  other arithmetic  11.6 us (11%)
  waiting for transfers between devices  11.5 us (11%)
  matrix products  3.53 us (3%)
  between operations  1.59 us (2%)
    ppermute x8, starting transfers between devices, shifted(): return lax.ppermute(value, ('az', 'rad'), pairs)  47.5 us
    ppermute x8, waiting for transfers between devices, shifted(): return lax.ppermute(value, ('az', 'rad'), pairs)  11.5 us
    slice x2, local copies, waits for them, and re-layouts, window(): raw[..., hi]  4.95 us
    concatenate x2, local copies, waits for them, and re-layouts, add_rows(): jnp.concatenate([base[:, :k] + head, base[:, k:rows - k], base[:, rows -...  4.1 us
    unnamed x14, local copies, waits for them, and re-layouts  4.06 us
    slice x2, local copies, waits for them, and re-layouts, window(): bottom[..., hi]  3.55 us
    dot_general x1, matrix products, deposit(): jnp.einsum('ls,scn->cln', onehot, values, precision=lax.Precision.HIGHEST)  3.53 us
    add x3, other arithmetic, add_rows(): base[:, :k] + head  2.72 us
  transfers between devices with their start and end apart: 8, of which 2 were waited for; matrix products, arithmetic and copies ran while one was open for 19% of the time, Pallas kernels for 0%

profile of v1, /device:TPU:1, one launch (start us, length us, event | category | flops | bytes accessed | tf_op | source)
XLA Modules:
  0.0 102.6 jit_solution(17087740710742511229)
XLA Ops:
  1.3 0.0 copy-start.4
  1.3 1.1 %copy.21 = f32[1,1,512,128]{2,3,1,0:T(8,128)S(1)} copy(f32[1,1,512,128]{3,2,1,0:T(8,128)} %param.4) | data formatting | bytes 524288 | tf_op args[0]
  2.4 2.1 %copy.22 = f32[1,1,512,9,128]{2,4,3,1,0:T(8,128)S(1)} copy(f32[1,1,512,9,128]{4,2,3,1,0:T(8,128)} %param.5) | data formatting | bytes 4718592 | tf_op args[1]
  4.5 3.5 %fusion.12 = f32[10,384,128]{1,2,0:T(8,128)} fusion(f32[512,9,128]{0,2,1:T(8,128)S(1)} %bitcast.17, f32[512,1,128]{0,2,1:T(8,128)S(1)} %bitcast.18, s32[512]{0:T(512)S(1)} %fusion.41, pred[512]{0:T(512)(128)(4,1)S(1)} %iota_compare_fusion.1), kind=kOutput, calls=%fused_computation.22 | convolution fusion | flops 3020947456 | bytes 4590080 | tf_op jit(solution)/shard_map/ls,scn->cln/dot_general | solution.py:29
  8.0 1.9 %copy.23 = f32[10,384,128]{2,1,0:T(8,128)S(1)} copy(f32[10,384,128]{1,2,0:T(8,128)} %fusion.12) | data formatting | bytes 3932160 | tf_op jit(solution)/shard_map/ls,scn->cln/transpose | solution.py:29
  9.9 1.2 %fusion.47 = (f32[10,4,32,128]{3,2,1,0:T(8,128)}, f32[10,4,32,128]{3,2,1,0:T(8,128)}) fusion(f32[10,12,32,128]{3,2,1,0:T(8,128)S(1)} %bitcast.13), kind=kLoop, calls=%fused_computation.99 | loop fusion | bytes 2621440 | tf_op jit(solution)/shard_map/slice | solution.py:52
  11.1 4.0 %collective-permute-start.3 = (f32[10,4,32,128]{3,2,1,0:T(8,128)}, f32[10,4,32,128]{3,2,1,0:T(8,128)}, u32[]{:S(2)}, u32[]{:S(2)}) collective-permute-start(f32[10,4,32,128]{3,2,1,0:T(8,128)} %get-tuple-element.19), channel_id=1, source_target_pairs={{0,4},{1,5},{2,6},{3,7},{4,8},{5,9},{6,10},{7,11},{8,12},{9,13},{1... | collective-permute-start | bytes 1966088 | tf_op jit(solution)/shard_map/ppermute | solution.py:25
  15.1 16.2 %collective-permute-start.4 = (f32[10,4,32,128]{3,2,1,0:T(8,128)}, f32[10,4,32,128]{3,2,1,0:T(8,128)}, u32[]{:S(2)}, u32[]{:S(2)}) collective-permute-start(f32[10,4,32,128]{3,2,1,0:T(8,128)} %get-tuple-element.20), channel_id=1, source_target_pairs={{0,508},{1,509},{2,510},{3,511},{4,0},{5,1},{6,2},{7,3},{8,4},{9,5... | collective-permute-start | bytes 1966088 | tf_op jit(solution)/shard_map/ppermute | solution.py:25
  31.4 1.5 %fusion.45 = (f32[10,4,32,2]{3,2,1,0:T(8,128)}, f32[10,4,32,2]{3,2,1,0:T(8,128)S(1)}, f32[10,4,32,2]{3,2,1,0:T(8,128)S(1)}, f32[10,4,32,2]{3,2,1,0:T(8,128)}) fusion(f32[10,12,32,128]{3,2,1,0:T(8,128)S(1)} %bitcast.14), kind=kLoop, calls=%fused_computation.97 | loop fusion | bytes 81920 | tf_op jit(solution)/shard_map/slice | solution.py:63
  32.9 2.0 %copy.27 = f32[10,4,32,2]{2,1,3,0:T(4,128)} copy(f32[10,4,32,2]{3,2,1,0:T(8,128)} %get-tuple-element.13) | data formatting | bytes 20480 | tf_op jit(solution)/shard_map/slice | solution.py:64
  34.9 5.2 %collective-permute-start.2 = (f32[10,4,32,2]{2,1,3,0:T(4,128)}, f32[10,4,32,2]{2,1,3,0:T(4,128)}, u32[]{:S(2)}, u32[]{:S(2)}) collective-permute-start(f32[10,4,32,2]{2,1,3,0:T(4,128)} %copy.27), channel_id=1, source_target_pairs={{0,509},{1,510},{2,511},{4,1},{5,2},{6,3},{8,5},{9,6},{10,7},{12,9... | collective-permute-start | bytes 30728 | tf_op jit(solution)/shard_map/ppermute | solution.py:25
  40.1 2.0 %copy.25 = f32[10,4,32,2]{2,1,3,0:T(4,128)} copy(f32[10,4,32,2]{3,2,1,0:T(8,128)} %get-tuple-element.10) | data formatting | bytes 20480 | tf_op jit(solution)/shard_map/slice | solution.py:63
  42.1 10.3 %collective-permute-start.1 = (f32[10,4,32,2]{2,1,3,0:T(4,128)}, f32[10,4,32,2]{2,1,3,0:T(4,128)}, u32[]{:S(2)}, u32[]{:S(2)}) collective-permute-start(f32[10,4,32,2]{2,1,3,0:T(4,128)} %copy.25), channel_id=1, source_target_pairs={{0,5},{1,6},{2,7},{4,9},{5,10},{6,11},{8,13},{9,14},{10,15},{12,17... | collective-permute-start | bytes 30728 | tf_op jit(solution)/shard_map/ppermute | solution.py:25
  52.4 2.6 %fusion.46 = (f32[10,12,32,2]{3,2,1,0:T(8,128)}, f32[10,12,32,2]{3,2,1,0:T(8,128)}) fusion(f32[10,12,32,128]{3,2,1,0:T(8,128)S(1)} %bitcast.15), kind=kLoop, calls=%fused_computation.98 | loop fusion | bytes 122880 | tf_op jit(solution)/shard_map/slice | solution.py:62
  55.0 2.3 %copy.24 = f32[10,12,32,2]{2,3,1,0:T(2,128)S(1)} copy(f32[10,12,32,2]{3,2,1,0:T(8,128)} %get-tuple-element.14) | data formatting | bytes 61440 | tf_op jit(solution)/shard_map/slice | solution.py:62
  57.3 1.9 %collective-permute-start = (f32[10,12,32,2]{2,3,1,0:T(2,128)S(1)}, f32[10,12,32,2]{2,3,1,0:T(2,128)S(1)}, u32[]{:S(2)}, u32[]{:S(2)}) collective-permute-start(f32[10,12,32,2]{2,3,1,0:T(2,128)S(1)} %copy.24), channel_id=1, source_target_pairs={{0,1},{1,2},{2,3},{4,5},{5,6},{6,7},{8,9},{9,10},{10,11},{12,13},{... | collective-permute-start | bytes 92168 | tf_op jit(solution)/shard_map/ppermute | solution.py:25
  59.3 0.9 copy.32
  60.2 0.3 copy.30
  60.5 2.3 %copy.29 = f32[10,12,32,2]{2,3,1,0:T(2,128)S(1)} copy(f32[10,12,32,2]{3,2,1,0:T(8,128)} %get-tuple-element.15) | data formatting | bytes 61440 | tf_op jit(solution)/shard_map/slice | solution.py:57
  62.9 3.1 %collective-permute-start.6 = (f32[10,4,32,2]{2,1,3,0:T(4,128)S(1)}, f32[10,4,32,2]{2,1,3,0:T(4,128)S(1)}, u32[]{:S(2)}, u32[]{:S(2)}) collective-permute-start(f32[10,4,32,2]{2,1,3,0:T(4,128)S(1)} %copy.30), channel_id=1, source_target_pairs={{1,4},{2,5},{3,6},{5,8},{6,9},{7,10},{9,12},{10,13},{11,14},{13,16... | collective-permute-start | bytes 30728 | tf_op jit(solution)/shard_map/ppermute | solution.py:25
  66.1 4.6 %collective-permute-start.7 = (f32[10,4,32,2]{2,1,3,0:T(4,128)S(1)}, f32[10,4,32,2]{2,1,3,0:T(4,128)S(1)}, u32[]{:S(2)}, u32[]{:S(2)}) collective-permute-start(f32[10,4,32,2]{2,1,3,0:T(4,128)S(1)} %copy-done.2), channel_id=1, source_target_pairs={{1,508},{2,509},{3,510},{5,0},{6,1},{7,2},{9,4},{10,5},{11,6},{13,... | collective-permute-start | bytes 30728 | tf_op jit(solution)/shard_map/ppermute | solution.py:25
  70.7 2.1 %collective-permute-start.5 = (f32[10,12,32,2]{2,3,1,0:T(2,128)S(1)}, f32[10,12,32,2]{2,3,1,0:T(2,128)S(1)}, u32[]{:S(2)}, u32[]{:S(2)}) collective-permute-start(f32[10,12,32,2]{2,3,1,0:T(2,128)S(1)} %copy.29), channel_id=1, source_target_pairs={{1,0},{2,1},{3,2},{5,4},{6,5},{7,6},{9,8},{10,9},{11,10},{13,12},{... | collective-permute-start | bytes 92168 | tf_op jit(solution)/shard_map/ppermute | solution.py:25
  72.8 0.9 slice_add_fusion.13
  73.7 0.1 pad_maximum_fusion.2
  73.7 2.0 %copy.34 = f32[10,12,32,2]{3,2,1,0:T(8,128)} copy(f32[10,12,32,2]{2,3,1,0:T(2,128)S(1)} %pad_maximum_fusion.2) | data formatting | bytes 61440 | tf_op jit(solution)/shard_map/concatenate | solution.py:44
  75.8 5.5 %collective-permute-done.7 = f32[10,4,32,2]{2,1,3,0:T(4,128)S(1)} collective-permute-done((f32[10,4,32,2]{2,1,3,0:T(4,128)S(1)}, f32[10,4,32,2]{2,1,3,0:T(4,128)S(1)}, u32[]{:S(2)}, u32[]{:S(2)}) %collective-permute-start.7) | collective-permute-done | bytes 10272 | tf_op jit(solution)/shard_map/ppermute | solution.py:25
  81.3 6.0 %collective-permute-done.5 = f32[10,12,32,2]{2,3,1,0:T(2,128)S(1)} collective-permute-done((f32[10,12,32,2]{2,3,1,0:T(2,128)S(1)}, f32[10,12,32,2]{2,3,1,0:T(2,128)S(1)}, u32[]{:S(2)}, u32[]{:S(2)}) %collective-permute-start.5) | collective-permute-done | bytes 30752 | tf_op jit(solution)/shard_map/ppermute | solution.py:25
  87.3 0.1 slice_add_fusion.11
  87.3 0.1 pad_maximum_fusion.3
  87.4 2.1 %copy.35 = f32[10,12,32,2]{3,2,1,0:T(8,128)} copy(f32[10,12,32,2]{2,3,1,0:T(2,128)S(1)} %pad_maximum_fusion.3) | data formatting | bytes 61440 | tf_op jit(solution)/shard_map/concatenate | solution.py:44
  89.5 1.8 %slice_add_fusion.15 = (f32[10,4,32,128]{3,2,1,0:T(8,128)S(1)}, f32[10,4,32,128]{3,2,1,0:T(8,128)S(1)}, f32[10,4,32,128]{3,2,1,0:T(8,128)S(1)}) fusion(f32[10,4,32,128]{3,2,1,0:T(8,128)} %collective-permute-done.3, f32[10,12,32,128]{3,2,1,0:T(8,128)S(1)} %bitcast.16, f32[10,4,32,128]{3,2,1,0:T(8,128)} %collective-permute-done.4), kind=kLoop, calls=%fused_computation.96 | loop fusion | flops 327680 | bytes 5242880 | tf_op jit(solution)/shard_map/add | solution.py:45
  91.3 0.1 copy-done
  91.4 0.6 copy-done.1
  92.0 1.6 %pad_maximum_fusion = f32[10,12,32,132]{3,2,1,0:T(8,128)S(1)} fusion(f32[10,12,32,2]{3,2,1,0:T(8,128)S(1)} %copy-done.1, f32[10,4,32,128]{3,2,1,0:T(8,128)S(1)} %get-tuple-element.17, f32[10,4,32,128]{3,2,1,0:T(8,128)S(1)} %get-tuple-element.18, f32[10,4,32,128]{3,2,1,0:T(8,128)S(1)} %get-tuple-element.16, f32[10,12,32,2]{3,2,1,0:T(8,128)S(1)} %copy-done), kind=kLoop, calls=%fused_computation.2 | loop fusion | flops 2027520 | bytes 4055040 | tf_op jit(solution)/shard_map/concatenate | solution.py:66
  93.6 0.8 fusion.6
  94.4 1.8 %fusion.4 = f32[10,10,32,130]{3,2,1,0:T(8,128)S(1)} fusion(f32[10,10,32,132]{3,2,1,0:T(8,128)S(1)} %fusion.6), kind=kLoop, calls=%fused_computation.8 | loop fusion | flops 2080000 | bytes 6656000 | tf_op jit(solution)/shard_map/add | solution.py:71
  96.2 1.2 %fusion.2 = f32[10,10,32,130]{3,2,1,0:T(8,128)S(1)} fusion(f32[10,10,32,130]{3,2,1,0:T(8,128)S(1)} %fusion.4), kind=kLoop, calls=%fused_computation.5 | loop fusion | flops 2080000 | bytes 3328000 | tf_op jit(solution)/shard_map/add | solution.py:73
  97.4 1.5 %slice.261 = f32[10,8,32,128]{3,2,1,0:T(8,128)} slice(f32[10,10,32,130]{3,2,1,0:T(8,128)S(1)} %fusion.2), slice={[0:10], [1:9], [0:32], [1:129]} | slice | bytes 2621440 | tf_op jit(solution)/shard_map/slice | solution.py:133
  98.8 0.1 slice.264
  99.0 0.1 slice_divide_fusion
  99.1 0.5 maximum_multiply_fusion
  99.6 1.3 %fusion.18 = (f32[9,8,32,128]{3,2,1,0:T(8,128)S(1)}, f32[9,8,32,128]{3,2,1,0:T(8,128)S(1)}, f32[9,8,32,128]{3,2,1,0:T(8,128)S(1)}) fusion(f32[9,10,32,130]{3,2,1,0:T(8,128)S(1)} %maximum_multiply_fusion, f32[128]{0:T(128)S(1)} %get-tuple-element.27), kind=kLoop, calls=%fused_computation.30 | loop fusion | flops 1179648 | bytes 9437696 | tf_op jit(solution)/shard_map/mul | solution.py:84
  100.9 0.3 fusion.16
  101.2 0.1 fusion.33
  101.4 0.2 fusion.36
  101.6 0.0 copy-start.3
  101.6 0.8 pad_maximum_fusion.1
  102.5 0.2 copy-done.3
  (21 shorter events, 0.2 us)
Async XLA Ops:
  1.3 3.2 %copy-start.4 = (s32[1,1,512]{2,1,0:T(1,128)S(1)}, s32[1,1,512]{2,1,0:T(1,128)}, u32[]{:S(2)}) copy-start(s32[1,1,512]{2,1,0:T(1,128)} %param.6) | copy-start | bytes 6148
  11.1 78.4 %collective-permute-start.3 = (f32[10,4,32,128]{3,2,1,0:T(8,128)}, f32[10,4,32,128]{3,2,1,0:T(8,128)}, u32[]{:S(2)}, u32[]{:S(2)}) collective-permute-start(f32[10,4,32,128]{3,2,1,0:T(8,128)} %get-tuple-element.19), channel_id=1, source_target_pairs={{0,4},{1,5},{2,6},{3,7},{4,8},{5,9},{6,10},{7,11},{8,12},{9,13},{1... | collective-permute-start | bytes 1966088 | tf_op jit(solution)/shard_map/ppermute | solution.py:25
  15.1 74.4 %collective-permute-start.4 = (f32[10,4,32,128]{3,2,1,0:T(8,128)}, f32[10,4,32,128]{3,2,1,0:T(8,128)}, u32[]{:S(2)}, u32[]{:S(2)}) collective-permute-start(f32[10,4,32,128]{3,2,1,0:T(8,128)} %get-tuple-element.20), channel_id=1, source_target_pairs={{0,508},{1,509},{2,510},{3,511},{4,0},{5,1},{6,2},{7,3},{8,4},{9,5... | collective-permute-start | bytes 1966088 | tf_op jit(solution)/shard_map/ppermute | solution.py:25
  34.9 28.0 %collective-permute-start.2 = (f32[10,4,32,2]{2,1,3,0:T(4,128)}, f32[10,4,32,2]{2,1,3,0:T(4,128)}, u32[]{:S(2)}, u32[]{:S(2)}) collective-permute-start(f32[10,4,32,2]{2,1,3,0:T(4,128)} %copy.27), channel_id=1, source_target_pairs={{0,509},{1,510},{2,511},{4,1},{5,2},{6,3},{8,5},{9,6},{10,7},{12,9... | collective-permute-start | bytes 30728 | tf_op jit(solution)/shard_map/ppermute | solution.py:25
  42.1 24.0 %collective-permute-start.1 = (f32[10,4,32,2]{2,1,3,0:T(4,128)}, f32[10,4,32,2]{2,1,3,0:T(4,128)}, u32[]{:S(2)}, u32[]{:S(2)}) collective-permute-start(f32[10,4,32,2]{2,1,3,0:T(4,128)} %copy.25), channel_id=1, source_target_pairs={{0,5},{1,6},{2,7},{4,9},{5,10},{6,11},{8,13},{9,14},{10,15},{12,17... | collective-permute-start | bytes 30728 | tf_op jit(solution)/shard_map/ppermute | solution.py:25
  57.3 13.4 %collective-permute-start = (f32[10,12,32,2]{2,3,1,0:T(2,128)S(1)}, f32[10,12,32,2]{2,3,1,0:T(2,128)S(1)}, u32[]{:S(2)}, u32[]{:S(2)}) collective-permute-start(f32[10,12,32,2]{2,3,1,0:T(2,128)S(1)} %copy.24), channel_id=1, source_target_pairs={{0,1},{1,2},{2,3},{4,5},{5,6},{6,7},{8,9},{9,10},{10,11},{12,13},{... | collective-permute-start | bytes 92168 | tf_op jit(solution)/shard_map/ppermute | solution.py:25
  60.2 5.8 %copy-start.2 = (f32[10,4,32,2]{2,1,3,0:T(4,128)S(1)}, f32[10,4,32,2]{2,1,3,0:T(4,128)}, u32[]{:S(2)}) copy-start(f32[10,4,32,2]{2,1,3,0:T(4,128)} %copy.32) | copy-start | bytes 30724
  62.9 12.9 %collective-permute-start.6 = (f32[10,4,32,2]{2,1,3,0:T(4,128)S(1)}, f32[10,4,32,2]{2,1,3,0:T(4,128)S(1)}, u32[]{:S(2)}, u32[]{:S(2)}) collective-permute-start(f32[10,4,32,2]{2,1,3,0:T(4,128)S(1)} %copy.30), channel_id=1, source_target_pairs={{1,4},{2,5},{3,6},{5,8},{6,9},{7,10},{9,12},{10,13},{11,14},{13,16... | collective-permute-start | bytes 30728 | tf_op jit(solution)/shard_map/ppermute | solution.py:25
  66.1 15.2 %collective-permute-start.7 = (f32[10,4,32,2]{2,1,3,0:T(4,128)S(1)}, f32[10,4,32,2]{2,1,3,0:T(4,128)S(1)}, u32[]{:S(2)}, u32[]{:S(2)}) collective-permute-start(f32[10,4,32,2]{2,1,3,0:T(4,128)S(1)} %copy-done.2), channel_id=1, source_target_pairs={{1,508},{2,509},{3,510},{5,0},{6,1},{7,2},{9,4},{10,5},{11,6},{13,... | collective-permute-start | bytes 30728 | tf_op jit(solution)/shard_map/ppermute | solution.py:25
  70.7 16.6 %collective-permute-start.5 = (f32[10,12,32,2]{2,3,1,0:T(2,128)S(1)}, f32[10,12,32,2]{2,3,1,0:T(2,128)S(1)}, u32[]{:S(2)}, u32[]{:S(2)}) collective-permute-start(f32[10,12,32,2]{2,3,1,0:T(2,128)S(1)} %copy.29), channel_id=1, source_target_pairs={{1,0},{2,1},{3,2},{5,4},{6,5},{7,6},{9,8},{10,9},{11,10},{13,12},{... | collective-permute-start | bytes 92168 | tf_op jit(solution)/shard_map/ppermute | solution.py:25
  89.5 1.9 %copy-start = (f32[10,12,32,2]{3,2,1,0:T(8,128)S(1)}, f32[10,12,32,2]{3,2,1,0:T(8,128)}, u32[]{:S(2)}) copy-start(f32[10,12,32,2]{3,2,1,0:T(8,128)} %copy.34) | copy-start | bytes 92164
  89.5 2.5 %copy-start.1 = (f32[10,12,32,2]{3,2,1,0:T(8,128)S(1)}, f32[10,12,32,2]{3,2,1,0:T(8,128)}, u32[]{:S(2)}) copy-start(f32[10,12,32,2]{3,2,1,0:T(8,128)} %copy.35) | copy-start | bytes 92164
  101.6 1.0 copy-start.3

commit v2 on v1

--- a/solution.py
+++ b/solution.py
@@ -47,23 +47,12 @@
 
 
 def window(raw):
+    cells = raw.shape[3]
+    right = shifted(raw[..., :HALO], 0, -1)
+    left = shifted(raw[..., cells - HALO :], 0, 1)
+    wide = jnp.concatenate([left, raw, right], axis=3)
     k = 2 * HALO
-    top = raw[:, :k]
-    bottom = raw[:, -k:]
-    center = add_rows(raw, shifted(bottom, 1, 0), shifted(top, -1, 0))
-    lo = slice(0, HALO)
-    hi = slice(raw.shape[3] - HALO, raw.shape[3])
-    right = add_rows(
-        shifted(raw[..., lo], 0, -1),
-        shifted(bottom[..., lo], 1, -1),
-        shifted(top[..., lo], -1, -1),
-    )
-    left = add_rows(
-        shifted(raw[..., hi], 0, 1),
-        shifted(bottom[..., hi], 1, 1),
-        shifted(top[..., hi], -1, 1),
-    )
-    return jnp.concatenate([left, center, right], axis=3)
+    return add_rows(wide, shifted(wide[:, -k:], 1, 0), shifted(wide[:, :k], -1, 0))
 
 
 def smooth_block(extended):

time: 103 us -> 96.4 us (0.936)
  starting transfers between devices: 47.5 us -> 35 us
  waiting for transfers between devices: 11.5 us -> 21.8 us
  local copies, waits for them, and re-layouts: 26.9 us -> 20 us
  other arithmetic: 11.6 us -> 14.2 us
    ppermute x8 -> x4, starting transfers between devices: 47.5 us -> 35 us  [shifted(): return lax.ppermute(value, ('az', 'rad'), pairs)]
    ppermute x8 -> x4, waiting for transfers between devices: 11.5 us -> 21.8 us  [shifted(): return lax.ppermute(value, ('az', 'rad'), pairs)]
    slice x9 -> x4, local copies, waits for them, and re-layouts: 15.3 us -> 9.07 us  [the longest x2 4.96 us: window(): left = shifted(raw[..., cells - HALO:], 0, 1)]
    ppermute x0 -> x2, local copies, waits for them, and re-layouts: none -> 4.12 us  [shifted(): return lax.ppermute(value, ('az', 'rad'), pairs)]
    concatenate x2 -> x0, local copies, waits for them, and re-layouts: 4.1 us -> none  [add_rows(): jnp.concatenate([base[:, :k] + head, base[:, k:rows - k], base[:, rows -...]
    concatenate x1, other arithmetic: 1.58 us -> 3.72 us  [window(): wide = jnp.concatenate([left, raw, right], axis=3)]
    unnamed x14 -> x12, local copies, waits for them, and re-layouts: 4.06 us -> 3.34 us
    add x3 -> x1, other arithmetic: 2.72 us -> 2.79 us  [add_rows(): base[:, :k] + head]
  transfers between devices with their start and end apart: 8 -> 4, of which waited for: 2 -> 2; matrix products, arithmetic and copies ran while one was open for 19% -> 5% of each run, Pallas kernels for 0% -> 0%
where the time goes in v2:
time: 96.4 us; the launch traced here: 96.1 us
  starting transfers between devices  35 us (36%)
  waiting for transfers between devices  21.8 us (23%)
  local copies, waits for them, and re-layouts  20 us (21%)
  other arithmetic  14.2 us (15%)
  matrix products  3.54 us (4%)
  between operations  1.54 us (2%)
    ppermute x4, starting transfers between devices, shifted(): return lax.ppermute(value, ('az', 'rad'), pairs)  35 us
    ppermute x4, waiting for transfers between devices, shifted(): return lax.ppermute(value, ('az', 'rad'), pairs)  21.8 us
    slice x2, local copies, waits for them, and re-layouts, window(): left = shifted(raw[..., cells - HALO:], 0, 1)  4.96 us
    ppermute x2, local copies, waits for them, and re-layouts, shifted(): return lax.ppermute(value, ('az', 'rad'), pairs)  4.12 us
    concatenate x1, other arithmetic, window(): wide = jnp.concatenate([left, raw, right], axis=3)  3.72 us
    dot_general x1, matrix products, deposit(): jnp.einsum('ls,scn->cln', onehot, values, precision=lax.Precision.HIGHEST)  3.54 us
    unnamed x12, local copies, waits for them, and re-layouts  3.34 us
    add x1, other arithmetic, add_rows(): base[:, :k] + head  2.79 us
  transfers between devices with their start and end apart: 4, of which 2 were waited for; matrix products, arithmetic and copies ran while one was open for 5% of the time, Pallas kernels for 0%

profile of v2, /device:TPU:1, one launch (start us, length us, event | category | flops | bytes accessed | tf_op | source)
XLA Modules:
  0.0 96.1 jit_solution(17065673976659777641)
XLA Ops:
  0.6 0.0 copy-start.1
  0.6 0.0 copy-start.3
  0.7 2.1 %copy.16 = f32[1,1,512,9,128]{2,4,3,1,0:T(8,128)S(1)} copy(f32[1,1,512,9,128]{4,2,3,1,0:T(8,128)} %param.5) | data formatting | bytes 4718592 | tf_op args[1]
  2.8 0.0 copy-done.1
  2.8 0.1 copy.15
  3.6 0.0 copy-done.3
  3.6 3.5 %fusion.12 = f32[10,384,128]{1,2,0:T(8,128)} fusion(f32[512,9,128]{0,2,1:T(8,128)S(1)} %bitcast.15, f32[512,1,128]{0,2,1:T(8,128)S(1)} %bitcast.16, s32[512]{0:T(512)S(1)} %fusion.41, pred[512]{0:T(512)(128)(4,1)S(1)} %iota_compare_fusion.1), kind=kOutput, calls=%fused_computation.23 | convolution fusion | flops 3020947456 | bytes 4590080 | tf_op jit(solution)/shard_map/ls,scn->cln/dot_general | solution.py:29
  7.1 1.9 %copy.17 = f32[10,384,128]{2,1,0:T(8,128)S(1)} copy(f32[10,384,128]{1,2,0:T(8,128)} %fusion.12) | data formatting | bytes 3932160 | tf_op jit(solution)/shard_map/ls,scn->cln/transpose | solution.py:29
  9.0 2.6 %fusion.46 = (f32[10,12,32,2]{3,2,1,0:T(8,128)}, f32[10,12,32,2]{3,2,1,0:T(8,128)}) fusion(f32[10,12,32,128]{3,2,1,0:T(8,128)S(1)} %bitcast.13), kind=kLoop, calls=%fused_computation.93 | loop fusion | bytes 122880 | tf_op jit(solution)/shard_map/slice | solution.py:52
  11.7 2.3 %copy.19 = f32[10,12,32,2]{2,3,1,0:T(2,128)S(1)} copy(f32[10,12,32,2]{3,2,1,0:T(8,128)} %get-tuple-element.16) | data formatting | bytes 61440 | tf_op jit(solution)/shard_map/slice | solution.py:51
  14.0 8.7 %collective-permute-start.1 = (f32[10,12,32,2]{2,3,1,0:T(2,128)S(1)}, f32[10,12,32,2]{2,3,1,0:T(2,128)S(1)}, u32[]{:S(2)}, u32[]{:S(2)}) collective-permute-start(f32[10,12,32,2]{2,3,1,0:T(2,128)S(1)} %copy.19), channel_id=1, source_target_pairs={{1,0},{2,1},{3,2},{5,4},{6,5},{7,6},{9,8},{10,9},{11,10},{13,12},{... | collective-permute-start | bytes 92168 | tf_op jit(solution)/shard_map/ppermute | solution.py:25
  22.7 2.3 %copy.18 = f32[10,12,32,2]{2,3,1,0:T(2,128)S(1)} copy(f32[10,12,32,2]{3,2,1,0:T(8,128)} %get-tuple-element.15) | data formatting | bytes 61440 | tf_op jit(solution)/shard_map/slice | solution.py:52
  25.1 10.0 %collective-permute-start = (f32[10,12,32,2]{2,3,1,0:T(2,128)S(1)}, f32[10,12,32,2]{2,3,1,0:T(2,128)S(1)}, u32[]{:S(2)}, u32[]{:S(2)}) collective-permute-start(f32[10,12,32,2]{2,3,1,0:T(2,128)S(1)} %copy.18), channel_id=1, source_target_pairs={{0,1},{1,2},{2,3},{4,5},{5,6},{6,7},{8,9},{9,10},{10,11},{12,13},{... | collective-permute-start | bytes 92168 | tf_op jit(solution)/shard_map/ppermute | solution.py:25
  35.1 0.0 collective-permute-done.1
  35.1 2.1 %copy.21 = f32[10,12,32,2]{3,2,1,0:T(8,128)} copy(f32[10,12,32,2]{2,3,1,0:T(2,128)S(1)} %collective-permute-done.1) | data formatting | bytes 61440 | tf_op jit(solution)/shard_map/ppermute | solution.py:25
  37.2 0.0 collective-permute-done
  37.2 2.0 %copy.20 = f32[10,12,32,2]{3,2,1,0:T(8,128)} copy(f32[10,12,32,2]{2,3,1,0:T(2,128)S(1)} %collective-permute-done) | data formatting | bytes 61440 | tf_op jit(solution)/shard_map/ppermute | solution.py:25
  39.2 3.7 %pad_maximum_fusion = f32[10,12,32,132]{3,2,1,0:T(8,128)S(1)} fusion(f32[10,12,32,2]{3,2,1,0:T(8,128)} %copy.21, f32[10,12,32,128]{3,2,1,0:T(8,128)S(1)} %bitcast.14, f32[10,12,32,2]{3,2,1,0:T(8,128)} %copy.20), kind=kLoop, calls=%fused_computation.2 | loop fusion | flops 1013760 | bytes 4055040 | tf_op jit(solution)/shard_map/concatenate | solution.py:53
  42.9 0.0 copy-start
  43.0 1.8 %fusion.45 = (f32[10,4,32,132]{3,2,1,0:T(8,128)}, f32[10,4,32,132]{3,2,1,0:T(8,128)}) fusion(f32[10,12,32,132]{3,2,1,0:T(8,128)S(1)} %pad_maximum_fusion), kind=kLoop, calls=%fused_computation.92 | loop fusion | bytes 2703360 | tf_op jit(solution)/shard_map/slice | solution.py:55
  44.7 0.9 copy-done
  45.6 3.2 %collective-permute-start.2 = (f32[10,4,32,132]{3,2,1,0:T(8,128)}, f32[10,4,32,132]{3,2,1,0:T(8,128)S(1)}, u32[]{:S(2)}, u32[]{:S(2)}) collective-permute-start(f32[10,4,32,132]{3,2,1,0:T(8,128)} %get-tuple-element.9), channel_id=1, source_target_pairs={{0,4},{1,5},{2,6},{3,7},{4,8},{5,9},{6,10},{7,11},{8,12},{9,13},{1... | collective-permute-start | bytes 2027528 | tf_op jit(solution)/shard_map/ppermute | solution.py:25
  48.8 13.1 %collective-permute-start.3 = (f32[10,4,32,132]{3,2,1,0:T(8,128)}, f32[10,4,32,132]{3,2,1,0:T(8,128)S(1)}, u32[]{:S(2)}, u32[]{:S(2)}) collective-permute-start(f32[10,4,32,132]{3,2,1,0:T(8,128)} %get-tuple-element.10), channel_id=1, source_target_pairs={{0,508},{1,509},{2,510},{3,511},{4,0},{5,1},{6,2},{7,3},{8,4},{9,5... | collective-permute-start | bytes 2027528 | tf_op jit(solution)/shard_map/ppermute | solution.py:25
  62.0 20.0 %collective-permute-done.2 = f32[10,4,32,132]{3,2,1,0:T(8,128)S(1)} collective-permute-done((f32[10,4,32,132]{3,2,1,0:T(8,128)}, f32[10,4,32,132]{3,2,1,0:T(8,128)S(1)}, u32[]{:S(2)}, u32[]{:S(2)}) %collective-permute-start.2) | collective-permute-done | bytes 675872 | tf_op jit(solution)/shard_map/ppermute | solution.py:25
  81.9 1.9 %collective-permute-done.3 = f32[10,4,32,132]{3,2,1,0:T(8,128)S(1)} collective-permute-done((f32[10,4,32,132]{3,2,1,0:T(8,128)}, f32[10,4,32,132]{3,2,1,0:T(8,128)S(1)}, u32[]{:S(2)}, u32[]{:S(2)}) %collective-permute-start.3) | collective-permute-done | bytes 675872 | tf_op jit(solution)/shard_map/ppermute | solution.py:25
  83.8 2.8 %slice_add_fusion.11 = (f32[10,4,32,132]{3,2,1,0:T(8,128)S(1)}, f32[10,4,32,132]{3,2,1,0:T(8,128)S(1)}, f32[10,4,32,132]{3,2,1,0:T(8,128)S(1)}) fusion(f32[10,4,32,132]{3,2,1,0:T(8,128)S(1)} %collective-permute-done.2, f32[10,12,32,132]{3,2,1,0:T(8,128)} %copy-done, f32[10,4,32,132]{3,2,1,0:T(8,128)S(1)} %collective-permute-done.3), kind=kLoop, calls=%fused_computation.91 | loop fusion | flops 337920 | bytes 5406720 | tf_op jit(solution)/shard_map/add | solution.py:45
  86.6 0.5 pad_maximum_fusion.1
  87.1 0.8 fusion.6
  87.9 1.8 %fusion.4 = f32[10,10,32,130]{3,2,1,0:T(8,128)S(1)} fusion(f32[10,10,32,132]{3,2,1,0:T(8,128)S(1)} %fusion.6), kind=kLoop, calls=%fused_computation.9 | loop fusion | flops 2080000 | bytes 6656000 | tf_op jit(solution)/shard_map/add | solution.py:60
  89.7 1.1 %fusion.2 = f32[10,10,32,130]{3,2,1,0:T(8,128)S(1)} fusion(f32[10,10,32,130]{3,2,1,0:T(8,128)S(1)} %fusion.4), kind=kLoop, calls=%fused_computation.6 | loop fusion | flops 2080000 | bytes 3328000 | tf_op jit(solution)/shard_map/add | solution.py:62
  90.8 1.5 %slice.207 = f32[10,8,32,128]{3,2,1,0:T(8,128)} slice(f32[10,10,32,130]{3,2,1,0:T(8,128)S(1)} %fusion.2), slice={[0:10], [1:9], [0:32], [1:129]} | slice | bytes 2621440 | tf_op jit(solution)/shard_map/slice | solution.py:122
  92.3 0.1 slice.210
  92.4 0.1 slice_divide_fusion
  92.6 0.5 maximum_multiply_fusion
  93.1 1.3 %fusion.18 = (f32[9,8,32,128]{3,2,1,0:T(8,128)S(1)}, f32[9,8,32,128]{3,2,1,0:T(8,128)S(1)}, f32[9,8,32,128]{3,2,1,0:T(8,128)S(1)}) fusion(f32[9,10,32,130]{3,2,1,0:T(8,128)S(1)} %maximum_multiply_fusion, f32[128]{0:T(128)S(1)} %get-tuple-element.17), kind=kLoop, calls=%fused_computation.31 | loop fusion | flops 1179648 | bytes 9437696 | tf_op jit(solution)/shard_map/mul | solution.py:73
  94.4 0.3 fusion.16
  94.7 0.1 fusion.33
  94.8 0.2 fusion.36
  95.1 0.0 copy-start.2
  95.1 0.8 pad_maximum_fusion.2
  95.9 0.2 copy-done.2
  (10 shorter events, 0.1 us)
Async XLA Ops:
  0.6 2.1 %copy-start.1 = (f32[1,1,512,128]{3,2,1,0:T(8,128)S(1)}, f32[1,1,512,128]{3,2,1,0:T(8,128)}, u32[]{:S(2)}) copy-start(f32[1,1,512,128]{3,2,1,0:T(8,128)} %param.4) | copy-start | bytes 786436
  0.6 2.9 %copy-start.3 = (s32[1,1,512]{2,1,0:T(1,128)S(1)}, s32[1,1,512]{2,1,0:T(1,128)}, u32[]{:S(2)}) copy-start(s32[1,1,512]{2,1,0:T(1,128)} %param.6) | copy-start | bytes 6148
  14.0 21.1 %collective-permute-start.1 = (f32[10,12,32,2]{2,3,1,0:T(2,128)S(1)}, f32[10,12,32,2]{2,3,1,0:T(2,128)S(1)}, u32[]{:S(2)}, u32[]{:S(2)}) collective-permute-start(f32[10,12,32,2]{2,3,1,0:T(2,128)S(1)} %copy.19), channel_id=1, source_target_pairs={{1,0},{2,1},{3,2},{5,4},{6,5},{7,6},{9,8},{10,9},{11,10},{13,12},{... | collective-permute-start | bytes 92168 | tf_op jit(solution)/shard_map/ppermute | solution.py:25
  25.1 12.1 %collective-permute-start = (f32[10,12,32,2]{2,3,1,0:T(2,128)S(1)}, f32[10,12,32,2]{2,3,1,0:T(2,128)S(1)}, u32[]{:S(2)}, u32[]{:S(2)}) collective-permute-start(f32[10,12,32,2]{2,3,1,0:T(2,128)S(1)} %copy.18), channel_id=1, source_target_pairs={{0,1},{1,2},{2,3},{4,5},{5,6},{6,7},{8,9},{9,10},{10,11},{12,13},{... | collective-permute-start | bytes 92168 | tf_op jit(solution)/shard_map/ppermute | solution.py:25
  42.9 2.7 %copy-start = (f32[10,12,32,132]{3,2,1,0:T(8,128)}, f32[10,12,32,132]{3,2,1,0:T(8,128)S(1)}, u32[]{:S(2)}) copy-start(f32[10,12,32,132]{3,2,1,0:T(8,128)S(1)} %pad_maximum_fusion) | copy-start | bytes 6082564
  45.6 36.3 %collective-permute-start.2 = (f32[10,4,32,132]{3,2,1,0:T(8,128)}, f32[10,4,32,132]{3,2,1,0:T(8,128)S(1)}, u32[]{:S(2)}, u32[]{:S(2)}) collective-permute-start(f32[10,4,32,132]{3,2,1,0:T(8,128)} %get-tuple-element.9), channel_id=1, source_target_pairs={{0,4},{1,5},{2,6},{3,7},{4,8},{5,9},{6,10},{7,11},{8,12},{9,13},{1... | collective-permute-start | bytes 2027528 | tf_op jit(solution)/shard_map/ppermute | solution.py:25
  48.8 35.0 %collective-permute-start.3 = (f32[10,4,32,132]{3,2,1,0:T(8,128)}, f32[10,4,32,132]{3,2,1,0:T(8,128)S(1)}, u32[]{:S(2)}, u32[]{:S(2)}) collective-permute-start(f32[10,4,32,132]{3,2,1,0:T(8,128)} %get-tuple-element.10), channel_id=1, source_target_pairs={{0,508},{1,509},{2,510},{3,511},{4,0},{5,1},{6,2},{7,3},{8,4},{9,5... | collective-permute-start | bytes 2027528 | tf_op jit(solution)/shard_map/ppermute | solution.py:25
  95.1 1.0 %copy-start.2 = (f32[6,8,32,128]{3,2,1,0:T(8,128)}, f32[6,8,32,128]{3,2,1,0:T(8,128)S(1)}, u32[]{:S(2)}) copy-start(f32[6,8,32,128]{3,2,1,0:T(8,128)S(1)} %fusion.26) | copy-start | bytes 2359300

commit v3 on v2

--- a/solution.py
+++ b/solution.py
@@ -22,7 +22,9 @@
             tb = b + db
             if 0 <= tb < n_rad:
                 pairs.append((a * n_rad + b, ((a + da) % n_az) * n_rad + tb))
-    return lax.ppermute(value, ("az", "rad"), pairs)
+    shape = value.shape
+    dense = value.reshape(value.size // 128, 128)
+    return lax.ppermute(dense, ("az", "rad"), pairs).reshape(shape)
 
 
 def deposit(onehot, values):

time: 96.4 us -> 90.5 us (0.939)
  waiting for transfers between devices: 21.8 us -> 6.69 us
  local copies, waits for them, and re-layouts: 20 us -> 29.2 us
    reshape x0 -> x8, local copies, waits for them, and re-layouts: none -> 18.8 us  [the longest x4 10.8 us: shifted(): return lax.ppermute(dense, ('az', 'rad'), pairs).reshape(shape)]
    ppermute x4, waiting for transfers between devices: 21.8 us -> 6.69 us  [shifted(): return lax.ppermute(dense, ('az', 'rad'), pairs).reshape(shape)]
    ppermute x2 -> x0, local copies, waits for them, and re-layouts: 4.12 us -> none  [shifted(): return lax.ppermute(value, ('az', 'rad'), pairs)]
    slice x2 -> x1, local copies, waits for them, and re-layouts: 4.96 us -> 2.62 us  [window(): left = shifted(raw[..., cells - HALO:], 0, 1)]
    slice x1 -> x0, local copies, waits for them, and re-layouts: 2.33 us -> none  [window(): right = shifted(raw[..., :HALO], 0, -1)]
    slice x1, local copies, waits for them, and re-layouts: 1.78 us -> 0.18 us  [window(): wide[:, -k:]]
  transfers between devices with their start and end apart: 4 -> 4, of which waited for: 2 -> 2; matrix products, arithmetic and copies ran while one was open for 5% -> 10% of each run, Pallas kernels for 0% -> 0%
where the time goes in v3:
time: 90.5 us; the launch traced here: 90.1 us
  starting transfers between devices  35 us (39%)
  local copies, waits for them, and re-layouts  29.2 us (32%)
  other arithmetic  14.2 us (16%)
  waiting for transfers between devices  6.69 us (7%)
  matrix products  3.54 us (4%)
  between operations  1.57 us (2%)
    ppermute x4, starting transfers between devices, shifted(): return lax.ppermute(dense, ('az', 'rad'), pairs).reshape(shape)  35 us
    reshape x4, local copies, waits for them, and re-layouts, shifted(): return lax.ppermute(dense, ('az', 'rad'), pairs).reshape(shape)  10.8 us
    reshape x4, local copies, waits for them, and re-layouts, shifted(): dense = value.reshape(value.size // 128, 128)  7.96 us
    ppermute x4, waiting for transfers between devices, shifted(): return lax.ppermute(dense, ('az', 'rad'), pairs).reshape(shape)  6.69 us
    unnamed x12, local copies, waits for them, and re-layouts  4.09 us
    concatenate x1, other arithmetic, window(): wide = jnp.concatenate([left, raw, right], axis=3)  3.72 us
    dot_general x1, matrix products, deposit(): jnp.einsum('ls,scn->cln', onehot, values, precision=lax.Precision.HIGHEST)  3.54 us
    add x1, other arithmetic, add_rows(): base[:, :k] + head  2.8 us
  transfers between devices with their start and end apart: 4, of which 2 were waited for; matrix products, arithmetic and copies ran while one was open for 10% of the time, Pallas kernels for 0%

profile of v3, /device:TPU:1, one launch (start us, length us, event | category | flops | bytes accessed | tf_op | source)
XLA Modules:
  0.0 90.1 jit_solution(14688255283088427364)
XLA Ops:
  0.6 0.0 copy-start.1
  0.6 0.0 copy-start.3
  0.7 2.1 %copy.11 = f32[1,1,512,9,128]{2,4,3,1,0:T(8,128)S(1)} copy(f32[1,1,512,9,128]{4,2,3,1,0:T(8,128)} %param.5) | data formatting | bytes 4718592 | tf_op args[1]
  2.8 0.0 copy-done.1
  2.8 0.1 copy.10
  3.6 0.0 copy-done.3
  3.6 3.5 %fusion.12 = f32[10,384,128]{1,2,0:T(8,128)} fusion(f32[512,9,128]{0,2,1:T(8,128)S(1)} %bitcast.23, f32[512,1,128]{0,2,1:T(8,128)S(1)} %bitcast.24, s32[512]{0:T(512)S(1)} %fusion.41, pred[512]{0:T(512)(128)(4,1)S(1)} %iota_compare_fusion.1), kind=kOutput, calls=%fused_computation.23 | convolution fusion | flops 3020947456 | bytes 4590080 | tf_op jit(solution)/shard_map/ls,scn->cln/dot_general | solution.py:31
  7.1 1.9 %copy.12 = f32[10,384,128]{2,1,0:T(8,128)S(1)} copy(f32[10,384,128]{1,2,0:T(8,128)} %fusion.12) | data formatting | bytes 3932160 | tf_op jit(solution)/shard_map/ls,scn->cln/transpose | solution.py:31
  9.0 2.6 %fusion.46 = (f32[10,12,32,2]{3,2,1,0:T(8,128)}, f32[10,12,32,2]{3,2,1,0:T(8,128)}) fusion(f32[10,12,32,128]{3,2,1,0:T(8,128)S(1)} %bitcast.21), kind=kLoop, calls=%fused_computation.93 | loop fusion | bytes 122880 | tf_op jit(solution)/shard_map/slice | solution.py:54
  11.7 2.6 %reshape.126 = f32[60,128]{1,0:T(8,128)S(1)} reshape(f32[10,12,32,2]{3,2,1,0:T(8,128)} %get-tuple-element.16) | data formatting | bytes 61440 | tf_op jit(solution)/shard_map/reshape | solution.py:26
  14.3 8.7 %collective-permute-start.1 = (f32[60,128]{1,0:T(8,128)S(1)}, f32[60,128]{1,0:T(8,128)S(1)}, u32[]{:S(2)}, u32[]{:S(2)}) collective-permute-start(f32[60,128]{1,0:T(8,128)S(1)} %reshape.126), channel_id=1, source_target_pairs={{1,0},{2,1},{3,2},{5,4},{6,5},{7,6},{9,8},{10,9},{11,10},{13,12},{... | collective-permute-start | bytes 92168 | tf_op jit(solution)/shard_map/ppermute | solution.py:27
  23.0 2.6 %reshape.124 = f32[60,128]{1,0:T(8,128)S(1)} reshape(f32[10,12,32,2]{3,2,1,0:T(8,128)} %get-tuple-element.15) | data formatting | bytes 61440 | tf_op jit(solution)/shard_map/reshape | solution.py:26
  25.6 10.0 %collective-permute-start = (f32[60,128]{1,0:T(8,128)S(1)}, f32[60,128]{1,0:T(8,128)S(1)}, u32[]{:S(2)}, u32[]{:S(2)}) collective-permute-start(f32[60,128]{1,0:T(8,128)S(1)} %reshape.124), channel_id=1, source_target_pairs={{0,1},{1,2},{2,3},{4,5},{5,6},{6,7},{8,9},{9,10},{10,11},{12,13},{... | collective-permute-start | bytes 92168 | tf_op jit(solution)/shard_map/ppermute | solution.py:27
  35.6 0.0 collective-permute-done.1
  35.6 3.3 %reshape.127 = f32[10,12,32,2]{3,2,1,0:T(8,128)} reshape(f32[60,128]{1,0:T(8,128)S(1)} %collective-permute-done.1) | data formatting | bytes 61440 | tf_op jit(solution)/shard_map/reshape | solution.py:27
  38.9 0.0 collective-permute-done
  38.9 3.2 %reshape.125 = f32[10,12,32,2]{3,2,1,0:T(8,128)} reshape(f32[60,128]{1,0:T(8,128)S(1)} %collective-permute-done) | data formatting | bytes 61440 | tf_op jit(solution)/shard_map/reshape | solution.py:27
  42.1 3.7 %pad_maximum_fusion = f32[10,12,32,132]{3,2,1,0:T(8,128)S(1)} fusion(f32[10,12,32,2]{3,2,1,0:T(8,128)} %reshape.127, f32[10,12,32,128]{3,2,1,0:T(8,128)S(1)} %bitcast.22, f32[10,12,32,2]{3,2,1,0:T(8,128)} %reshape.125), kind=kLoop, calls=%fused_computation.2 | loop fusion | flops 1013760 | bytes 4055040 | tf_op jit(solution)/shard_map/concatenate | solution.py:55
  45.8 0.0 copy-start
  45.8 0.2 fusion.45
  46.0 1.7 %copy-done = f32[10,12,32,132]{3,2,1,0:T(8,128)} copy-done((f32[10,12,32,132]{3,2,1,0:T(8,128)}, f32[10,12,32,132]{3,2,1,0:T(8,128)S(1)}, u32[]{:S(2)}) %copy-start) | copy-done | bytes 2027544
  47.7 1.0 %reshape.128 = f32[1320,128]{1,0:T(8,128)S(1)} reshape(f32[10,4,32,132]{3,2,1,0:T(8,128)S(1)} %get-tuple-element.9) | data formatting | bytes 1351680 | tf_op jit(solution)/shard_map/reshape | solution.py:26
  48.6 3.4 %collective-permute-start.2 = (f32[1320,128]{1,0:T(8,128)S(1)}, f32[1320,128]{1,0:T(8,128)S(1)}, u32[]{:S(2)}, u32[]{:S(2)}) collective-permute-start(f32[1320,128]{1,0:T(8,128)S(1)} %reshape.128), channel_id=1, source_target_pairs={{0,4},{1,5},{2,6},{3,7},{4,8},{5,9},{6,10},{7,11},{8,12},{9,13},{1... | collective-permute-start | bytes 2027528 | tf_op jit(solution)/shard_map/ppermute | solution.py:27
  52.0 1.8 %reshape.130 = f32[1320,128]{1,0:T(8,128)} reshape(f32[10,4,32,132]{3,2,1,0:T(8,128)S(1)} %get-tuple-element.10) | data formatting | bytes 1351680 | tf_op jit(solution)/shard_map/reshape | solution.py:26
  53.8 12.9 %collective-permute-start.3 = (f32[1320,128]{1,0:T(8,128)}, f32[1320,128]{1,0:T(8,128)}, u32[]{:S(2)}, u32[]{:S(2)}) collective-permute-start(f32[1320,128]{1,0:T(8,128)} %reshape.130), channel_id=1, source_target_pairs={{0,508},{1,509},{2,510},{3,511},{4,0},{5,1},{6,2},{7,3},{8,4},{9,5... | collective-permute-start | bytes 2027528 | tf_op jit(solution)/shard_map/ppermute | solution.py:27
  66.8 4.3 %collective-permute-done.2 = f32[1320,128]{1,0:T(8,128)S(1)} collective-permute-done((f32[1320,128]{1,0:T(8,128)S(1)}, f32[1320,128]{1,0:T(8,128)S(1)}, u32[]{:S(2)}, u32[]{:S(2)}) %collective-permute-start.2) | collective-permute-done | bytes 675872 | tf_op jit(solution)/shard_map/ppermute | solution.py:27
  71.1 1.7 %reshape.129 = f32[10,4,32,132]{3,2,1,0:T(8,128)S(1)} reshape(f32[1320,128]{1,0:T(8,128)S(1)} %collective-permute-done.2) | data formatting | bytes 1351680 | tf_op jit(solution)/shard_map/reshape | solution.py:27
  72.8 2.3 %collective-permute-done.3 = f32[1320,128]{1,0:T(8,128)} collective-permute-done((f32[1320,128]{1,0:T(8,128)}, f32[1320,128]{1,0:T(8,128)}, u32[]{:S(2)}, u32[]{:S(2)}) %collective-permute-start.3) | collective-permute-done | bytes 675872 | tf_op jit(solution)/shard_map/ppermute | solution.py:27
  75.2 2.7 %reshape.131 = f32[10,4,32,132]{3,2,1,0:T(8,128)S(1)} reshape(f32[1320,128]{1,0:T(8,128)} %collective-permute-done.3) | data formatting | bytes 1351680 | tf_op jit(solution)/shard_map/reshape | solution.py:27
  77.8 2.8 %slice_add_fusion.11 = (f32[10,4,32,132]{3,2,1,0:T(8,128)S(1)}, f32[10,4,32,132]{3,2,1,0:T(8,128)S(1)}, f32[10,4,32,132]{3,2,1,0:T(8,128)S(1)}) fusion(f32[10,4,32,132]{3,2,1,0:T(8,128)S(1)} %reshape.129, f32[10,12,32,132]{3,2,1,0:T(8,128)} %copy-done, f32[10,4,32,132]{3,2,1,0:T(8,128)S(1)} %reshape.131), kind=kLoop, calls=%fused_computation.91 | loop fusion | flops 337920 | bytes 5406720 | tf_op jit(solution)/shard_map/add | solution.py:47
  80.6 0.5 pad_maximum_fusion.1
  81.1 0.8 fusion.6
  81.9 1.8 %fusion.4 = f32[10,10,32,130]{3,2,1,0:T(8,128)S(1)} fusion(f32[10,10,32,132]{3,2,1,0:T(8,128)S(1)} %fusion.6), kind=kLoop, calls=%fused_computation.9 | loop fusion | flops 2080000 | bytes 6656000 | tf_op jit(solution)/shard_map/add | solution.py:62
  83.7 1.1 %fusion.2 = f32[10,10,32,130]{3,2,1,0:T(8,128)S(1)} fusion(f32[10,10,32,130]{3,2,1,0:T(8,128)S(1)} %fusion.4), kind=kLoop, calls=%fused_computation.6 | loop fusion | flops 2080000 | bytes 3328000 | tf_op jit(solution)/shard_map/add | solution.py:64
  84.8 1.5 %slice.207 = f32[10,8,32,128]{3,2,1,0:T(8,128)} slice(f32[10,10,32,130]{3,2,1,0:T(8,128)S(1)} %fusion.2), slice={[0:10], [1:9], [0:32], [1:129]} | slice | bytes 2621440 | tf_op jit(solution)/shard_map/slice | solution.py:124
  86.3 0.1 slice.210
  86.5 0.1 slice_divide_fusion
  86.6 0.5 maximum_multiply_fusion
  87.1 1.3 %fusion.18 = (f32[9,8,32,128]{3,2,1,0:T(8,128)S(1)}, f32[9,8,32,128]{3,2,1,0:T(8,128)S(1)}, f32[9,8,32,128]{3,2,1,0:T(8,128)S(1)}) fusion(f32[9,10,32,130]{3,2,1,0:T(8,128)S(1)} %maximum_multiply_fusion, f32[128]{0:T(128)S(1)} %get-tuple-element.17), kind=kLoop, calls=%fused_computation.31 | loop fusion | flops 1179648 | bytes 9437696 | tf_op jit(solution)/shard_map/mul | solution.py:75
  88.4 0.3 fusion.16
  88.7 0.1 fusion.33
  88.9 0.2 fusion.36
  89.1 0.0 copy-start.2
  89.1 0.8 pad_maximum_fusion.2
  90.0 0.2 copy-done.2
  (10 shorter events, 0.1 us)
Async XLA Ops:
  0.6 2.1 %copy-start.1 = (f32[1,1,512,128]{3,2,1,0:T(8,128)S(1)}, f32[1,1,512,128]{3,2,1,0:T(8,128)}, u32[]{:S(2)}) copy-start(f32[1,1,512,128]{3,2,1,0:T(8,128)} %param.4) | copy-start | bytes 786436
  0.6 2.9 %copy-start.3 = (s32[1,1,512]{2,1,0:T(1,128)S(1)}, s32[1,1,512]{2,1,0:T(1,128)}, u32[]{:S(2)}) copy-start(s32[1,1,512]{2,1,0:T(1,128)} %param.6) | copy-start | bytes 6148
  14.3 21.3 %collective-permute-start.1 = (f32[60,128]{1,0:T(8,128)S(1)}, f32[60,128]{1,0:T(8,128)S(1)}, u32[]{:S(2)}, u32[]{:S(2)}) collective-permute-start(f32[60,128]{1,0:T(8,128)S(1)} %reshape.126), channel_id=1, source_target_pairs={{1,0},{2,1},{3,2},{5,4},{6,5},{7,6},{9,8},{10,9},{11,10},{13,12},{... | collective-permute-start | bytes 92168 | tf_op jit(solution)/shard_map/ppermute | solution.py:27
  25.6 13.3 %collective-permute-start = (f32[60,128]{1,0:T(8,128)S(1)}, f32[60,128]{1,0:T(8,128)S(1)}, u32[]{:S(2)}, u32[]{:S(2)}) collective-permute-start(f32[60,128]{1,0:T(8,128)S(1)} %reshape.124), channel_id=1, source_target_pairs={{0,1},{1,2},{2,3},{4,5},{5,6},{6,7},{8,9},{9,10},{10,11},{12,13},{... | collective-permute-start | bytes 92168 | tf_op jit(solution)/shard_map/ppermute | solution.py:27
  45.8 1.9 %copy-start = (f32[10,12,32,132]{3,2,1,0:T(8,128)}, f32[10,12,32,132]{3,2,1,0:T(8,128)S(1)}, u32[]{:S(2)}) copy-start(f32[10,12,32,132]{3,2,1,0:T(8,128)S(1)} %pad_maximum_fusion) | copy-start | bytes 6082564
  48.6 22.5 %collective-permute-start.2 = (f32[1320,128]{1,0:T(8,128)S(1)}, f32[1320,128]{1,0:T(8,128)S(1)}, u32[]{:S(2)}, u32[]{:S(2)}) collective-permute-start(f32[1320,128]{1,0:T(8,128)S(1)} %reshape.128), channel_id=1, source_target_pairs={{0,4},{1,5},{2,6},{3,7},{4,8},{5,9},{6,10},{7,11},{8,12},{9,13},{1... | collective-permute-start | bytes 2027528 | tf_op jit(solution)/shard_map/ppermute | solution.py:27
  53.8 21.3 %collective-permute-start.3 = (f32[1320,128]{1,0:T(8,128)}, f32[1320,128]{1,0:T(8,128)}, u32[]{:S(2)}, u32[]{:S(2)}) collective-permute-start(f32[1320,128]{1,0:T(8,128)} %reshape.130), channel_id=1, source_target_pairs={{0,508},{1,509},{2,510},{3,511},{4,0},{5,1},{6,2},{7,3},{8,4},{9,5... | collective-permute-start | bytes 2027528 | tf_op jit(solution)/shard_map/ppermute | solution.py:27
  89.1 1.0 %copy-start.2 = (f32[6,8,32,128]{3,2,1,0:T(8,128)}, f32[6,8,32,128]{3,2,1,0:T(8,128)S(1)}, u32[]{:S(2)}) copy-start(f32[6,8,32,128]{3,2,1,0:T(8,128)S(1)} %fusion.26) | copy-start | bytes 2359300

commit v4 on v3

--- a/solution.py
+++ b/solution.py
@@ -23,6 +23,8 @@
             if 0 <= tb < n_rad:
                 pairs.append((a * n_rad + b, ((a + da) % n_az) * n_rad + tb))
     shape = value.shape
+    if shape[-1] % 128 == 0:
+        return lax.ppermute(value, ("az", "rad"), pairs)
     dense = value.reshape(value.size // 128, 128)
     return lax.ppermute(dense, ("az", "rad"), pairs).reshape(shape)
 
@@ -48,32 +50,53 @@
     )
 
 
+def selector(cells, picks):
+    return (jnp.arange(cells, dtype=jnp.int32)[None, :] == jnp.array(picks, jnp.int32)[:, None]).astype(
+        jnp.float32
+    )
+
+
 def window(raw):
-    cells = raw.shape[3]
-    right = shifted(raw[..., :HALO], 0, -1)
-    left = shifted(raw[..., cells - HALO :], 0, 1)
-    wide = jnp.concatenate([left, raw, right], axis=3)
     k = 2 * HALO
-    return add_rows(wide, shifted(wide[:, -k:], 1, 0), shifted(wide[:, :k], -1, 0))
+    center = add_rows(raw, shifted(raw[:, -k:], 1, 0), shifted(raw[:, :k], -1, 0))
+    shape = center.shape
+    cells = shape[3]
+    flat = center.reshape(-1, cells)
+    edge_cells = list(range(HALO)) + list(range(cells - HALO, cells))
+    picked = jnp.einsum(
+        "jn,mn->jm", selector(cells, edge_cells), flat, precision=lax.Precision.HIGHEST
+    )
+    right = shifted(picked[:HALO], 0, -1)
+    left = shifted(picked[HALO:], 0, 1)
+    edges = jnp.einsum(
+        "jm,jn->mn",
+        jnp.concatenate([right, left], axis=0),
+        selector(cells, edge_cells),
+        precision=lax.Precision.HIGHEST,
+    )
+    return jnp.concatenate([center, edges.reshape(shape)], axis=3)
 
 
 def smooth_block(extended):
     fields = 0.25 * extended[:, :-2] + 0.5 * extended[:, 1:-1] + 0.25 * extended[:, 2:]
-    fields = 0.25 * fields[..., :-2] + 0.5 * fields[..., 1:-1] + 0.25 * fields[..., 2:]
+    fields = 0.25 * jnp.roll(fields, 1, 3) + 0.5 * fields + 0.25 * jnp.roll(fields, -1, 3)
     padded = jnp.pad(fields, ((0, 0), (0, 0), (1, 1), (0, 0)))
     return 0.25 * padded[:, :, :-2] + 0.5 * padded[:, :, 1:-1] + 0.25 * padded[:, :, 2:]
 
 
-def radial_mask(extended, depth, band_index, width, n_rad):
-    columns = band_index * width - depth + jnp.arange(width + 2 * depth, dtype=jnp.int32)
+def ring_mask(extended, band_index, width, n_rad):
+    lane = jnp.arange(2 * width, dtype=jnp.int32)
+    columns = band_index * width + jnp.where(lane < width + width // 2, lane, lane - 2 * width)
     inside = (columns >= 0) & (columns < width * n_rad)
     return extended * inside.astype(jnp.float32)
 
 
-def gradients(extended, scale_az):
-    center = extended[:, 1:-1, :, 1:-1]
-    grad_az = (extended[:, 2:, :, 1:-1] - extended[:, :-2, :, 1:-1]) * scale_az
-    grad_rad = (extended[:, 1:-1, :, 2:] - extended[:, 1:-1, :, :-2]) * 0.5
+def gradients(extended, scale_az, width):
+    center = extended[:, 1:-1, :, :width]
+    grad_az = (extended[:, 2:, :, :width] - extended[:, :-2, :, :width]) * scale_az
+    grad_rad = (
+        jnp.roll(extended[:, 1:-1], -1, 3)[..., :width] - jnp.roll(extended[:, 1:-1], 1, 3)[..., :width]
+    ) * 0.5
     padded = jnp.pad(center, ((0, 0), (0, 0), (1, 1), (0, 0)))
     grad_height = (padded[:, :, 2:] - padded[:, :, :-2]) * 0.5
     return (grad_az, grad_height, grad_rad, center)
@@ -121,11 +144,11 @@
     scale_az = 0.5 / (radius * dtheta)
     recip = 1.0 / radius
     smoothed_ext = smooth_block(extended)
-    smoothed = smoothed_ext[:, 1:-1, :, 1:-1]
+    smoothed = smoothed_ext[:, 1:-1, :, :width]
     velocity = smoothed_ext[1:4] / (smoothed_ext[0:1] + density_base)
     combined = jnp.concatenate([velocity, smoothed_ext[4:]], axis=0)
-    combined = radial_mask(combined, 1, band_index, width, n_rad)
-    grad_az, grad_height, grad_rad, center = gradients(combined, scale_az)
+    combined = ring_mask(combined, band_index, width, n_rad)
+    grad_az, grad_height, grad_rad, center = gradients(combined, scale_az, width)
     force, strain = assemble(grad_az, grad_height, grad_rad, center, recip)
     return (smoothed, force, strain)
 

time: 90.5 us -> 77.2 us (0.85)
  the two profiles are of different devices: /device:TPU:1 before, /device:TPU:510 now
where the time goes in v4:
time: 77.2 us; the launch traced here: 76.9 us
  waiting for transfers between devices  38.8 us (50%)
  starting transfers between devices  12.8 us (17%)
  local copies, waits for them, and re-layouts  9.81 us (13%)
  other arithmetic  7.72 us (10%)
  matrix products  6.26 us (8%)
  between operations  1.6 us (2%)
    ppermute x4, waiting for transfers between devices, shifted(): return lax.ppermute(value, ('az', 'rad'), pairs)  38.8 us
    ppermute x4, starting transfers between devices, shifted(): return lax.ppermute(value, ('az', 'rad'), pairs)  12.8 us
    dot_general x1, matrix products, deposit(): jnp.einsum('ls,scn->cln', onehot, values, precision=lax.Precision.HIGHEST)  3.55 us
    unnamed x12, local copies, waits for them, and re-layouts  2.91 us
    add x1, other arithmetic, smooth_block(): 0.25 * jnp.roll(fields, 1, 3) + 0.5 * fields  2.29 us
    slice x2, local copies, waits for them, and re-layouts, smooth_block(): jnp.roll(fields, -1, 3)  1.93 us
    transpose x1, local copies, waits for them, and re-layouts, deposit(): jnp.einsum('ls,scn->cln', onehot, values, precision=lax.Precision.HIGHEST)  1.88 us
    dot_general x1, matrix products, window(): jnp.einsum('jm,jn->mn', jnp.concatenate([right, left], axis=0), selector(...  1.72 us
  transfers between devices with their start and end apart: 4, of which 3 were waited for; matrix products, arithmetic and copies ran while one was open for 0% of the time, Pallas kernels for 0%

profile of v4, /device:TPU:510, one launch (start us, length us, event | category | flops | bytes accessed | tf_op | source)
XLA Modules:
  0.0 76.9 jit_solution(11883782033102789723)
XLA Ops:
  0.6 0.0 copy-start
  0.6 0.0 copy-start.3
  0.7 2.1 %copy.15 = f32[1,1,512,9,128]{2,4,3,1,0:T(8,128)S(1)} copy(f32[1,1,512,9,128]{4,2,3,1,0:T(8,128)} %param.7) | data formatting | bytes 4718592 | tf_op args[1]
  2.8 0.0 copy-done
  2.8 0.1 copy.14
  3.6 0.0 copy-done.3
  3.6 3.6 %fusion.12 = f32[10,384,128]{1,2,0:T(8,128)} fusion(f32[512,9,128]{0,2,1:T(8,128)S(1)} %bitcast.18, f32[512,1,128]{0,2,1:T(8,128)S(1)} %bitcast.21, s32[512]{0:T(512)S(1)} %fusion.46, pred[512]{0:T(512)(128)(4,1)S(1)} %iota_compare_fusion.4), kind=kOutput, calls=%fused_computation.22 | convolution fusion | flops 3020947456 | bytes 4590080 | tf_op jit(solution)/shard_map/ls,scn->cln/dot_general | solution.py:33
  7.2 1.9 %copy.16 = f32[10,384,128]{2,1,0:T(8,128)S(1)} copy(f32[10,384,128]{1,2,0:T(8,128)} %fusion.12) | data formatting | bytes 3932160 | tf_op jit(solution)/shard_map/ls,scn->cln/transpose | solution.py:33
  9.0 1.2 %fusion.57 = (f32[10,4,32,128]{3,2,1,0:T(8,128)}, f32[10,4,32,128]{3,2,1,0:T(8,128)}) fusion(f32[10,12,32,128]{3,2,1,0:T(8,128)S(1)} %bitcast.16), kind=kLoop, calls=%fused_computation.105 | loop fusion | bytes 2621440 | tf_op jit(solution)/shard_map/slice | solution.py:61
  10.2 6.4 %collective-permute-start = (f32[10,4,32,128]{3,2,1,0:T(8,128)}, f32[10,4,32,128]{3,2,1,0:T(8,128)S(1)}, u32[]{:S(2)}, u32[]{:S(2)}) collective-permute-start(f32[10,4,32,128]{3,2,1,0:T(8,128)} %get-tuple-element.17), channel_id=1, source_target_pairs={{0,4},{1,5},{2,6},{3,7},{4,8},{5,9},{6,10},{7,11},{8,12},{9,13},{1... | collective-permute-start | bytes 1966088 | tf_op jit(solution)/shard_map/ppermute | solution.py:27
  16.6 1.9 %collective-permute-start.1 = (f32[10,4,32,128]{3,2,1,0:T(8,128)}, f32[10,4,32,128]{3,2,1,0:T(8,128)S(1)}, u32[]{:S(2)}, u32[]{:S(2)}) collective-permute-start(f32[10,4,32,128]{3,2,1,0:T(8,128)} %get-tuple-element.18), channel_id=1, source_target_pairs={{0,508},{1,509},{2,510},{3,511},{4,0},{5,1},{6,2},{7,3},{8,4},{9,5... | collective-permute-start | bytes 1966088 | tf_op jit(solution)/shard_map/ppermute | solution.py:27
  18.6 12.3 %collective-permute-done = f32[10,4,32,128]{3,2,1,0:T(8,128)S(1)} collective-permute-done((f32[10,4,32,128]{3,2,1,0:T(8,128)}, f32[10,4,32,128]{3,2,1,0:T(8,128)S(1)}, u32[]{:S(2)}, u32[]{:S(2)}) %collective-permute-start) | collective-permute-done | bytes 655392 | tf_op jit(solution)/shard_map/ppermute | solution.py:27
  30.9 15.1 %collective-permute-done.1 = f32[10,4,32,128]{3,2,1,0:T(8,128)S(1)} collective-permute-done((f32[10,4,32,128]{3,2,1,0:T(8,128)}, f32[10,4,32,128]{3,2,1,0:T(8,128)S(1)}, u32[]{:S(2)}, u32[]{:S(2)}) %collective-permute-start.1) | collective-permute-done | bytes 655392 | tf_op jit(solution)/shard_map/ppermute | solution.py:27
  46.0 0.4 slice_add_fusion.11
  46.4 0.0 copy-start.2
  46.4 0.2 pad_maximum_fusion.1
  46.6 0.5 copy-done.2
  47.0 1.0 %fusion.47 = f32[4,3840]{1,0:T(4,128)S(1)} fusion(f32[3840,128]{1,0:T(8,128)S(1)} %bitcast.19, s32[4]{0:T(128)S(1)} %copy-done.2), kind=kOutput, calls=%fused_computation.87 | convolution fusion | flops 23593472 | bytes 2027536 | tf_op jit(solution)/shard_map/jn,mn->jm/dot_general | solution.py:66
  48.1 1.9 %collective-permute-start.2 = (f32[2,3840]{1,0:T(2,128)S(1)}, f32[2,3840]{1,0:T(2,128)S(1)}, u32[]{:S(2)}, u32[]{:S(2)}) collective-permute-start(f32[2,3840]{1,0:T(2,128)S(1)} %get-tuple-element.19), channel_id=1, source_target_pairs={{1,0},{2,1},{3,2},{5,4},{6,5},{7,6},{9,8},{10,9},{11,10},{13,12},{... | collective-permute-start | bytes 92168 | tf_op jit(solution)/shard_map/ppermute | solution.py:27
  50.0 2.6 %collective-permute-start.3 = (f32[2,3840]{1,0:T(2,128)S(1)}, f32[2,3840]{1,0:T(2,128)S(1)}, u32[]{:S(2)}, u32[]{:S(2)}) collective-permute-start(f32[2,3840]{1,0:T(2,128)S(1)} %get-tuple-element.20), channel_id=1, source_target_pairs={{0,1},{1,2},{2,3},{4,5},{5,6},{6,7},{8,9},{9,10},{10,11},{12,13},{... | collective-permute-start | bytes 92168 | tf_op jit(solution)/shard_map/ppermute | solution.py:27
  52.6 0.0 collective-permute-done.2
  52.6 11.3 %collective-permute-done.3 = f32[2,3840]{1,0:T(2,128)S(1)} collective-permute-done((f32[2,3840]{1,0:T(2,128)S(1)}, f32[2,3840]{1,0:T(2,128)S(1)}, u32[]{:S(2)}, u32[]{:S(2)}) %collective-permute-start.3) | collective-permute-done | bytes 30752 | tf_op jit(solution)/shard_map/ppermute | solution.py:27
  63.9 1.7 %fusion.38 = f32[3840,128]{1,0:T(8,128)S(1)} fusion(f32[2,3840]{1,0:T(2,128)S(1)} %collective-permute-done.3, f32[2,3840]{1,0:T(2,128)S(1)} %collective-permute-done.2, s32[4]{0:T(128)S(1)} %copy-done.2), kind=kOutput, calls=%fused_computation.68 | convolution fusion | flops 23608832 | bytes 2027536 | tf_op jit(solution)/shard_map/jm,jn->mn/dot_general | solution.py:71
  65.6 0.4 pad_maximum_fusion
  66.1 0.8 %fusion.4 = f32[10,10,32,256]{3,2,1,0:T(8,128)S(1)} fusion(f32[10,12,32,256]{3,2,1,0:T(8,128)S(1)} %pad_maximum_fusion), kind=kLoop, calls=%fused_computation.8 | loop fusion | flops 4096000 | bytes 13107200 | tf_op jit(solution)/shard_map/add | solution.py:81
  66.9 1.3 %fusion.55 = (f32[10,10,32,255]{3,2,1,0:T(8,128)S(1)}, f32[10,10,32,255]{3,2,1,0:T(8,128)S(1)}) fusion(f32[10,10,32,256]{3,2,1,0:T(8,128)S(1)} %fusion.4), kind=kLoop, calls=%fused_computation.103 | loop fusion | bytes 13056000 | tf_op jit(solution)/shard_map/jit(_roll_static)/slice | solution.py:82
  68.2 0.6 fusion.56
  68.8 2.3 %fusion.7 = f32[10,10,32,256]{3,2,1,0:T(8,128)S(1)} fusion(f32[10,10,32,255]{3,2,1,0:T(8,128)S(1)} %get-tuple-element.8, f32[10,10,32,1]{3,2,1,0:T(8,128)S(1)} %get-tuple-element.10, f32[10,10,32,1]{3,2,1,0:T(8,128)S(1)} %get-tuple-element.9, f32[10,10,32,255]{3,2,1,0:T(8,128)S(1)} %get-tuple-element.7, f32[10,12,32,256]{3,2,1,0:T(8,128)S(1)} %pad_maximum_fusion), kind=kLoop, calls=%fused_computation.14 | loop fusion | flops 9830400 | bytes 19660800 | tf_op jit(solution)/shard_map/add | solution.py:82
  71.1 1.0 %fusion.2 = f32[10,10,32,256]{3,2,1,0:T(8,128)S(1)} fusion(f32[10,10,32,256]{3,2,1,0:T(8,128)S(1)} %fusion.7), kind=kLoop, calls=%fused_computation.5 | loop fusion | flops 4096000 | bytes 6553600 | tf_op jit(solution)/shard_map/add | solution.py:84
  72.1 0.1 slice.241
  72.3 0.1 slice_divide_fusion
  72.4 0.3 maximum_multiply_fusion.2
  72.7 0.2 slice.249
  72.8 0.4 slice.248
  73.2 1.2 %slice.238 = f32[10,8,32,128]{3,2,1,0:T(8,128)} slice(f32[10,10,32,256]{3,2,1,0:T(8,128)S(1)} %fusion.2), slice={[0:10], [1:9], [0:32], [0:128]} | slice | bytes 2621440 | tf_op jit(solution)/shard_map/slice | solution.py:147
  74.4 0.9 %fusion.19 = (f32[9,8,32,128]{3,2,1,0:T(8,128)S(1)}, f32[9,8,32,128]{3,2,1,0:T(8,128)S(1)}, f32[9,8,32,128]{3,2,1,0:T(8,128)S(1)}) fusion(f32[9,10,32,256]{3,2,1,0:T(8,128)S(1)} %maximum_multiply_fusion.2, f32[128]{0:T(128)S(1)} %get-tuple-element.21, f32[9,8,32,255]{3,2,1,0:T(8,128)S(1)} %slice.249, f32[9,8,32,1]{3,2,1,0:T(8,128)S(1)} %slice.248), kind=kLoop, calls=%fused_computation.31 | loop fusion | flops 1474560 | bytes 10617344 | tf_op jit(solution)/shard_map/mul | solution.py:96
  75.3 0.3 fusion.16
  75.7 0.2 fusion.37
  75.9 0.0 copy-start.1
  75.9 0.8 %pad_maximum_fusion.3 = f32[3,8,32,128]{3,2,1,0:T(8,128)} fusion(f32[1,8,32,128]{3,2,1,0:T(8,128)S(1)} %get-tuple-element.4, f32[1,8,32,128]{3,2,1,0:T(8,128)S(1)} %get-tuple-element.6, f32[1,8,32,128]{3,2,1,0:T(8,128)S(1)} %get-tuple-element.3), kind=kLoop, calls=%fused_computation.36 | loop fusion | flops 196608 | bytes 786432 | tf_op jit(solution)/shard_map/stack | solution.py:106
  76.8 0.2 copy-done.1
  (12 shorter events, 0.2 us)
Async XLA Ops:
  0.6 2.1 %copy-start = (f32[1,1,512,128]{3,2,1,0:T(8,128)S(1)}, f32[1,1,512,128]{3,2,1,0:T(8,128)}, u32[]{:S(2)}) copy-start(f32[1,1,512,128]{3,2,1,0:T(8,128)} %param.6) | copy-start | bytes 786436
  0.6 2.9 %copy-start.3 = (s32[1,1,512]{2,1,0:T(1,128)S(1)}, s32[1,1,512]{2,1,0:T(1,128)}, u32[]{:S(2)}) copy-start(s32[1,1,512]{2,1,0:T(1,128)} %param.8) | copy-start | bytes 6148
  10.2 20.6 %collective-permute-start = (f32[10,4,32,128]{3,2,1,0:T(8,128)}, f32[10,4,32,128]{3,2,1,0:T(8,128)S(1)}, u32[]{:S(2)}, u32[]{:S(2)}) collective-permute-start(f32[10,4,32,128]{3,2,1,0:T(8,128)} %get-tuple-element.17), channel_id=1, source_target_pairs={{0,4},{1,5},{2,6},{3,7},{4,8},{5,9},{6,10},{7,11},{8,12},{9,13},{1... | collective-permute-start | bytes 1966088 | tf_op jit(solution)/shard_map/ppermute | solution.py:27
  16.6 29.4 %collective-permute-start.1 = (f32[10,4,32,128]{3,2,1,0:T(8,128)}, f32[10,4,32,128]{3,2,1,0:T(8,128)S(1)}, u32[]{:S(2)}, u32[]{:S(2)}) collective-permute-start(f32[10,4,32,128]{3,2,1,0:T(8,128)} %get-tuple-element.18), channel_id=1, source_target_pairs={{0,508},{1,509},{2,510},{3,511},{4,0},{5,1},{6,2},{7,3},{8,4},{9,5... | collective-permute-start | bytes 1966088 | tf_op jit(solution)/shard_map/ppermute | solution.py:27
  46.4 0.7 copy-start.2
  48.1 4.5 %collective-permute-start.2 = (f32[2,3840]{1,0:T(2,128)S(1)}, f32[2,3840]{1,0:T(2,128)S(1)}, u32[]{:S(2)}, u32[]{:S(2)}) collective-permute-start(f32[2,3840]{1,0:T(2,128)S(1)} %get-tuple-element.19), channel_id=1, source_target_pairs={{1,0},{2,1},{3,2},{5,4},{6,5},{7,6},{9,8},{10,9},{11,10},{13,12},{... | collective-permute-start | bytes 92168 | tf_op jit(solution)/shard_map/ppermute | solution.py:27
  50.0 13.9 %collective-permute-start.3 = (f32[2,3840]{1,0:T(2,128)S(1)}, f32[2,3840]{1,0:T(2,128)S(1)}, u32[]{:S(2)}, u32[]{:S(2)}) collective-permute-start(f32[2,3840]{1,0:T(2,128)S(1)} %get-tuple-element.20), channel_id=1, source_target_pairs={{0,1},{1,2},{2,3},{4,5},{5,6},{6,7},{8,9},{9,10},{10,11},{12,13},{... | collective-permute-start | bytes 92168 | tf_op jit(solution)/shard_map/ppermute | solution.py:27
  75.9 1.0 %copy-start.1 = (f32[6,8,32,128]{3,2,1,0:T(8,128)}, f32[6,8,32,128]{3,2,1,0:T(8,128)S(1)}, u32[]{:S(2)}) copy-start(f32[6,8,32,128]{3,2,1,0:T(8,128)S(1)} %fusion.27) | copy-start | bytes 2359300

commit v5 on v4

--- a/solution.py
+++ b/solution.py
@@ -58,19 +58,34 @@
 
 def window(raw):
     k = 2 * HALO
-    center = add_rows(raw, shifted(raw[:, -k:], 1, 0), shifted(raw[:, :k], -1, 0))
-    shape = center.shape
-    cells = shape[3]
-    flat = center.reshape(-1, cells)
+    shape = raw.shape
+    channels, rows, height, cells = shape
+    top = raw[:, :k]
+    bottom = raw[:, -k:]
     edge_cells = list(range(HALO)) + list(range(cells - HALO, cells))
     picked = jnp.einsum(
-        "jn,mn->jm", selector(cells, edge_cells), flat, precision=lax.Precision.HIGHEST
-    )
-    right = shifted(picked[:HALO], 0, -1)
-    left = shifted(picked[HALO:], 0, 1)
+        "jn,mn->jm", selector(cells, edge_cells), raw.reshape(-1, cells), precision=lax.Precision.HIGHEST
+    ).reshape(2 * HALO, channels, rows * height)
+    span = k * height
+    head = picked[:, :, :span]
+    tail = picked[:, :, -span:]
+
+    def side(part, db):
+        flat = lambda v: v.reshape(HALO, -1)
+        whole = shifted(flat(part), 0, db).reshape(HALO, channels, rows * height)
+        from_prev = shifted(flat(tail[part_rows[db]]), 1, db).reshape(HALO, channels, span)
+        from_next = shifted(flat(head[part_rows[db]]), -1, db).reshape(HALO, channels, span)
+        return jnp.concatenate(
+            [whole[..., :span] + from_prev, whole[..., span:-span], whole[..., -span:] + from_next], axis=2
+        )
+
+    part_rows = {-1: slice(0, HALO), 1: slice(HALO, 2 * HALO)}
+    center = add_rows(raw, shifted(bottom, 1, 0), shifted(top, -1, 0))
+    right = side(picked[:HALO], -1)
+    left = side(picked[HALO:], 1)
     edges = jnp.einsum(
         "jm,jn->mn",
-        jnp.concatenate([right, left], axis=0),
+        jnp.concatenate([right, left], axis=0).reshape(2 * HALO, -1),
         selector(cells, edge_cells),
         precision=lax.Precision.HIGHEST,
     )

time: 77.2 us -> 91.7 us (1.19)
  the two profiles are of different devices: /device:TPU:510 before, /device:TPU:1 now
where the time goes in v5:
time: 91.7 us; the launch traced here: 91.3 us
  starting transfers between devices  56.2 us (61%)
  local copies, waits for them, and re-layouts  9.46 us (10%)
  other arithmetic  8.84 us (10%)
  waiting for transfers between devices  8.81 us (10%)
  matrix products  6.28 us (7%)
  between operations  1.78 us (2%)
    ppermute x8, starting transfers between devices, shifted(): return lax.ppermute(value, ('az', 'rad'), pairs)  56.2 us
    ppermute x8, waiting for transfers between devices, shifted(): return lax.ppermute(value, ('az', 'rad'), pairs)  8.81 us
    dot_general x1, matrix products, deposit(): jnp.einsum('ls,scn->cln', onehot, values, precision=lax.Precision.HIGHEST)  3.54 us
    unnamed x18, local copies, waits for them, and re-layouts  2.5 us
    add x1, other arithmetic, smooth_block(): 0.25 * jnp.roll(fields, 1, 3) + 0.5 * fields  2.29 us
    slice x2, local copies, waits for them, and re-layouts, smooth_block(): jnp.roll(fields, -1, 3)  1.93 us
    transpose x1, local copies, waits for them, and re-layouts, deposit(): jnp.einsum('ls,scn->cln', onehot, values, precision=lax.Precision.HIGHEST)  1.9 us
  transfers between devices with their start and end apart: 8, of which 2 were waited for; matrix products, arithmetic and copies ran while one was open for 3% of the time, Pallas kernels for 0%

profile of v5, /device:TPU:1, one launch (start us, length us, event | category | flops | bytes accessed | tf_op | source)
XLA Modules:
  0.0 91.3 jit_solution(6948214918083020410)
XLA Ops:
  0.6 0.0 copy-start
  0.6 0.0 copy-start.3
  0.7 2.1 %copy.15 = f32[1,1,512,9,128]{2,4,3,1,0:T(8,128)S(1)} copy(f32[1,1,512,9,128]{4,2,3,1,0:T(8,128)} %param.7) | data formatting | bytes 4718592 | tf_op args[1]
  2.8 0.0 copy-done
  2.8 0.1 copy.14
  3.6 3.5 %fusion.12 = f32[10,384,128]{1,2,0:T(8,128)} fusion(f32[512,9,128]{0,2,1:T(8,128)S(1)} %bitcast.50, f32[512,1,128]{0,2,1:T(8,128)S(1)} %bitcast.51, s32[512]{0:T(512)S(1)} %fusion.44, pred[512]{0:T(512)(128)(4,1)S(1)} %iota_compare_fusion.3), kind=kOutput, calls=%fused_computation.21 | convolution fusion | flops 3020947456 | bytes 4590080 | tf_op jit(solution)/shard_map/ls,scn->cln/dot_general | solution.py:33
  7.1 1.9 %copy.16 = f32[10,384,128]{2,1,0:T(8,128)S(1)} copy(f32[10,384,128]{1,2,0:T(8,128)} %fusion.12) | data formatting | bytes 3932160 | tf_op jit(solution)/shard_map/ls,scn->cln/transpose | solution.py:33
  9.1 0.0 copy-done.2
  9.1 1.0 %fusion.46 = f32[4,3840]{1,0:T(4,128)S(1)} fusion(f32[3840,128]{1,0:T(8,128)S(1)} %bitcast.47, s32[4]{0:T(128)S(1)} %copy-done.2), kind=kOutput, calls=%fused_computation.98 | convolution fusion | flops 23593472 | bytes 2027536 | tf_op jit(solution)/shard_map/jn,mn->jm/dot_general | solution.py:66
  10.1 0.1 reshape.152
  10.1 4.6 %collective-permute-start.3 = (f32[2,1280]{1,0:T(2,128)S(1)}, f32[2,1280]{1,0:T(2,128)S(1)}, u32[]{:S(2)}, u32[]{:S(2)}) collective-permute-start(f32[2,1280]{1,0:T(2,128)S(1)} %bitcast.56), channel_id=1, source_target_pairs={{1,4},{2,5},{3,6},{5,8},{6,9},{7,10},{9,12},{10,13},{11,14},{13,16... | collective-permute-start | bytes 30728 | tf_op jit(solution)/shard_map/ppermute | solution.py:27
  14.7 15.6 %collective-permute-start.4 = (f32[2,1280]{1,0:T(2,128)S(1)}, f32[2,1280]{1,0:T(2,128)S(1)}, u32[]{:S(2)}, u32[]{:S(2)}) collective-permute-start(f32[2,1280]{1,0:T(2,128)S(1)} %bitcast.53), channel_id=1, source_target_pairs={{1,508},{2,509},{3,510},{5,0},{6,1},{7,2},{9,4},{10,5},{11,6},{13,... | collective-permute-start | bytes 30728 | tf_op jit(solution)/shard_map/ppermute | solution.py:27
  30.4 1.9 %collective-permute-start.2 = (f32[2,3840]{1,0:T(2,128)S(1)}, f32[2,3840]{1,0:T(2,128)S(1)}, u32[]{:S(2)}, u32[]{:S(2)}) collective-permute-start(f32[2,3840]{1,0:T(2,128)S(1)} %get-tuple-element.23), channel_id=1, source_target_pairs={{1,0},{2,1},{3,2},{5,4},{6,5},{7,6},{9,8},{10,9},{11,10},{13,12},{... | collective-permute-start | bytes 92168 | tf_op jit(solution)/shard_map/ppermute | solution.py:27
  32.3 3.3 %collective-permute-start.6 = (f32[2,1280]{1,0:T(2,128)S(1)}, f32[2,1280]{1,0:T(2,128)S(1)}, u32[]{:S(2)}, u32[]{:S(2)}) collective-permute-start(f32[2,1280]{1,0:T(2,128)S(1)} %bitcast.55), channel_id=1, source_target_pairs={{0,5},{1,6},{2,7},{4,9},{5,10},{6,11},{8,13},{9,14},{10,15},{12,17... | collective-permute-start | bytes 30728 | tf_op jit(solution)/shard_map/ppermute | solution.py:27
  35.6 11.4 %collective-permute-start.7 = (f32[2,1280]{1,0:T(2,128)S(1)}, f32[2,1280]{1,0:T(2,128)S(1)}, u32[]{:S(2)}, u32[]{:S(2)}) collective-permute-start(f32[2,1280]{1,0:T(2,128)S(1)} %bitcast.54), channel_id=1, source_target_pairs={{0,509},{1,510},{2,511},{4,1},{5,2},{6,3},{8,5},{9,6},{10,7},{12,9... | collective-permute-start | bytes 30728 | tf_op jit(solution)/shard_map/ppermute | solution.py:27
  47.0 1.0 %fusion.56 = (f32[10,4,32,128]{3,2,1,0:T(8,128)}, f32[10,4,32,128]{3,2,1,0:T(8,128)S(1)}) fusion(f32[10,12,32,128]{3,2,1,0:T(8,128)S(1)} %bitcast.48), kind=kLoop, calls=%fused_computation.115 | loop fusion | bytes 2621440 | tf_op jit(solution)/shard_map/slice | solution.py:64
  48.0 0.0 collective-permute-done.3
  48.0 3.1 %collective-permute-start.5 = (f32[2,3840]{1,0:T(2,128)S(1)}, f32[2,3840]{1,0:T(2,128)S(1)}, u32[]{:S(2)}, u32[]{:S(2)}) collective-permute-start(f32[2,3840]{1,0:T(2,128)S(1)} %get-tuple-element.24), channel_id=1, source_target_pairs={{0,1},{1,2},{2,3},{4,5},{5,6},{6,7},{8,9},{9,10},{10,11},{12,13},{... | collective-permute-start | bytes 92168 | tf_op jit(solution)/shard_map/ppermute | solution.py:27
  51.2 0.0 collective-permute-done.4
  51.2 1.9 %collective-permute-start = (f32[10,4,32,128]{3,2,1,0:T(8,128)}, f32[10,4,32,128]{3,2,1,0:T(8,128)}, u32[]{:S(2)}, u32[]{:S(2)}) collective-permute-start(f32[10,4,32,128]{3,2,1,0:T(8,128)} %get-tuple-element.17), channel_id=1, source_target_pairs={{0,4},{1,5},{2,6},{3,7},{4,8},{5,9},{6,10},{7,11},{8,12},{9,13},{1... | collective-permute-start | bytes 1966088 | tf_op jit(solution)/shard_map/ppermute | solution.py:27
  53.1 0.0 collective-permute-done.6
  53.1 14.4 %collective-permute-start.1 = (f32[10,4,32,128]{3,2,1,0:T(8,128)S(1)}, f32[10,4,32,128]{3,2,1,0:T(8,128)}, u32[]{:S(2)}, u32[]{:S(2)}) collective-permute-start(f32[10,4,32,128]{3,2,1,0:T(8,128)S(1)} %get-tuple-element.18), channel_id=1, source_target_pairs={{0,508},{1,509},{2,510},{3,511},{4,0},{5,1},{6,2},{7,3},{8,4},{9,5... | collective-permute-start | bytes 1966088 | tf_op jit(solution)/shard_map/ppermute | solution.py:27
  67.5 0.0 collective-permute-done.7
  67.6 0.0 collective-permute-done.2
  67.6 0.0 collective-permute-done.5
  67.7 0.1 dot_general.16
  67.9 1.8 %fusion.26 = f32[10,12,32,128]{3,2,1,0:T(8,128)S(1)} fusion(f32[10,12,32,4]{2,1,0,3:T(8,128)S(1)} %dot_general.16, s32[4]{0:T(128)S(1)} %copy-done.2), kind=kOutput, calls=%fused_computation.40 | convolution fusion | flops 23593472 | bytes 2027536 | tf_op jit(solution)/shard_map/jm,jn->mn/dot_general | solution.py:86
  69.6 8.2 %collective-permute-done = f32[10,4,32,128]{3,2,1,0:T(8,128)} collective-permute-done((f32[10,4,32,128]{3,2,1,0:T(8,128)}, f32[10,4,32,128]{3,2,1,0:T(8,128)}, u32[]{:S(2)}, u32[]{:S(2)}) %collective-permute-start) | collective-permute-done | bytes 655392 | tf_op jit(solution)/shard_map/ppermute | solution.py:27
  77.8 0.6 collective-permute-done.1
  78.4 1.6 %slice_add_fusion.15 = (f32[10,4,32,128]{3,2,1,0:T(8,128)S(1)}, f32[10,4,32,128]{3,2,1,0:T(8,128)S(1)}, f32[10,4,32,128]{3,2,1,0:T(8,128)S(1)}) fusion(f32[10,4,32,128]{3,2,1,0:T(8,128)} %collective-permute-done, f32[10,12,32,128]{3,2,1,0:T(8,128)S(1)} %bitcast.49, f32[10,4,32,128]{3,2,1,0:T(8,128)} %collective-permute-done.1), kind=kLoop, calls=%fused_computation.112 | loop fusion | flops 327680 | bytes 5242880 | tf_op jit(solution)/shard_map/add | solution.py:49
  80.1 0.4 pad_maximum_fusion
  80.5 0.8 fusion.4
  81.3 1.3 %fusion.54 = (f32[10,10,32,255]{3,2,1,0:T(8,128)S(1)}, f32[10,10,32,255]{3,2,1,0:T(8,128)S(1)}) fusion(f32[10,10,32,256]{3,2,1,0:T(8,128)S(1)} %fusion.4), kind=kLoop, calls=%fused_computation.113 | loop fusion | bytes 13056000 | tf_op jit(solution)/shard_map/jit(_roll_static)/slice | solution.py:97
  82.6 0.6 fusion.55
  83.3 2.3 %fusion.7 = f32[10,10,32,256]{3,2,1,0:T(8,128)S(1)} fusion(f32[10,10,32,255]{3,2,1,0:T(8,128)S(1)} %get-tuple-element.8, f32[10,10,32,1]{3,2,1,0:T(8,128)S(1)} %get-tuple-element.10, f32[10,10,32,1]{3,2,1,0:T(8,128)S(1)} %get-tuple-element.9, f32[10,10,32,255]{3,2,1,0:T(8,128)S(1)} %get-tuple-element.7, f32[10,12,32,256]{3,2,1,0:T(8,128)S(1)} %pad_maximum_fusion), kind=kLoop, calls=%fused_computation.14 | loop fusion | flops 9830400 | bytes 19660800 | tf_op jit(solution)/shard_map/add | solution.py:97
  85.6 1.0 %fusion.2 = f32[10,10,32,256]{3,2,1,0:T(8,128)S(1)} fusion(f32[10,10,32,256]{3,2,1,0:T(8,128)S(1)} %fusion.7), kind=kLoop, calls=%fused_computation.5 | loop fusion | flops 4096000 | bytes 6553600 | tf_op jit(solution)/shard_map/add | solution.py:99
  86.5 0.1 slice.299
  86.7 0.1 slice_divide_fusion
  86.8 0.3 maximum_multiply_fusion.2
  87.1 0.2 slice.307
  87.2 0.4 slice.306
  87.6 1.2 %slice.296 = f32[10,8,32,128]{3,2,1,0:T(8,128)} slice(f32[10,10,32,256]{3,2,1,0:T(8,128)S(1)} %fusion.2), slice={[0:10], [1:9], [0:32], [0:128]} | slice | bytes 2621440 | tf_op jit(solution)/shard_map/slice | solution.py:162
  88.8 0.9 fusion.19
  89.7 0.3 fusion.16
  90.1 0.2 fusion.39
  90.3 0.0 copy-start.1
  90.3 0.8 pad_maximum_fusion.2
  91.1 0.2 copy-done.1
  (29 shorter events, 0.4 us)
Async XLA Ops:
  0.6 2.1 %copy-start = (f32[1,1,512,128]{3,2,1,0:T(8,128)S(1)}, f32[1,1,512,128]{3,2,1,0:T(8,128)}, u32[]{:S(2)}) copy-start(f32[1,1,512,128]{3,2,1,0:T(8,128)} %param.6) | copy-start | bytes 786436
  0.6 2.9 %copy-start.3 = (s32[1,1,512]{2,1,0:T(1,128)S(1)}, s32[1,1,512]{2,1,0:T(1,128)}, u32[]{:S(2)}) copy-start(s32[1,1,512]{2,1,0:T(1,128)} %param.8) | copy-start | bytes 6148
  7.1 1.9 %copy-start.2 = (s32[4]{0:T(128)S(1)}, s32[4]{0:T(128)}, u32[]{:S(2)}) copy-start(s32[4]{0:T(128)} %constant.85.clone) | copy-start | bytes 52
  10.1 37.9 %collective-permute-start.3 = (f32[2,1280]{1,0:T(2,128)S(1)}, f32[2,1280]{1,0:T(2,128)S(1)}, u32[]{:S(2)}, u32[]{:S(2)}) collective-permute-start(f32[2,1280]{1,0:T(2,128)S(1)} %bitcast.56), channel_id=1, source_target_pairs={{1,4},{2,5},{3,6},{5,8},{6,9},{7,10},{9,12},{10,13},{11,14},{13,16... | collective-permute-start | bytes 30728 | tf_op jit(solution)/shard_map/ppermute | solution.py:27
  14.7 36.4 %collective-permute-start.4 = (f32[2,1280]{1,0:T(2,128)S(1)}, f32[2,1280]{1,0:T(2,128)S(1)}, u32[]{:S(2)}, u32[]{:S(2)}) collective-permute-start(f32[2,1280]{1,0:T(2,128)S(1)} %bitcast.53), channel_id=1, source_target_pairs={{1,508},{2,509},{3,510},{5,0},{6,1},{7,2},{9,4},{10,5},{11,6},{13,... | collective-permute-start | bytes 30728 | tf_op jit(solution)/shard_map/ppermute | solution.py:27
  30.4 37.2 %collective-permute-start.2 = (f32[2,3840]{1,0:T(2,128)S(1)}, f32[2,3840]{1,0:T(2,128)S(1)}, u32[]{:S(2)}, u32[]{:S(2)}) collective-permute-start(f32[2,3840]{1,0:T(2,128)S(1)} %get-tuple-element.23), channel_id=1, source_target_pairs={{1,0},{2,1},{3,2},{5,4},{6,5},{7,6},{9,8},{10,9},{11,10},{13,12},{... | collective-permute-start | bytes 92168 | tf_op jit(solution)/shard_map/ppermute | solution.py:27
  32.3 20.8 %collective-permute-start.6 = (f32[2,1280]{1,0:T(2,128)S(1)}, f32[2,1280]{1,0:T(2,128)S(1)}, u32[]{:S(2)}, u32[]{:S(2)}) collective-permute-start(f32[2,1280]{1,0:T(2,128)S(1)} %bitcast.55), channel_id=1, source_target_pairs={{0,5},{1,6},{2,7},{4,9},{5,10},{6,11},{8,13},{9,14},{10,15},{12,17... | collective-permute-start | bytes 30728 | tf_op jit(solution)/shard_map/ppermute | solution.py:27
  35.6 31.9 %collective-permute-start.7 = (f32[2,1280]{1,0:T(2,128)S(1)}, f32[2,1280]{1,0:T(2,128)S(1)}, u32[]{:S(2)}, u32[]{:S(2)}) collective-permute-start(f32[2,1280]{1,0:T(2,128)S(1)} %bitcast.54), channel_id=1, source_target_pairs={{0,509},{1,510},{2,511},{4,1},{5,2},{6,3},{8,5},{9,6},{10,7},{12,9... | collective-permute-start | bytes 30728 | tf_op jit(solution)/shard_map/ppermute | solution.py:27
  48.0 19.6 %collective-permute-start.5 = (f32[2,3840]{1,0:T(2,128)S(1)}, f32[2,3840]{1,0:T(2,128)S(1)}, u32[]{:S(2)}, u32[]{:S(2)}) collective-permute-start(f32[2,3840]{1,0:T(2,128)S(1)} %get-tuple-element.24), channel_id=1, source_target_pairs={{0,1},{1,2},{2,3},{4,5},{5,6},{6,7},{8,9},{9,10},{10,11},{12,13},{... | collective-permute-start | bytes 92168 | tf_op jit(solution)/shard_map/ppermute | solution.py:27
  51.2 26.6 %collective-permute-start = (f32[10,4,32,128]{3,2,1,0:T(8,128)}, f32[10,4,32,128]{3,2,1,0:T(8,128)}, u32[]{:S(2)}, u32[]{:S(2)}) collective-permute-start(f32[10,4,32,128]{3,2,1,0:T(8,128)} %get-tuple-element.17), channel_id=1, source_target_pairs={{0,4},{1,5},{2,6},{3,7},{4,8},{5,9},{6,10},{7,11},{8,12},{9,13},{1... | collective-permute-start | bytes 1966088 | tf_op jit(solution)/shard_map/ppermute | solution.py:27
  53.1 25.3 %collective-permute-start.1 = (f32[10,4,32,128]{3,2,1,0:T(8,128)S(1)}, f32[10,4,32,128]{3,2,1,0:T(8,128)}, u32[]{:S(2)}, u32[]{:S(2)}) collective-permute-start(f32[10,4,32,128]{3,2,1,0:T(8,128)S(1)} %get-tuple-element.18), channel_id=1, source_target_pairs={{0,508},{1,509},{2,510},{3,511},{4,0},{5,1},{6,2},{7,3},{8,4},{9,5... | collective-permute-start | bytes 1966088 | tf_op jit(solution)/shard_map/ppermute | solution.py:27
  90.3 1.0 %copy-start.1 = (f32[6,8,32,128]{3,2,1,0:T(8,128)}, f32[6,8,32,128]{3,2,1,0:T(8,128)S(1)}, u32[]{:S(2)}) copy-start(f32[6,8,32,128]{3,2,1,0:T(8,128)S(1)} %fusion.29) | copy-start | bytes 2359300

commit v6 on v4

--- a/solution.py
+++ b/solution.py
@@ -3,6 +3,8 @@
 import jax
 import jax.numpy as jnp
 from jax import lax
+from jax.experimental import pallas as pl
+from jax.experimental.pallas import tpu as pltpu
 from jax.sharding import PartitionSpec as P
 
 CA = 8
@@ -74,7 +76,7 @@
         selector(cells, edge_cells),
         precision=lax.Precision.HIGHEST,
     )
-    return jnp.concatenate([center, edges.reshape(shape)], axis=3)
+    return center, edges.reshape(shape)
 
 
 def smooth_block(extended):
@@ -121,6 +123,89 @@
         ]
     )
     return (force, strain)
+
+
+def stencil_kernel(c_ref, x_ref, scale_ref, recip_ref, xmask_ref, sm_ref, force_ref, strain_ref, sc_ref, sx_ref):
+    rows, height, cells = sc_ref.shape[1:]
+    lane = lax.broadcasted_iota(jnp.int32, (height, cells), 1)
+    sub = lax.broadcasted_iota(jnp.int32, (height, cells), 0)
+
+    def ring(cc, xx, shift, edge):
+        rc = pltpu.roll(cc, shift, 1)
+        rx = pltpu.roll(xx, shift, 1)
+        return jnp.where(lane == edge, rx, rc), jnp.where(lane == edge, rc, rx)
+
+    def below(f):
+        return jnp.where(sub == 0, 0.0, pltpu.roll(f, 1, 0))
+
+    def above(f):
+        return jnp.where(sub == height - 1, 0.0, pltpu.roll(f, height - 1, 0))
+
+    def hsmooth(f):
+        return 0.25 * below(f) + 0.5 * f + 0.25 * above(f)
+
+    def smooth_channel(c, carry):
+        wc = [c_ref[c, j] for j in range(rows + 2)]
+        wx = [x_ref[c, j] for j in range(rows + 2)]
+        for j in range(rows):
+            f1c = 0.25 * wc[j] + 0.5 * wc[j + 1] + 0.25 * wc[j + 2]
+            f1x = 0.25 * wx[j] + 0.5 * wx[j + 1] + 0.25 * wx[j + 2]
+            pc, px = ring(f1c, f1x, 1, 0)
+            nc, nx = ring(f1c, f1x, cells - 1, cells - 1)
+            sc_ref[c, j] = hsmooth(0.25 * pc + 0.5 * f1c + 0.25 * nc)
+            sx_ref[c, j] = hsmooth(0.25 * px + 0.5 * f1x + 0.25 * nx)
+        return carry
+
+    lax.fori_loop(0, sc_ref.shape[0], smooth_channel, 0)
+    scale = scale_ref[...]
+    recip = recip_ref[...]
+    xmask = xmask_ref[...]
+
+    def comb(ref, j, k):
+        if k < 3:
+            return ref[k + 1, j] / (ref[0, j] + density_base)
+        return ref[k + 1, j]
+
+    def out_row(r, carry):
+        for c in range(sm_ref.shape[0]):
+            sm_ref[c, r] = sc_ref[c, r + 1]
+        center = [comb(sc_ref, r + 1, k) for k in range(9)]
+        grad_az = {}
+        for k in (0, 1, 2, 3, 6, 7):
+            grad_az[k] = (comb(sc_ref, r + 2, k) - comb(sc_ref, r, k)) * scale
+        grad_height = {k: (above(center[k]) - below(center[k])) * 0.5 for k in (0, 1, 2, 4, 6, 8)}
+        grad_rad = {}
+        for k in (0, 1, 2, 5, 7, 8):
+            edge = comb(sx_ref, r + 1, k) * xmask
+            pc, _ = ring(center[k], edge, 1, 0)
+            nc, _ = ring(center[k], edge, cells - 1, cells - 1)
+            grad_rad[k] = (nc - pc) * 0.5
+        force_ref[0, r] = grad_az[3] + grad_height[6] + grad_rad[7] + 2.0 * center[7] * recip
+        force_ref[1, r] = grad_az[6] + grad_height[4] + grad_rad[8]
+        force_ref[2, r] = grad_az[7] + grad_height[8] + grad_rad[5] + (center[5] - center[3]) * recip
+        strain_ref[0, r] = grad_az[0] + center[2] * recip
+        strain_ref[1, r] = grad_height[1]
+        strain_ref[2, r] = grad_rad[2]
+        strain_ref[3, r] = 0.5 * (grad_height[0] + grad_az[1])
+        strain_ref[4, r] = 0.5 * (grad_rad[0] + grad_az[2] - center[0] * recip)
+        strain_ref[5, r] = 0.5 * (grad_rad[1] + grad_height[2])
+        return carry
+
+    lax.fori_loop(0, sm_ref.shape[1], out_row, 0)
+
+
+def stencil(center, edges, scale_az, recip, xmask):
+    channels, rows, height, cells = center.shape
+    own = rows - 2 * HALO
+    vmem = pl.BlockSpec(memory_space=pltpu.VMEM)
+    shape = lambda n: jax.ShapeDtypeStruct((n, own, height, cells), jnp.float32)
+    return pl.pallas_call(
+        stencil_kernel,
+        out_shape=(shape(channels), shape(3), shape(6)),
+        in_specs=[vmem] * 5,
+        out_specs=(vmem, vmem, vmem),
+        scratch_shapes=[pltpu.VMEM((channels, rows - 2, height, cells), jnp.float32)] * 2,
+    )(center, edges, scale_az.reshape(1, cells), recip.reshape(1, cells), xmask.reshape(1, cells))
 
 
 def local(block_mass, block_flux, block_dest, block_count):
@@ -137,20 +222,14 @@
     slot_index = jnp.arange(slots, dtype=jnp.int32)
     live = slot_index < block_count[0, 0]
     raw = local_rows(values, dest, live, start, total_rows, width)
-    extended = window(raw)
+    center, edges = window(raw)
     glob_cells = (band_index * width + jnp.arange(width, dtype=jnp.int32)).astype(jnp.float32)
     radius = width * n_rad + glob_cells + 0.5
     dtheta = 2.0 * math.pi / total_rows
     scale_az = 0.5 / (radius * dtheta)
     recip = 1.0 / radius
-    smoothed_ext = smooth_block(extended)
-    smoothed = smoothed_ext[:, 1:-1, :, :width]
-    velocity = smoothed_ext[1:4] / (smoothed_ext[0:1] + density_base)
-    combined = jnp.concatenate([velocity, smoothed_ext[4:]], axis=0)
-    combined = ring_mask(combined, band_index, width, n_rad)
-    grad_az, grad_height, grad_rad, center = gradients(combined, scale_az, width)
-    force, strain = assemble(grad_az, grad_height, grad_rad, center, recip)
-    return (smoothed, force, strain)
+    xmask = ring_mask(jnp.ones((2 * width,), jnp.float32), band_index, width, n_rad)[width:]
+    return stencil(center, edges, scale_az, recip, xmask)
 
 
 def solution(mesh):

time: 77.2 us -> 75.7 us (0.981)
  Pallas kernels: 0 us -> 7.61 us
  other arithmetic: 7.72 us -> 1.73 us
  local copies, waits for them, and re-layouts: 9.81 us -> 6.73 us
  matrix products: 6.26 us -> 7.51 us
  waiting for transfers between devices: 38.8 us -> 37.8 us
    pallas_call x0 -> x1, Pallas kernels: none -> 7.61 us  [stencil(): pl.pallas_call(stencil_kernel, out_shape=(shape(channels), shape(3), shap...]
    add x4 -> x0, other arithmetic: 4.22 us -> none  [the longest x1 2.29 us: smooth_block(): 0.25 * jnp.roll(fields, 1, 3) + 0.5 * fields]
    slice x6 -> x0, local copies, waits for them, and re-layouts: 3.78 us -> none  [the longest x2 1.93 us: smooth_block(): jnp.roll(fields, -1, 3)]
    mul x4 -> x0, other arithmetic: 1.48 us -> none  [the longest x1 0.93 us: gradients(): (extended[:, 2:, :, :width] - extended[:, :-2, :, :width]) * scale_az]
    dot_general x1, matrix products: 1.72 us -> 2.98 us  [window(): jnp.einsum('jm,jn->mn', jnp.concatenate([right, left], axis=0), selector(...]
    ppermute x4, waiting for transfers between devices: 38.8 us -> 37.8 us  [shifted(): return lax.ppermute(value, ('az', 'rad'), pairs)]
    another operation x2 -> x0, other arithmetic: 0.84 us -> none  [the longest x1 0.82 us: assemble(): jnp.stack([grad_az[3] + grad_height[6] + grad_rad[7] + 2.0 * center[7] *...]
    unnamed x12 -> x8, local copies, waits for them, and re-layouts: 2.91 us -> 3.62 us
  transfers between devices with their start and end apart: 4 -> 4, of which waited for: 3 -> 3; matrix products, arithmetic and copies ran while one was open for 0% -> 2% of each run, Pallas kernels for 0% -> 0%
where the time goes in v6:
time: 75.7 us; the launch traced here: 75.4 us
  waiting for transfers between devices  37.8 us (50%)
  starting transfers between devices  12.6 us (17%)
  Pallas kernels  7.61 us (10%)
  matrix products  7.51 us (10%)
  local copies, waits for them, and re-layouts  6.73 us (9%)
  other arithmetic  1.73 us (2%)
  between operations  1.42 us (2%)
    ppermute x4, waiting for transfers between devices, shifted(): return lax.ppermute(value, ('az', 'rad'), pairs)  37.8 us
    ppermute x4, starting transfers between devices, shifted(): return lax.ppermute(value, ('az', 'rad'), pairs)  12.6 us
    pallas_call x1, Pallas kernels, stencil(): pl.pallas_call(stencil_kernel, out_shape=(shape(channels), shape(3), shap...  7.61 us
    unnamed x8, local copies, waits for them, and re-layouts  3.62 us
    dot_general x1, matrix products, deposit(): jnp.einsum('ls,scn->cln', onehot, values, precision=lax.Precision.HIGHEST)  3.54 us
    dot_general x1, matrix products, window(): jnp.einsum('jm,jn->mn', jnp.concatenate([right, left], axis=0), selector(...  2.98 us
    transpose x1, local copies, waits for them, and re-layouts, deposit(): jnp.einsum('ls,scn->cln', onehot, values, precision=lax.Precision.HIGHEST)  1.88 us
  transfers between devices with their start and end apart: 4, of which 3 were waited for; matrix products, arithmetic and copies ran while one was open for 2% of the time, Pallas kernels for 0%

profile of v6, /device:TPU:510, one launch (start us, length us, event | category | flops | bytes accessed | tf_op | source)
XLA Modules:
  0.0 75.4 jit_solution(11847287498181141277)
XLA Ops:
  1.3 1.1 %copy.9 = f32[1,1,512,128]{2,3,1,0:T(8,128)S(1)} copy(f32[1,1,512,128]{3,2,1,0:T(8,128)} %param.6) | data formatting | bytes 524288 | tf_op args[0]
  2.4 0.0 copy-start.2
  2.4 2.1 %copy.10 = f32[1,1,512,9,128]{2,4,3,1,0:T(8,128)S(1)} copy(f32[1,1,512,9,128]{4,2,3,1,0:T(8,128)} %param.7) | data formatting | bytes 4718592 | tf_op args[1]
  4.5 0.0 copy-done.2
  4.5 3.5 %fusion.4 = f32[10,384,128]{1,2,0:T(8,128)} fusion(f32[512,9,128]{0,2,1:T(8,128)S(1)} %bitcast.19, f32[512,1,128]{0,2,1:T(8,128)S(1)} %bitcast.21, s32[512]{0:T(512)S(1)} %fusion.20, pred[512]{0:T(512)(128)(4,1)S(1)} %iota_compare_fusion.4), kind=kOutput, calls=%fused_computation.5 | convolution fusion | flops 3020947456 | bytes 4590080 | tf_op jit(solution)/shard_map/ls,scn->cln/dot_general | solution.py:35
  8.0 1.9 %copy.11 = f32[10,384,128]{2,1,0:T(8,128)S(1)} copy(f32[10,384,128]{1,2,0:T(8,128)} %fusion.4) | data formatting | bytes 3932160 | tf_op jit(solution)/shard_map/ls,scn->cln/transpose | solution.py:35
  9.9 1.2 %fusion.30 = (f32[10,4,32,128]{3,2,1,0:T(8,128)}, f32[10,4,32,128]{3,2,1,0:T(8,128)}) fusion(f32[10,12,32,128]{3,2,1,0:T(8,128)S(1)} %bitcast.17), kind=kLoop, calls=%fused_computation.47 | loop fusion | bytes 2621440 | tf_op jit(solution)/shard_map/slice | solution.py:63
  11.1 6.4 %collective-permute-start = (f32[10,4,32,128]{3,2,1,0:T(8,128)}, f32[10,4,32,128]{3,2,1,0:T(8,128)S(1)}, u32[]{:S(2)}, u32[]{:S(2)}) collective-permute-start(f32[10,4,32,128]{3,2,1,0:T(8,128)} %get-tuple-element.6), channel_id=1, source_target_pairs={{0,4},{1,5},{2,6},{3,7},{4,8},{5,9},{6,10},{7,11},{8,12},{9,13},{1... | collective-permute-start | bytes 1966088 | tf_op jit(solution)/shard_map/ppermute | solution.py:29
  17.5 1.9 %collective-permute-start.1 = (f32[10,4,32,128]{3,2,1,0:T(8,128)}, f32[10,4,32,128]{3,2,1,0:T(8,128)S(1)}, u32[]{:S(2)}, u32[]{:S(2)}) collective-permute-start(f32[10,4,32,128]{3,2,1,0:T(8,128)} %get-tuple-element.7), channel_id=1, source_target_pairs={{0,508},{1,509},{2,510},{3,511},{4,0},{5,1},{6,2},{7,3},{8,4},{9,5... | collective-permute-start | bytes 1966088 | tf_op jit(solution)/shard_map/ppermute | solution.py:29
  19.4 0.6 fusion.26.xmask_ref
  20.0 11.7 %collective-permute-done = f32[10,4,32,128]{3,2,1,0:T(8,128)S(1)} collective-permute-done((f32[10,4,32,128]{3,2,1,0:T(8,128)}, f32[10,4,32,128]{3,2,1,0:T(8,128)S(1)}, u32[]{:S(2)}, u32[]{:S(2)}) %collective-permute-start) | collective-permute-done | bytes 655392 | tf_op jit(solution)/shard_map/ppermute | solution.py:29
  31.8 15.1 %collective-permute-done.1 = f32[10,4,32,128]{3,2,1,0:T(8,128)S(1)} collective-permute-done((f32[10,4,32,128]{3,2,1,0:T(8,128)}, f32[10,4,32,128]{3,2,1,0:T(8,128)S(1)}, u32[]{:S(2)}, u32[]{:S(2)}) %collective-permute-start.1) | collective-permute-done | bytes 655392 | tf_op jit(solution)/shard_map/ppermute | solution.py:29
  46.9 0.4 slice_add_fusion.1
  47.2 0.0 copy-start.1
  47.3 0.2 pad_maximum_fusion.c_ref
  47.4 0.0 copy-start
  47.4 0.5 copy-done.1
  47.9 1.0 %fusion.21 = f32[4,3840]{1,0:T(4,128)S(1)} fusion(f32[3840,128]{1,0:T(8,128)S(1)} %bitcast.16, s32[4]{0:T(128)S(1)} %copy-done.1), kind=kOutput, calls=%fused_computation.30 | convolution fusion | flops 23593472 | bytes 2027536 | tf_op jit(solution)/shard_map/jn,mn->jm/dot_general | solution.py:68
  48.9 1.9 %collective-permute-start.2 = (f32[2,3840]{1,0:T(2,128)S(1)}, f32[2,3840]{1,0:T(2,128)S(1)}, u32[]{:S(2)}, u32[]{:S(2)}) collective-permute-start(f32[2,3840]{1,0:T(2,128)S(1)} %get-tuple-element.8), channel_id=1, source_target_pairs={{1,0},{2,1},{3,2},{5,4},{6,5},{7,6},{9,8},{10,9},{11,10},{13,12},{... | collective-permute-start | bytes 92168 | tf_op jit(solution)/shard_map/ppermute | solution.py:29
  50.9 2.4 %collective-permute-start.3 = (f32[2,3840]{1,0:T(2,128)S(1)}, f32[2,3840]{1,0:T(2,128)S(1)}, u32[]{:S(2)}, u32[]{:S(2)}) collective-permute-start(f32[2,3840]{1,0:T(2,128)S(1)} %get-tuple-element.9), channel_id=1, source_target_pairs={{0,1},{1,2},{2,3},{4,5},{5,6},{6,7},{8,9},{9,10},{10,11},{12,13},{... | collective-permute-start | bytes 92168 | tf_op jit(solution)/shard_map/ppermute | solution.py:29
  53.3 0.6 multiply_divide_fusion
  53.9 0.0 collective-permute-done.2
  53.9 10.9 %collective-permute-done.3 = f32[2,3840]{1,0:T(2,128)S(1)} collective-permute-done((f32[2,3840]{1,0:T(2,128)S(1)}, f32[2,3840]{1,0:T(2,128)S(1)}, u32[]{:S(2)}, u32[]{:S(2)}) %collective-permute-start.3) | collective-permute-done | bytes 30752 | tf_op jit(solution)/shard_map/ppermute | solution.py:29
  64.8 3.0 %fusion.12 = f32[3840,128]{1,0:T(8,128)} fusion(f32[2,3840]{1,0:T(2,128)S(1)} %collective-permute-done.3, f32[2,3840]{1,0:T(2,128)S(1)} %collective-permute-done.2, s32[4]{0:T(128)S(1)} %copy-done.1), kind=kOutput, calls=%fused_computation.11 | convolution fusion | flops 23608832 | bytes 2027536 | tf_op jit(solution)/shard_map/jm,jn->mn/dot_general | solution.py:73
  67.8 0.0 copy-done
  67.8 7.6 %shard_map.85 = (f32[10,8,32,128]{3,2,1,0:T(8,128)}, f32[3,8,32,128]{3,2,1,0:T(8,128)}, f32[6,8,32,128]{3,2,1,0:T(8,128)}) custom-call(f32[10,12,32,128]{3,2,1,0:T(8,128)} %copy-done, f32[10,12,32,128]{3,2,1,0:T(8,128)} %bitcast.20, f32[1,128]{1,0:T(1,128)} %get-tuple-element.10.scale_ref, f32[1,128]{1,0:T(1,128)} %get-tuple-element.11.recip_ref, ...), custom_call_target="tpu_custom_call" | custom-call | tf_op jit(solution)/shard_map/pallas_call | solution.py:202
  (4 shorter events, 0.1 us)
Async XLA Ops:
  2.4 2.1 %copy-start.2 = (s32[1,1,512]{2,1,0:T(1,128)S(1)}, s32[1,1,512]{2,1,0:T(1,128)}, u32[]{:S(2)}) copy-start(s32[1,1,512]{2,1,0:T(1,128)} %param.8) | copy-start | bytes 6148
  11.1 20.6 %collective-permute-start = (f32[10,4,32,128]{3,2,1,0:T(8,128)}, f32[10,4,32,128]{3,2,1,0:T(8,128)S(1)}, u32[]{:S(2)}, u32[]{:S(2)}) collective-permute-start(f32[10,4,32,128]{3,2,1,0:T(8,128)} %get-tuple-element.6), channel_id=1, source_target_pairs={{0,4},{1,5},{2,6},{3,7},{4,8},{5,9},{6,10},{7,11},{8,12},{9,13},{1... | collective-permute-start | bytes 1966088 | tf_op jit(solution)/shard_map/ppermute | solution.py:29
  17.5 29.4 %collective-permute-start.1 = (f32[10,4,32,128]{3,2,1,0:T(8,128)}, f32[10,4,32,128]{3,2,1,0:T(8,128)S(1)}, u32[]{:S(2)}, u32[]{:S(2)}) collective-permute-start(f32[10,4,32,128]{3,2,1,0:T(8,128)} %get-tuple-element.7), channel_id=1, source_target_pairs={{0,508},{1,509},{2,510},{3,511},{4,0},{5,1},{6,2},{7,3},{8,4},{9,5... | collective-permute-start | bytes 1966088 | tf_op jit(solution)/shard_map/ppermute | solution.py:29
  47.2 0.7 copy-start.1
  47.4 20.4 %copy-start = (f32[10,12,32,128]{3,2,1,0:T(8,128)}, f32[10,12,32,128]{3,2,1,0:T(8,128)S(1)}, u32[]{:S(2)}) copy-start(f32[10,12,32,128]{3,2,1,0:T(8,128)S(1)} %pad_maximum_fusion.c_ref) | copy-start | bytes 5898244
  48.9 4.9 %collective-permute-start.2 = (f32[2,3840]{1,0:T(2,128)S(1)}, f32[2,3840]{1,0:T(2,128)S(1)}, u32[]{:S(2)}, u32[]{:S(2)}) collective-permute-start(f32[2,3840]{1,0:T(2,128)S(1)} %get-tuple-element.8), channel_id=1, source_target_pairs={{1,0},{2,1},{3,2},{5,4},{6,5},{7,6},{9,8},{10,9},{11,10},{13,12},{... | collective-permute-start | bytes 92168 | tf_op jit(solution)/shard_map/ppermute | solution.py:29
  50.9 13.9 %collective-permute-start.3 = (f32[2,3840]{1,0:T(2,128)S(1)}, f32[2,3840]{1,0:T(2,128)S(1)}, u32[]{:S(2)}, u32[]{:S(2)}) collective-permute-start(f32[2,3840]{1,0:T(2,128)S(1)} %get-tuple-element.9), channel_id=1, source_target_pairs={{0,1},{1,2},{2,3},{4,5},{5,6},{6,7},{8,9},{9,10},{10,11},{12,13},{... | collective-permute-start | bytes 92168 | tf_op jit(solution)/shard_map/ppermute | solution.py:29

commit v7 on v6

--- a/solution.py
+++ b/solution.py
@@ -35,13 +35,11 @@
     return jnp.einsum("ls,scn->cln", onehot, values, precision=lax.Precision.HIGHEST)
 
 
-def local_rows(values, dest, live, start, total_rows, width):
+def local_rows(values, dest, live, start, total_rows, width, lines):
     local_row = jnp.mod(dest // H - start + HALO, total_rows)
     line = local_row * H + dest % H
-    onehot = (
-        (jnp.arange((CA + 2 * HALO) * H, dtype=jnp.int32)[:, None] == line[None, :]) & live[None, :]
-    ).astype(jnp.float32)
-    return deposit(onehot, values).reshape(10, CA + 2 * HALO, H, width)
+    onehot = ((lines[:, None] == line[None, :]) & live[None, :]).astype(jnp.float32)
+    return deposit(onehot, values).reshape(10, -1, H, width)
 
 
 def add_rows(base, head, tail):
@@ -58,9 +56,13 @@
     )
 
 
-def window(raw):
+def window(outer, inner):
     k = 2 * HALO
-    center = add_rows(raw, shifted(raw[:, -k:], 1, 0), shifted(raw[:, :k], -1, 0))
+    top = outer[:, :k]
+    bottom = outer[:, k:]
+    from_prev = shifted(bottom, 1, 0)
+    from_next = shifted(top, -1, 0)
+    center = jnp.concatenate([top + from_prev, inner(), bottom + from_next], axis=1)
     shape = center.shape
     cells = shape[3]
     flat = center.reshape(-1, cells)
@@ -221,8 +223,11 @@
     dest = block_dest[0, 0]
     slot_index = jnp.arange(slots, dtype=jnp.int32)
     live = slot_index < block_count[0, 0]
-    raw = local_rows(values, dest, live, start, total_rows, width)
-    center, edges = window(raw)
+    k = 2 * HALO * H
+    lines = jnp.arange((CA + 2 * HALO) * H, dtype=jnp.int32)
+    outer = local_rows(values, dest, live, start, total_rows, width, jnp.concatenate([lines[:k], lines[-k:]]))
+    inner = lambda: local_rows(values, dest, live, start, total_rows, width, lines[k:-k])
+    center, edges = window(outer, inner)
     glob_cells = (band_index * width + jnp.arange(width, dtype=jnp.int32)).astype(jnp.float32)
     radius = width * n_rad + glob_cells + 0.5
     dtheta = 2.0 * math.pi / total_rows

time: 75.7 us -> 77.9 us (1.029)
  local copies, waits for them, and re-layouts: 6.73 us -> 8.75 us
  waiting for transfers between devices: 37.8 us -> 36 us
  other arithmetic: 1.73 us -> 2.94 us
    ppermute x4, waiting for transfers between devices: 37.8 us -> 36 us  [shifted(): return lax.ppermute(value, ('az', 'rad'), pairs)]
    add x1, other arithmetic: 0.35 us -> 1.56 us  [window(): top + from_prev]
    slice x1 -> x4, local copies, waits for them, and re-layouts: 1.19 us -> 2.27 us  [the longest x1 2.26 us: window(): bottom = outer[:, k:]]
    transpose x1, local copies, waits for them, and re-layouts: 1.88 us -> 2.81 us  [deposit(): jnp.einsum('ls,scn->cln', onehot, values, precision=lax.Precision.HIGHEST)]
    dot_general x1 -> x2, matrix products: 3.54 us -> 4.18 us  [deposit(): jnp.einsum('ls,scn->cln', onehot, values, precision=lax.Precision.HIGHEST)]
    unnamed x8 -> x10, local copies, waits for them, and re-layouts: 3.62 us -> 3.62 us
  transfers between devices with their start and end apart: 4 -> 4, of which waited for: 3 -> 3; matrix products, arithmetic and copies ran while one was open for 2% -> 4% of each run, Pallas kernels for 0% -> 0%
where the time goes in v7:
time: 77.9 us; the launch traced here: 77.5 us
  waiting for transfers between devices  36 us (46%)
  starting transfers between devices  12.6 us (16%)
  local copies, waits for them, and re-layouts  8.75 us (11%)
  matrix products  8.14 us (10%)
  Pallas kernels  7.61 us (10%)
  other arithmetic  2.94 us (4%)
  between operations  1.48 us (2%)
    ppermute x4, waiting for transfers between devices, shifted(): return lax.ppermute(value, ('az', 'rad'), pairs)  36 us
    ppermute x4, starting transfers between devices, shifted(): return lax.ppermute(value, ('az', 'rad'), pairs)  12.6 us
    pallas_call x1, Pallas kernels, stencil(): pl.pallas_call(stencil_kernel, out_shape=(shape(channels), shape(3), shap...  7.61 us
    dot_general x2, matrix products, deposit(): jnp.einsum('ls,scn->cln', onehot, values, precision=lax.Precision.HIGHEST)  4.18 us
    unnamed x10, local copies, waits for them, and re-layouts  3.62 us
    dot_general x1, matrix products, window(): jnp.einsum('jm,jn->mn', jnp.concatenate([right, left], axis=0), selector(...  2.98 us
    transpose x1, local copies, waits for them, and re-layouts, deposit(): jnp.einsum('ls,scn->cln', onehot, values, precision=lax.Precision.HIGHEST)  2.81 us
    slice x1, local copies, waits for them, and re-layouts, window(): bottom = outer[:, k:]  2.26 us
  transfers between devices with their start and end apart: 4, of which 3 were waited for; matrix products, arithmetic and copies ran while one was open for 4% of the time, Pallas kernels for 0%

profile of v7, /device:TPU:510, one launch (start us, length us, event | category | flops | bytes accessed | tf_op | source)
XLA Modules:
  0.0 77.5 jit_solution(13187176231015241267)
XLA Ops:
  1.3 1.1 %copy.9 = f32[1,1,512,128]{2,3,1,0:T(8,128)S(1)} copy(f32[1,1,512,128]{3,2,1,0:T(8,128)} %param.6) | data formatting | bytes 524288 | tf_op args[0]
  2.4 0.0 copy-start.3
  2.4 2.1 %copy.10 = f32[1,1,512,9,128]{2,4,3,1,0:T(8,128)S(1)} copy(f32[1,1,512,9,128]{4,2,3,1,0:T(8,128)} %param.7) | data formatting | bytes 4718592 | tf_op args[1]
  4.5 0.0 copy-done.3
  4.5 2.5 %fusion.2 = f32[10,256,128]{1,2,0:T(8,128)} fusion(f32[512,9,128]{0,2,1:T(8,128)S(1)} %bitcast.22, f32[512,1,128]{0,2,1:T(8,128)S(1)} %bitcast.29, s32[512]{0:T(512)S(1)} %fusion.23, s32[256]{0:T(256)S(1)} %pad_add_fusion, pred[512]{0:T(512)(128)(4,1)S(1)} %iota_compare_fusion.3), kind=kOutput, calls=%fused_computation.4 | convolution fusion | flops 2014183424 | bytes 3935744 | tf_op jit(solution)/shard_map/ls,scn->cln/dot_general | solution.py:35
  7.1 2.8 %copy.11 = f32[10,256,128]{2,1,0:T(8,128)} copy(f32[10,256,128]{1,2,0:T(8,128)} %fusion.2) | data formatting | bytes 2621440 | tf_op jit(solution)/shard_map/ls,scn->cln/transpose | solution.py:35
  9.9 2.3 %fusion.34 = (f32[10,4,32,128]{3,2,1,0:T(8,128)}, f32[10,4,32,128]{3,2,1,0:T(8,128)S(1)}) fusion(f32[10,8,32,128]{3,2,1,0:T(8,128)} %bitcast.25), kind=kLoop, calls=%fused_computation.55 | loop fusion | bytes 2621440 | tf_op jit(solution)/shard_map/slice | solution.py:62
  12.2 6.4 %collective-permute-start = (f32[10,4,32,128]{3,2,1,0:T(8,128)}, f32[10,4,32,128]{3,2,1,0:T(8,128)}, u32[]{:S(2)}, u32[]{:S(2)}) collective-permute-start(f32[10,4,32,128]{3,2,1,0:T(8,128)} %get-tuple-element.5), channel_id=1, source_target_pairs={{0,4},{1,5},{2,6},{3,7},{4,8},{5,9},{6,10},{7,11},{8,12},{9,13},{1... | collective-permute-start | bytes 1966088 | tf_op jit(solution)/shard_map/ppermute | solution.py:29
  18.5 1.9 %collective-permute-start.1 = (f32[10,4,32,128]{3,2,1,0:T(8,128)S(1)}, f32[10,4,32,128]{3,2,1,0:T(8,128)}, u32[]{:S(2)}, u32[]{:S(2)}) collective-permute-start(f32[10,4,32,128]{3,2,1,0:T(8,128)S(1)} %get-tuple-element.6), channel_id=1, source_target_pairs={{0,508},{1,509},{2,510},{3,511},{4,0},{5,1},{6,2},{7,3},{8,4},{9,5... | collective-permute-start | bytes 1966088 | tf_op jit(solution)/shard_map/ppermute | solution.py:29
  20.5 0.0 copy-start.1
  20.5 0.6 fusion.29.xmask_ref
  21.1 1.6 %fusion = f32[10,128,128]{1,2,0:T(8,128)S(1)} fusion(f32[512,9,128]{0,2,1:T(8,128)S(1)} %bitcast.23, f32[512,1,128]{0,2,1:T(8,128)S(1)} %bitcast.30, s32[512]{0:T(512)S(1)} %fusion.23, s32[128]{0:T(128)S(1)} %slice.29, pred[512]{0:T(512)(128)(4,1)S(1)} %iota_compare_fusion.3), kind=kOutput, calls=%fused_computation.1 | convolution fusion | flops 1007419392 | bytes 3279872 | tf_op jit(solution)/shard_map/ls,scn->cln/dot_general | solution.py:35
  22.7 10.1 %collective-permute-done = f32[10,4,32,128]{3,2,1,0:T(8,128)} collective-permute-done((f32[10,4,32,128]{3,2,1,0:T(8,128)}, f32[10,4,32,128]{3,2,1,0:T(8,128)}, u32[]{:S(2)}, u32[]{:S(2)}) %collective-permute-start) | collective-permute-done | bytes 655392 | tf_op jit(solution)/shard_map/ppermute | solution.py:29
  32.8 15.0 %collective-permute-done.1 = f32[10,4,32,128]{3,2,1,0:T(8,128)} collective-permute-done((f32[10,4,32,128]{3,2,1,0:T(8,128)S(1)}, f32[10,4,32,128]{3,2,1,0:T(8,128)}, u32[]{:S(2)}, u32[]{:S(2)}) %collective-permute-start.1) | collective-permute-done | bytes 655392 | tf_op jit(solution)/shard_map/ppermute | solution.py:29
  47.8 0.0 copy-done.1
  47.8 1.6 %slice_add_fusion.1 = (f32[10,4,32,128]{3,2,1,0:T(8,128)S(1)}, f32[10,4,32,128]{3,2,1,0:T(8,128)S(1)}) fusion(f32[10,4,32,128]{3,2,1,0:T(8,128)} %collective-permute-done, f32[10,8,32,128]{3,2,1,0:T(8,128)S(1)} %bitcast.26, f32[10,4,32,128]{3,2,1,0:T(8,128)} %collective-permute-done.1), kind=kLoop, calls=%fused_computation.54 | loop fusion | flops 327680 | bytes 3932160 | tf_op jit(solution)/shard_map/add | solution.py:65
  49.4 0.0 copy-start.2
  49.4 0.2 pad_maximum_fusion.3.c_ref
  49.6 0.0 copy-start
  49.6 0.5 copy-done.2
  50.1 1.0 %fusion.24 = f32[4,3840]{1,0:T(4,128)S(1)} fusion(f32[3840,128]{1,0:T(8,128)S(1)} %bitcast.24, s32[4]{0:T(128)S(1)} %copy-done.2), kind=kOutput, calls=%fused_computation.36 | convolution fusion | flops 23593472 | bytes 2027536 | tf_op jit(solution)/shard_map/jn,mn->jm/dot_general | solution.py:70
  51.1 1.9 %collective-permute-start.2 = (f32[2,3840]{1,0:T(2,128)S(1)}, f32[2,3840]{1,0:T(2,128)S(1)}, u32[]{:S(2)}, u32[]{:S(2)}) collective-permute-start(f32[2,3840]{1,0:T(2,128)S(1)} %get-tuple-element.7), channel_id=1, source_target_pairs={{1,0},{2,1},{3,2},{5,4},{6,5},{7,6},{9,8},{10,9},{11,10},{13,12},{... | collective-permute-start | bytes 92168 | tf_op jit(solution)/shard_map/ppermute | solution.py:29
  53.0 2.4 %collective-permute-start.3 = (f32[2,3840]{1,0:T(2,128)S(1)}, f32[2,3840]{1,0:T(2,128)S(1)}, u32[]{:S(2)}, u32[]{:S(2)}) collective-permute-start(f32[2,3840]{1,0:T(2,128)S(1)} %get-tuple-element.8), channel_id=1, source_target_pairs={{0,1},{1,2},{2,3},{4,5},{5,6},{6,7},{8,9},{9,10},{10,11},{12,13},{... | collective-permute-start | bytes 92168 | tf_op jit(solution)/shard_map/ppermute | solution.py:29
  55.4 0.6 multiply_divide_fusion
  56.0 0.0 collective-permute-done.2
  56.0 10.9 %collective-permute-done.3 = f32[2,3840]{1,0:T(2,128)S(1)} collective-permute-done((f32[2,3840]{1,0:T(2,128)S(1)}, f32[2,3840]{1,0:T(2,128)S(1)}, u32[]{:S(2)}, u32[]{:S(2)}) %collective-permute-start.3) | collective-permute-done | bytes 30752 | tf_op jit(solution)/shard_map/ppermute | solution.py:29
  67.0 3.0 %fusion.15 = f32[3840,128]{1,0:T(8,128)} fusion(f32[2,3840]{1,0:T(2,128)S(1)} %collective-permute-done.3, f32[2,3840]{1,0:T(2,128)S(1)} %collective-permute-done.2, s32[4]{0:T(128)S(1)} %copy-done.2), kind=kOutput, calls=%fused_computation.17 | convolution fusion | flops 23608832 | bytes 2027536 | tf_op jit(solution)/shard_map/jm,jn->mn/dot_general | solution.py:75
  69.9 0.0 copy-done
  69.9 7.6 %shard_map.85 = (f32[10,8,32,128]{3,2,1,0:T(8,128)}, f32[3,8,32,128]{3,2,1,0:T(8,128)}, f32[6,8,32,128]{3,2,1,0:T(8,128)}) custom-call(f32[10,12,32,128]{3,2,1,0:T(8,128)} %copy-done, f32[10,12,32,128]{3,2,1,0:T(8,128)} %bitcast.27, f32[1,128]{1,0:T(1,128)} %get-tuple-element.9.scale_ref, f32[1,128]{1,0:T(1,128)} %get-tuple-element.10.recip_ref, ...), custom_call_target="tpu_custom_call" | custom-call | tf_op jit(solution)/shard_map/pallas_call | solution.py:204
  (11 shorter events, 0.1 us)
Async XLA Ops:
  2.4 2.1 %copy-start.3 = (s32[1,1,512]{2,1,0:T(1,128)S(1)}, s32[1,1,512]{2,1,0:T(1,128)}, u32[]{:S(2)}) copy-start(s32[1,1,512]{2,1,0:T(1,128)} %param.8) | copy-start | bytes 6148
  12.2 20.6 %collective-permute-start = (f32[10,4,32,128]{3,2,1,0:T(8,128)}, f32[10,4,32,128]{3,2,1,0:T(8,128)}, u32[]{:S(2)}, u32[]{:S(2)}) collective-permute-start(f32[10,4,32,128]{3,2,1,0:T(8,128)} %get-tuple-element.5), channel_id=1, source_target_pairs={{0,4},{1,5},{2,6},{3,7},{4,8},{5,9},{6,10},{7,11},{8,12},{9,13},{1... | collective-permute-start | bytes 1966088 | tf_op jit(solution)/shard_map/ppermute | solution.py:29
  18.5 29.3 %collective-permute-start.1 = (f32[10,4,32,128]{3,2,1,0:T(8,128)S(1)}, f32[10,4,32,128]{3,2,1,0:T(8,128)}, u32[]{:S(2)}, u32[]{:S(2)}) collective-permute-start(f32[10,4,32,128]{3,2,1,0:T(8,128)S(1)} %get-tuple-element.6), channel_id=1, source_target_pairs={{0,508},{1,509},{2,510},{3,511},{4,0},{5,1},{6,2},{7,3},{8,4},{9,5... | collective-permute-start | bytes 1966088 | tf_op jit(solution)/shard_map/ppermute | solution.py:29
  20.5 27.4 %copy-start.1 = (f32[10,256,128]{2,1,0:T(8,128)S(1)}, f32[10,256,128]{2,1,0:T(8,128)}, u32[]{:S(2)}) copy-start(f32[10,256,128]{2,1,0:T(8,128)} %copy.11) | copy-start | bytes 3932164
  49.4 0.7 copy-start.2
  49.6 20.4 %copy-start = (f32[10,12,32,128]{3,2,1,0:T(8,128)}, f32[10,12,32,128]{3,2,1,0:T(8,128)S(1)}, u32[]{:S(2)}) copy-start(f32[10,12,32,128]{3,2,1,0:T(8,128)S(1)} %pad_maximum_fusion.3.c_ref) | copy-start | bytes 5898244
  51.1 5.0 %collective-permute-start.2 = (f32[2,3840]{1,0:T(2,128)S(1)}, f32[2,3840]{1,0:T(2,128)S(1)}, u32[]{:S(2)}, u32[]{:S(2)}) collective-permute-start(f32[2,3840]{1,0:T(2,128)S(1)} %get-tuple-element.7), channel_id=1, source_target_pairs={{1,0},{2,1},{3,2},{5,4},{6,5},{7,6},{9,8},{10,9},{11,10},{13,12},{... | collective-permute-start | bytes 92168 | tf_op jit(solution)/shard_map/ppermute | solution.py:29
  53.0 13.9 %collective-permute-start.3 = (f32[2,3840]{1,0:T(2,128)S(1)}, f32[2,3840]{1,0:T(2,128)S(1)}, u32[]{:S(2)}, u32[]{:S(2)}) collective-permute-start(f32[2,3840]{1,0:T(2,128)S(1)} %get-tuple-element.8), channel_id=1, source_target_pairs={{0,1},{1,2},{2,3},{4,5},{5,6},{6,7},{8,9},{9,10},{10,11},{12,13},{... | collective-permute-start | bytes 92168 | tf_op jit(solution)/shard_map/ppermute | solution.py:29

commit v8 on v6

--- a/solution.py
+++ b/solution.py
@@ -32,7 +32,8 @@
 
 
 def deposit(onehot, values):
-    return jnp.einsum("ls,scn->cln", onehot, values, precision=lax.Precision.HIGHEST)
+    out = jnp.einsum("ls,scn->lcn", onehot, values, precision=lax.Precision.HIGHEST)
+    return jnp.transpose(out, (1, 0, 2))
 
 
 def local_rows(values, dest, live, start, total_rows, width):

time: 75.7 us -> 71.3 us (0.942)
  local copies, waits for them, and re-layouts: 6.73 us -> 1.71 us
    unnamed x8 -> x4, local copies, waits for them, and re-layouts: 3.62 us -> 0.48 us
    transpose x1 -> x0, local copies, waits for them, and re-layouts: 1.88 us -> none  [deposit(): jnp.einsum('ls,scn->cln', onehot, values, precision=lax.Precision.HIGHEST)]
where the time goes in v8:
time: 71.3 us; the launch traced here: 71.1 us
  waiting for transfers between devices  37.8 us (53%)
  starting transfers between devices  12.6 us (18%)
  Pallas kernels  7.61 us (11%)
  matrix products  7.56 us (11%)
  other arithmetic  2.39 us (3%)
  local copies, waits for them, and re-layouts  1.71 us (2%)
  between operations  1.38 us (2%)
    ppermute x4, waiting for transfers between devices, shifted(): return lax.ppermute(value, ('az', 'rad'), pairs)  37.8 us
    ppermute x4, starting transfers between devices, shifted(): return lax.ppermute(value, ('az', 'rad'), pairs)  12.6 us
    pallas_call x1, Pallas kernels, stencil(): pl.pallas_call(stencil_kernel, out_shape=(shape(channels), shape(3), shap...  7.61 us
    dot_general x1, matrix products, deposit(): jnp.einsum('ls,scn->lcn', onehot, values, precision=lax.Precision.HIGHEST)  3.59 us
    dot_general x1, matrix products, window(): jnp.einsum('jm,jn->mn', jnp.concatenate([right, left], axis=0), selector(...  2.99 us
  transfers between devices with their start and end apart: 4, of which 3 were waited for; matrix products, arithmetic and copies ran while one was open for 2% of the time, Pallas kernels for 0%

profile of v8, /device:TPU:510, one launch (start us, length us, event | category | flops | bytes accessed | tf_op | source)
XLA Modules:
  0.0 71.1 jit_solution(17358712640272670781)
XLA Ops:
  1.3 0.7 fusion.17
  2.0 3.6 %fusion = f32[384,10,128]{2,0,1:T(8,128)S(1)} fusion(f32[512,9,128]{2,0,1:T(8,128)} %bitcast.20, f32[512,1,128]{2,0,1:T(8,128)} %bitcast.21, s32[512]{0:T(512)S(1)} %fusion.17, pred[512]{0:T(512)(128)(4,1)S(1)} %iota_compare_fusion.4), kind=kOutput, calls=%fused_computation | convolution fusion | flops 3020947456 | bytes 4590080 | tf_op jit(solution)/shard_map/ls,scn->lcn/dot_general | solution.py:35
  5.6 1.2 %fusion.27 = (f32[10,4,32,128]{3,2,1,0:T(8,128)}, f32[10,4,32,128]{3,2,1,0:T(8,128)}) fusion(f32[10,12,32,128]{3,2,1,0:T(8,128)S(1)} %bitcast.17), kind=kLoop, calls=%fused_computation.46 | loop fusion | bytes 2621440 | tf_op jit(solution)/shard_map/slice | solution.py:64
  6.8 6.4 %collective-permute-start = (f32[10,4,32,128]{3,2,1,0:T(8,128)}, f32[10,4,32,128]{3,2,1,0:T(8,128)S(1)}, u32[]{:S(2)}, u32[]{:S(2)}) collective-permute-start(f32[10,4,32,128]{3,2,1,0:T(8,128)} %get-tuple-element.6), channel_id=1, source_target_pairs={{0,4},{1,5},{2,6},{3,7},{4,8},{5,9},{6,10},{7,11},{8,12},{9,13},{1... | collective-permute-start | bytes 1966088 | tf_op jit(solution)/shard_map/ppermute | solution.py:29
  13.1 1.9 %collective-permute-start.1 = (f32[10,4,32,128]{3,2,1,0:T(8,128)}, f32[10,4,32,128]{3,2,1,0:T(8,128)S(1)}, u32[]{:S(2)}, u32[]{:S(2)}) collective-permute-start(f32[10,4,32,128]{3,2,1,0:T(8,128)} %get-tuple-element.7), channel_id=1, source_target_pairs={{0,508},{1,509},{2,510},{3,511},{4,0},{5,1},{6,2},{7,3},{8,4},{9,5... | collective-permute-start | bytes 1966088 | tf_op jit(solution)/shard_map/ppermute | solution.py:29
  15.1 0.6 fusion.23.xmask_ref
  15.7 11.8 %collective-permute-done = f32[10,4,32,128]{3,2,1,0:T(8,128)S(1)} collective-permute-done((f32[10,4,32,128]{3,2,1,0:T(8,128)}, f32[10,4,32,128]{3,2,1,0:T(8,128)S(1)}, u32[]{:S(2)}, u32[]{:S(2)}) %collective-permute-start) | collective-permute-done | bytes 655392 | tf_op jit(solution)/shard_map/ppermute | solution.py:29
  27.4 15.1 %collective-permute-done.1 = f32[10,4,32,128]{3,2,1,0:T(8,128)S(1)} collective-permute-done((f32[10,4,32,128]{3,2,1,0:T(8,128)}, f32[10,4,32,128]{3,2,1,0:T(8,128)S(1)}, u32[]{:S(2)}, u32[]{:S(2)}) %collective-permute-start.1) | collective-permute-done | bytes 655392 | tf_op jit(solution)/shard_map/ppermute | solution.py:29
  42.6 0.4 slice_add_fusion.1
  42.9 0.0 copy-start.1
  42.9 0.2 pad_maximum_fusion.c_ref
  43.1 0.0 copy-start
  43.1 0.5 copy-done.1
  43.6 1.0 %fusion.18 = f32[4,3840]{1,0:T(4,128)S(1)} fusion(f32[3840,128]{1,0:T(8,128)S(1)} %bitcast.16, s32[4]{0:T(128)S(1)} %copy-done.1), kind=kOutput, calls=%fused_computation.29 | convolution fusion | flops 23593472 | bytes 2027536 | tf_op jit(solution)/shard_map/jn,mn->jm/dot_general | solution.py:69
  44.6 1.9 %collective-permute-start.2 = (f32[2,3840]{1,0:T(2,128)S(1)}, f32[2,3840]{1,0:T(2,128)S(1)}, u32[]{:S(2)}, u32[]{:S(2)}) collective-permute-start(f32[2,3840]{1,0:T(2,128)S(1)} %get-tuple-element.8), channel_id=1, source_target_pairs={{1,0},{2,1},{3,2},{5,4},{6,5},{7,6},{9,8},{10,9},{11,10},{13,12},{... | collective-permute-start | bytes 92168 | tf_op jit(solution)/shard_map/ppermute | solution.py:29
  46.5 2.4 %collective-permute-start.3 = (f32[2,3840]{1,0:T(2,128)S(1)}, f32[2,3840]{1,0:T(2,128)S(1)}, u32[]{:S(2)}, u32[]{:S(2)}) collective-permute-start(f32[2,3840]{1,0:T(2,128)S(1)} %get-tuple-element.9), channel_id=1, source_target_pairs={{0,1},{1,2},{2,3},{4,5},{5,6},{6,7},{8,9},{9,10},{10,11},{12,13},{... | collective-permute-start | bytes 92168 | tf_op jit(solution)/shard_map/ppermute | solution.py:29
  49.0 0.6 multiply_divide_fusion
  49.5 0.0 collective-permute-done.2
  49.5 10.9 %collective-permute-done.3 = f32[2,3840]{1,0:T(2,128)S(1)} collective-permute-done((f32[2,3840]{1,0:T(2,128)S(1)}, f32[2,3840]{1,0:T(2,128)S(1)}, u32[]{:S(2)}, u32[]{:S(2)}) %collective-permute-start.3) | collective-permute-done | bytes 30752 | tf_op jit(solution)/shard_map/ppermute | solution.py:29
  60.5 3.0 %fusion.9 = f32[3840,128]{1,0:T(8,128)} fusion(f32[2,3840]{1,0:T(2,128)S(1)} %collective-permute-done.3, f32[2,3840]{1,0:T(2,128)S(1)} %collective-permute-done.2, s32[4]{0:T(128)S(1)} %copy-done.1), kind=kOutput, calls=%fused_computation.10 | convolution fusion | flops 23608832 | bytes 2027536 | tf_op jit(solution)/shard_map/jm,jn->mn/dot_general | solution.py:74
  63.5 0.0 copy-done
  63.5 7.6 %shard_map.85 = (f32[10,8,32,128]{3,2,1,0:T(8,128)}, f32[3,8,32,128]{3,2,1,0:T(8,128)}, f32[6,8,32,128]{3,2,1,0:T(8,128)}) custom-call(f32[10,12,32,128]{3,2,1,0:T(8,128)} %copy-done, f32[10,12,32,128]{3,2,1,0:T(8,128)} %bitcast.19, f32[1,128]{1,0:T(1,128)} %get-tuple-element.10.scale_ref, f32[1,128]{1,0:T(1,128)} %get-tuple-element.11.recip_ref, ...), custom_call_target="tpu_custom_call" | custom-call | tf_op jit(solution)/shard_map/pallas_call | solution.py:203
  (3 shorter events, 0.1 us)
Async XLA Ops:
  6.8 20.6 %collective-permute-start = (f32[10,4,32,128]{3,2,1,0:T(8,128)}, f32[10,4,32,128]{3,2,1,0:T(8,128)S(1)}, u32[]{:S(2)}, u32[]{:S(2)}) collective-permute-start(f32[10,4,32,128]{3,2,1,0:T(8,128)} %get-tuple-element.6), channel_id=1, source_target_pairs={{0,4},{1,5},{2,6},{3,7},{4,8},{5,9},{6,10},{7,11},{8,12},{9,13},{1... | collective-permute-start | bytes 1966088 | tf_op jit(solution)/shard_map/ppermute | solution.py:29
  13.1 29.4 %collective-permute-start.1 = (f32[10,4,32,128]{3,2,1,0:T(8,128)}, f32[10,4,32,128]{3,2,1,0:T(8,128)S(1)}, u32[]{:S(2)}, u32[]{:S(2)}) collective-permute-start(f32[10,4,32,128]{3,2,1,0:T(8,128)} %get-tuple-element.7), channel_id=1, source_target_pairs={{0,508},{1,509},{2,510},{3,511},{4,0},{5,1},{6,2},{7,3},{8,4},{9,5... | collective-permute-start | bytes 1966088 | tf_op jit(solution)/shard_map/ppermute | solution.py:29
  42.9 0.7 copy-start.1
  43.1 20.4 %copy-start = (f32[10,12,32,128]{3,2,1,0:T(8,128)}, f32[10,12,32,128]{3,2,1,0:T(8,128)S(1)}, u32[]{:S(2)}) copy-start(f32[10,12,32,128]{3,2,1,0:T(8,128)S(1)} %pad_maximum_fusion.c_ref) | copy-start | bytes 5898244
  44.6 4.9 %collective-permute-start.2 = (f32[2,3840]{1,0:T(2,128)S(1)}, f32[2,3840]{1,0:T(2,128)S(1)}, u32[]{:S(2)}, u32[]{:S(2)}) collective-permute-start(f32[2,3840]{1,0:T(2,128)S(1)} %get-tuple-element.8), channel_id=1, source_target_pairs={{1,0},{2,1},{3,2},{5,4},{6,5},{7,6},{9,8},{10,9},{11,10},{13,12},{... | collective-permute-start | bytes 92168 | tf_op jit(solution)/shard_map/ppermute | solution.py:29
  46.5 13.9 %collective-permute-start.3 = (f32[2,3840]{1,0:T(2,128)S(1)}, f32[2,3840]{1,0:T(2,128)S(1)}, u32[]{:S(2)}, u32[]{:S(2)}) collective-permute-start(f32[2,3840]{1,0:T(2,128)S(1)} %get-tuple-element.9), channel_id=1, source_target_pairs={{0,1},{1,2},{2,3},{4,5},{5,6},{6,7},{8,9},{9,10},{10,11},{12,13},{... | collective-permute-start | bytes 92168 | tf_op jit(solution)/shard_map/ppermute | solution.py:29

commit v9 on v8

--- a/solution.py
+++ b/solution.py
@@ -126,7 +126,9 @@
     return (force, strain)
 
 
-def stencil_kernel(c_ref, x_ref, scale_ref, recip_ref, xmask_ref, sm_ref, force_ref, strain_ref, sc_ref, sx_ref):
+def stencil_kernel(
+    c_ref, x_ref, scale_ref, recip_ref, xmask_ref, sm_ref, force_ref, strain_ref, sc_ref, sx_ref, cc_ref, cx_ref
+):
     rows, height, cells = sc_ref.shape[1:]
     lane = lax.broadcasted_iota(jnp.int32, (height, cells), 1)
     sub = lax.broadcasted_iota(jnp.int32, (height, cells), 0)
@@ -162,22 +164,29 @@
     recip = recip_ref[...]
     xmask = xmask_ref[...]
 
-    def comb(ref, j, k):
-        if k < 3:
-            return ref[k + 1, j] / (ref[0, j] + density_base)
-        return ref[k + 1, j]
+    def combine_row(j, carry):
+        dc = sc_ref[0, j] + density_base
+        dx = sx_ref[0, j] + density_base
+        for k in range(cc_ref.shape[0]):
+            if k < 3:
+                cc_ref[k, j] = sc_ref[k + 1, j] / dc
+                cx_ref[k, j] = sx_ref[k + 1, j] / dx * xmask
+            else:
+                cc_ref[k, j] = sc_ref[k + 1, j]
+                cx_ref[k, j] = sx_ref[k + 1, j] * xmask
+        return carry
+
+    lax.fori_loop(0, rows, combine_row, 0)
 
     def out_row(r, carry):
         for c in range(sm_ref.shape[0]):
             sm_ref[c, r] = sc_ref[c, r + 1]
-        center = [comb(sc_ref, r + 1, k) for k in range(9)]
-        grad_az = {}
-        for k in (0, 1, 2, 3, 6, 7):
-            grad_az[k] = (comb(sc_ref, r + 2, k) - comb(sc_ref, r, k)) * scale
+        center = [cc_ref[k, r + 1] for k in range(cc_ref.shape[0])]
+        grad_az = {k: (cc_ref[k, r + 2] - cc_ref[k, r]) * scale for k in (0, 1, 2, 3, 6, 7)}
         grad_height = {k: (above(center[k]) - below(center[k])) * 0.5 for k in (0, 1, 2, 4, 6, 8)}
         grad_rad = {}
         for k in (0, 1, 2, 5, 7, 8):
-            edge = comb(sx_ref, r + 1, k) * xmask
+            edge = cx_ref[k, r + 1]
             pc, _ = ring(center[k], edge, 1, 0)
             nc, _ = ring(center[k], edge, cells - 1, cells - 1)
             grad_rad[k] = (nc - pc) * 0.5
@@ -200,12 +209,13 @@
     own = rows - 2 * HALO
     vmem = pl.BlockSpec(memory_space=pltpu.VMEM)
     shape = lambda n: jax.ShapeDtypeStruct((n, own, height, cells), jnp.float32)
+    scratch = lambda n: pltpu.VMEM((n, rows - 2, height, cells), jnp.float32)
     return pl.pallas_call(
         stencil_kernel,
         out_shape=(shape(channels), shape(3), shape(6)),
         in_specs=[vmem] * 5,
         out_specs=(vmem, vmem, vmem),
-        scratch_shapes=[pltpu.VMEM((channels, rows - 2, height, cells), jnp.float32)] * 2,
+        scratch_shapes=[scratch(channels), scratch(channels), scratch(channels - 1), scratch(channels - 1)],
     )(center, edges, scale_az.reshape(1, cells), recip.reshape(1, cells), xmask.reshape(1, cells))
 
 

time: 71.3 us -> 71.6 us (level)
  no operation moved by 1% of the time
where the time goes in v9:
time: 71.6 us; the launch traced here: 71.3 us
  waiting for transfers between devices  37.8 us (53%)
  starting transfers between devices  12.6 us (18%)
  Pallas kernels  7.82 us (11%)
  matrix products  7.56 us (11%)
  other arithmetic  2.39 us (3%)
  local copies, waits for them, and re-layouts  1.71 us (2%)
  between operations  1.38 us (2%)
    ppermute x4, waiting for transfers between devices, shifted(): return lax.ppermute(value, ('az', 'rad'), pairs)  37.8 us
    ppermute x4, starting transfers between devices, shifted(): return lax.ppermute(value, ('az', 'rad'), pairs)  12.6 us
    pallas_call x1, Pallas kernels, stencil(): pl.pallas_call(stencil_kernel, out_shape=(shape(channels), shape(3), shap...  7.82 us
    dot_general x1, matrix products, deposit(): jnp.einsum('ls,scn->lcn', onehot, values, precision=lax.Precision.HIGHEST)  3.59 us
    dot_general x1, matrix products, window(): jnp.einsum('jm,jn->mn', jnp.concatenate([right, left], axis=0), selector(...  2.99 us
  transfers between devices with their start and end apart: 4, of which 3 were waited for; matrix products, arithmetic and copies ran while one was open for 2% of the time, Pallas kernels for 0%

profile of v9, /device:TPU:510, one launch (start us, length us, event | category | flops | bytes accessed | tf_op | source)
XLA Modules:
  0.0 71.3 jit_solution(6756929294580134442)
XLA Ops:
  1.3 0.7 fusion.17
  2.0 3.6 %fusion = f32[384,10,128]{2,0,1:T(8,128)S(1)} fusion(f32[512,9,128]{2,0,1:T(8,128)} %bitcast.20, f32[512,1,128]{2,0,1:T(8,128)} %bitcast.21, s32[512]{0:T(512)S(1)} %fusion.17, pred[512]{0:T(512)(128)(4,1)S(1)} %iota_compare_fusion.4), kind=kOutput, calls=%fused_computation | convolution fusion | flops 3020947456 | bytes 4590080 | tf_op jit(solution)/shard_map/ls,scn->lcn/dot_general | solution.py:35
  5.6 1.2 %fusion.27 = (f32[10,4,32,128]{3,2,1,0:T(8,128)}, f32[10,4,32,128]{3,2,1,0:T(8,128)}) fusion(f32[10,12,32,128]{3,2,1,0:T(8,128)S(1)} %bitcast.17), kind=kLoop, calls=%fused_computation.46 | loop fusion | bytes 2621440 | tf_op jit(solution)/shard_map/slice | solution.py:64
  6.8 6.4 %collective-permute-start = (f32[10,4,32,128]{3,2,1,0:T(8,128)}, f32[10,4,32,128]{3,2,1,0:T(8,128)S(1)}, u32[]{:S(2)}, u32[]{:S(2)}) collective-permute-start(f32[10,4,32,128]{3,2,1,0:T(8,128)} %get-tuple-element.6), channel_id=1, source_target_pairs={{0,4},{1,5},{2,6},{3,7},{4,8},{5,9},{6,10},{7,11},{8,12},{9,13},{1... | collective-permute-start | bytes 1966088 | tf_op jit(solution)/shard_map/ppermute | solution.py:29
  13.1 1.9 %collective-permute-start.1 = (f32[10,4,32,128]{3,2,1,0:T(8,128)}, f32[10,4,32,128]{3,2,1,0:T(8,128)S(1)}, u32[]{:S(2)}, u32[]{:S(2)}) collective-permute-start(f32[10,4,32,128]{3,2,1,0:T(8,128)} %get-tuple-element.7), channel_id=1, source_target_pairs={{0,508},{1,509},{2,510},{3,511},{4,0},{5,1},{6,2},{7,3},{8,4},{9,5... | collective-permute-start | bytes 1966088 | tf_op jit(solution)/shard_map/ppermute | solution.py:29
  15.1 0.6 fusion.23.xmask_ref
  15.7 11.8 %collective-permute-done = f32[10,4,32,128]{3,2,1,0:T(8,128)S(1)} collective-permute-done((f32[10,4,32,128]{3,2,1,0:T(8,128)}, f32[10,4,32,128]{3,2,1,0:T(8,128)S(1)}, u32[]{:S(2)}, u32[]{:S(2)}) %collective-permute-start) | collective-permute-done | bytes 655392 | tf_op jit(solution)/shard_map/ppermute | solution.py:29
  27.4 15.1 %collective-permute-done.1 = f32[10,4,32,128]{3,2,1,0:T(8,128)S(1)} collective-permute-done((f32[10,4,32,128]{3,2,1,0:T(8,128)}, f32[10,4,32,128]{3,2,1,0:T(8,128)S(1)}, u32[]{:S(2)}, u32[]{:S(2)}) %collective-permute-start.1) | collective-permute-done | bytes 655392 | tf_op jit(solution)/shard_map/ppermute | solution.py:29
  42.6 0.4 slice_add_fusion.1
  42.9 0.0 copy-start.1
  42.9 0.2 pad_maximum_fusion.c_ref
  43.1 0.0 copy-start
  43.1 0.5 copy-done.1
  43.6 1.0 %fusion.18 = f32[4,3840]{1,0:T(4,128)S(1)} fusion(f32[3840,128]{1,0:T(8,128)S(1)} %bitcast.16, s32[4]{0:T(128)S(1)} %copy-done.1), kind=kOutput, calls=%fused_computation.29 | convolution fusion | flops 23593472 | bytes 2027536 | tf_op jit(solution)/shard_map/jn,mn->jm/dot_general | solution.py:69
  44.6 1.9 %collective-permute-start.2 = (f32[2,3840]{1,0:T(2,128)S(1)}, f32[2,3840]{1,0:T(2,128)S(1)}, u32[]{:S(2)}, u32[]{:S(2)}) collective-permute-start(f32[2,3840]{1,0:T(2,128)S(1)} %get-tuple-element.8), channel_id=1, source_target_pairs={{1,0},{2,1},{3,2},{5,4},{6,5},{7,6},{9,8},{10,9},{11,10},{13,12},{... | collective-permute-start | bytes 92168 | tf_op jit(solution)/shard_map/ppermute | solution.py:29
  46.5 2.4 %collective-permute-start.3 = (f32[2,3840]{1,0:T(2,128)S(1)}, f32[2,3840]{1,0:T(2,128)S(1)}, u32[]{:S(2)}, u32[]{:S(2)}) collective-permute-start(f32[2,3840]{1,0:T(2,128)S(1)} %get-tuple-element.9), channel_id=1, source_target_pairs={{0,1},{1,2},{2,3},{4,5},{5,6},{6,7},{8,9},{9,10},{10,11},{12,13},{... | collective-permute-start | bytes 92168 | tf_op jit(solution)/shard_map/ppermute | solution.py:29
  49.0 0.6 multiply_divide_fusion
  49.5 0.0 collective-permute-done.2
  49.5 10.9 %collective-permute-done.3 = f32[2,3840]{1,0:T(2,128)S(1)} collective-permute-done((f32[2,3840]{1,0:T(2,128)S(1)}, f32[2,3840]{1,0:T(2,128)S(1)}, u32[]{:S(2)}, u32[]{:S(2)}) %collective-permute-start.3) | collective-permute-done | bytes 30752 | tf_op jit(solution)/shard_map/ppermute | solution.py:29
  60.5 3.0 %fusion.9 = f32[3840,128]{1,0:T(8,128)} fusion(f32[2,3840]{1,0:T(2,128)S(1)} %collective-permute-done.3, f32[2,3840]{1,0:T(2,128)S(1)} %collective-permute-done.2, s32[4]{0:T(128)S(1)} %copy-done.1), kind=kOutput, calls=%fused_computation.10 | convolution fusion | flops 23608832 | bytes 2027536 | tf_op jit(solution)/shard_map/jm,jn->mn/dot_general | solution.py:74
  63.5 0.0 copy-done
  63.5 7.8 %shard_map.85 = (f32[10,8,32,128]{3,2,1,0:T(8,128)}, f32[3,8,32,128]{3,2,1,0:T(8,128)}, f32[6,8,32,128]{3,2,1,0:T(8,128)}) custom-call(f32[10,12,32,128]{3,2,1,0:T(8,128)} %copy-done, f32[10,12,32,128]{3,2,1,0:T(8,128)} %bitcast.19, f32[1,128]{1,0:T(1,128)} %get-tuple-element.10.scale_ref, f32[1,128]{1,0:T(1,128)} %get-tuple-element.11.recip_ref, ...), custom_call_target="tpu_custom_call" | custom-call | tf_op jit(solution)/shard_map/pallas_call | solution.py:213
  (3 shorter events, 0.1 us)
Async XLA Ops:
  6.8 20.6 %collective-permute-start = (f32[10,4,32,128]{3,2,1,0:T(8,128)}, f32[10,4,32,128]{3,2,1,0:T(8,128)S(1)}, u32[]{:S(2)}, u32[]{:S(2)}) collective-permute-start(f32[10,4,32,128]{3,2,1,0:T(8,128)} %get-tuple-element.6), channel_id=1, source_target_pairs={{0,4},{1,5},{2,6},{3,7},{4,8},{5,9},{6,10},{7,11},{8,12},{9,13},{1... | collective-permute-start | bytes 1966088 | tf_op jit(solution)/shard_map/ppermute | solution.py:29
  13.1 29.4 %collective-permute-start.1 = (f32[10,4,32,128]{3,2,1,0:T(8,128)}, f32[10,4,32,128]{3,2,1,0:T(8,128)S(1)}, u32[]{:S(2)}, u32[]{:S(2)}) collective-permute-start(f32[10,4,32,128]{3,2,1,0:T(8,128)} %get-tuple-element.7), channel_id=1, source_target_pairs={{0,508},{1,509},{2,510},{3,511},{4,0},{5,1},{6,2},{7,3},{8,4},{9,5... | collective-permute-start | bytes 1966088 | tf_op jit(solution)/shard_map/ppermute | solution.py:29
  42.9 0.7 copy-start.1
  43.1 20.4 %copy-start = (f32[10,12,32,128]{3,2,1,0:T(8,128)}, f32[10,12,32,128]{3,2,1,0:T(8,128)S(1)}, u32[]{:S(2)}) copy-start(f32[10,12,32,128]{3,2,1,0:T(8,128)S(1)} %pad_maximum_fusion.c_ref) | copy-start | bytes 5898244
  44.6 4.9 %collective-permute-start.2 = (f32[2,3840]{1,0:T(2,128)S(1)}, f32[2,3840]{1,0:T(2,128)S(1)}, u32[]{:S(2)}, u32[]{:S(2)}) collective-permute-start(f32[2,3840]{1,0:T(2,128)S(1)} %get-tuple-element.8), channel_id=1, source_target_pairs={{1,0},{2,1},{3,2},{5,4},{6,5},{7,6},{9,8},{10,9},{11,10},{13,12},{... | collective-permute-start | bytes 92168 | tf_op jit(solution)/shard_map/ppermute | solution.py:29
  46.5 13.9 %collective-permute-start.3 = (f32[2,3840]{1,0:T(2,128)S(1)}, f32[2,3840]{1,0:T(2,128)S(1)}, u32[]{:S(2)}, u32[]{:S(2)}) collective-permute-start(f32[2,3840]{1,0:T(2,128)S(1)} %get-tuple-element.9), channel_id=1, source_target_pairs={{0,1},{1,2},{2,3},{4,5},{5,6},{6,7},{8,9},{9,10},{10,11},{12,13},{... | collective-permute-start | bytes 92168 | tf_op jit(solution)/shard_map/ppermute | solution.py:29

commit v10 on v8

--- a/solution.py
+++ b/solution.py
@@ -59,6 +59,15 @@
     )
 
 
+def placed(values, sel):
+    hi = lax.reduce_precision(values, exponent_bits=8, mantissa_bits=7)
+    rest = values - hi
+    mid = lax.reduce_precision(rest, exponent_bits=8, mantissa_bits=7)
+    parts = jnp.concatenate([hi, mid, rest - mid], axis=0).astype(jnp.bfloat16)
+    sel3 = jnp.concatenate([sel] * 3, axis=0).astype(jnp.bfloat16)
+    return jnp.einsum("jm,jn->mn", parts, sel3, preferred_element_type=jnp.float32)
+
+
 def window(raw):
     k = 2 * HALO
     center = add_rows(raw, shifted(raw[:, -k:], 1, 0), shifted(raw[:, :k], -1, 0))
@@ -71,12 +80,7 @@
     )
     right = shifted(picked[:HALO], 0, -1)
     left = shifted(picked[HALO:], 0, 1)
-    edges = jnp.einsum(
-        "jm,jn->mn",
-        jnp.concatenate([right, left], axis=0),
-        selector(cells, edge_cells),
-        precision=lax.Precision.HIGHEST,
-    )
+    edges = placed(jnp.concatenate([right, left], axis=0), selector(cells, edge_cells))
     return center, edges.reshape(shape)
 
 

time: 71.3 us -> 69.7 us (0.978)
  matrix products: 7.56 us -> 6.31 us
    dot_general x1, matrix products: 2.99 us -> 1.74 us  [placed(): jnp.einsum('jm,jn->mn', parts, sel3, preferred_element_type=jnp.float32)]
where the time goes in v10:
time: 69.7 us; the launch traced here: 69.4 us
  waiting for transfers between devices  37.7 us (54%)
  starting transfers between devices  12.6 us (18%)
  Pallas kernels  7.61 us (11%)
  matrix products  6.31 us (9%)
  other arithmetic  2.55 us (4%)
  between operations  1.39 us (2%)
  local copies, waits for them, and re-layouts  1.24 us (2%)
    ppermute x4, waiting for transfers between devices, shifted(): return lax.ppermute(value, ('az', 'rad'), pairs)  37.7 us
    ppermute x4, starting transfers between devices, shifted(): return lax.ppermute(value, ('az', 'rad'), pairs)  12.6 us
    pallas_call x1, Pallas kernels, stencil(): pl.pallas_call(stencil_kernel, out_shape=(shape(channels), shape(3), shap...  7.61 us
    dot_general x1, matrix products, deposit(): jnp.einsum('ls,scn->lcn', onehot, values, precision=lax.Precision.HIGHEST)  3.59 us
    dot_general x1, matrix products, placed(): jnp.einsum('jm,jn->mn', parts, sel3, preferred_element_type=jnp.float32)  1.74 us
  transfers between devices with their start and end apart: 4, of which 3 were waited for; matrix products, arithmetic and copies ran while one was open for 2% of the time, Pallas kernels for 0%

profile of v10, /device:TPU:510, one launch (start us, length us, event | category | flops | bytes accessed | tf_op | source)
XLA Modules:
  0.0 69.4 jit_solution(14447891079493041322)
XLA Ops:
  1.3 0.7 %fusion.20 = s32[512]{0:T(512)S(1)} fusion(s32[512]{0:T(512)} %bitcast.22, s32[]{:T(128)S(6)} %mul.28), kind=kLoop, calls=%fused_computation.36 | loop fusion | flops 17408 | bytes 4100 | tf_op jit(solution)/shard_map/add | solution.py:41
  2.0 3.6 %fusion = f32[384,10,128]{2,0,1:T(8,128)S(1)} fusion(f32[512,9,128]{2,0,1:T(8,128)} %bitcast.20, f32[512,1,128]{2,0,1:T(8,128)} %bitcast.21, s32[512]{0:T(512)S(1)} %fusion.20, pred[512]{0:T(512)(128)(4,1)S(1)} %iota_compare_fusion.2), kind=kOutput, calls=%fused_computation | convolution fusion | flops 3020947456 | bytes 4590080 | tf_op jit(solution)/shard_map/ls,scn->lcn/dot_general | solution.py:35
  5.6 0.0 copy-start.1
  5.6 1.2 %fusion.29 = (f32[10,4,32,128]{3,2,1,0:T(8,128)}, f32[10,4,32,128]{3,2,1,0:T(8,128)}) fusion(f32[10,12,32,128]{3,2,1,0:T(8,128)S(1)} %bitcast.17), kind=kLoop, calls=%fused_computation.54 | loop fusion | bytes 2621440 | tf_op jit(solution)/shard_map/slice | solution.py:73
  6.8 6.4 %collective-permute-start = (f32[10,4,32,128]{3,2,1,0:T(8,128)}, f32[10,4,32,128]{3,2,1,0:T(8,128)S(1)}, u32[]{:S(2)}, u32[]{:S(2)}) collective-permute-start(f32[10,4,32,128]{3,2,1,0:T(8,128)} %get-tuple-element.6), channel_id=1, source_target_pairs={{0,4},{1,5},{2,6},{3,7},{4,8},{5,9},{6,10},{7,11},{8,12},{9,13},{1... | collective-permute-start | bytes 1966088 | tf_op jit(solution)/shard_map/ppermute | solution.py:29
  13.2 1.9 %collective-permute-start.1 = (f32[10,4,32,128]{3,2,1,0:T(8,128)}, f32[10,4,32,128]{3,2,1,0:T(8,128)S(1)}, u32[]{:S(2)}, u32[]{:S(2)}) collective-permute-start(f32[10,4,32,128]{3,2,1,0:T(8,128)} %get-tuple-element.7), channel_id=1, source_target_pairs={{0,508},{1,509},{2,510},{3,511},{4,0},{5,1},{6,2},{7,3},{8,4},{9,5... | collective-permute-start | bytes 1966088 | tf_op jit(solution)/shard_map/ppermute | solution.py:29
  15.1 0.0 copy-done.1
  15.1 0.1 iota_compare_fusion.1
  15.2 0.6 fusion.23.xmask_ref
  15.8 11.7 %collective-permute-done = f32[10,4,32,128]{3,2,1,0:T(8,128)S(1)} collective-permute-done((f32[10,4,32,128]{3,2,1,0:T(8,128)}, f32[10,4,32,128]{3,2,1,0:T(8,128)S(1)}, u32[]{:S(2)}, u32[]{:S(2)}) %collective-permute-start) | collective-permute-done | bytes 655392 | tf_op jit(solution)/shard_map/ppermute | solution.py:29
  27.4 15.1 %collective-permute-done.1 = f32[10,4,32,128]{3,2,1,0:T(8,128)S(1)} collective-permute-done((f32[10,4,32,128]{3,2,1,0:T(8,128)}, f32[10,4,32,128]{3,2,1,0:T(8,128)S(1)}, u32[]{:S(2)}, u32[]{:S(2)}) %collective-permute-start.1) | collective-permute-done | bytes 655392 | tf_op jit(solution)/shard_map/ppermute | solution.py:29
  42.6 0.4 slice_add_fusion.1
  42.9 0.2 pad_maximum_fusion.c_ref
  43.1 0.0 copy-start
  43.1 1.0 %fusion.28 = f32[4,3840]{1,0:T(4,128)S(1)} fusion(f32[3840,128]{1,0:T(8,128)S(1)} %bitcast.16, s32[4]{0:T(128)S(1)} %copy-done.1), kind=kOutput, calls=%fused_computation.51 | convolution fusion | flops 23593472 | bytes 2027536 | tf_op jit(solution)/shard_map/jn,mn->jm/dot_general | solution.py:78
  44.1 1.9 %collective-permute-start.2 = (f32[2,3840]{1,0:T(2,128)S(1)}, f32[2,3840]{1,0:T(2,128)S(1)}, u32[]{:S(2)}, u32[]{:S(2)}) collective-permute-start(f32[2,3840]{1,0:T(2,128)S(1)} %get-tuple-element.11), channel_id=1, source_target_pairs={{1,0},{2,1},{3,2},{5,4},{6,5},{7,6},{9,8},{10,9},{11,10},{13,12},{... | collective-permute-start | bytes 92168 | tf_op jit(solution)/shard_map/ppermute | solution.py:29
  46.1 2.4 %collective-permute-start.3 = (f32[2,3840]{1,0:T(2,128)S(1)}, f32[2,3840]{1,0:T(2,128)S(1)}, u32[]{:S(2)}, u32[]{:S(2)}) collective-permute-start(f32[2,3840]{1,0:T(2,128)S(1)} %get-tuple-element.12), channel_id=1, source_target_pairs={{0,1},{1,2},{2,3},{4,5},{5,6},{6,7},{8,9},{9,10},{10,11},{12,13},{... | collective-permute-start | bytes 92168 | tf_op jit(solution)/shard_map/ppermute | solution.py:29
  48.5 0.6 multiply_divide_fusion
  49.1 0.0 collective-permute-done.2
  49.1 10.9 %collective-permute-done.3 = f32[2,3840]{1,0:T(2,128)S(1)} collective-permute-done((f32[2,3840]{1,0:T(2,128)S(1)}, f32[2,3840]{1,0:T(2,128)S(1)}, u32[]{:S(2)}, u32[]{:S(2)}) %collective-permute-start.3) | collective-permute-done | bytes 30752 | tf_op jit(solution)/shard_map/ppermute | solution.py:29
  60.0 0.1 reduce-precision_convert_fusion.1
  60.1 1.7 %fusion.9 = f32[3840,128]{1,0:T(8,128)} fusion(bf16[4,3840]{1,0:T(4,128)(2,1)S(1)} %get-tuple-element.10, bf16[4,3840]{1,0:T(4,128)(2,1)S(1)} %get-tuple-element.9, bf16[4,3840]{1,0:T(4,128)(2,1)S(1)} %get-tuple-element.8, pred[4,128]{1,0:T(4,128)(4,1)S(1)} %iota_compare_fusion.1), kind=kOutput, calls=%fused_computation.10 | convolution fusion | flops 12079104 | bytes 2058752 | tf_op jit(solution)/shard_map/jm,jn->mn/dot_general | solution.py:68
  61.8 0.0 copy-done
  61.8 7.6 %shard_map.85 = (f32[10,8,32,128]{3,2,1,0:T(8,128)}, f32[3,8,32,128]{3,2,1,0:T(8,128)}, f32[6,8,32,128]{3,2,1,0:T(8,128)}) custom-call(f32[10,12,32,128]{3,2,1,0:T(8,128)} %copy-done, f32[10,12,32,128]{3,2,1,0:T(8,128)} %bitcast.19, f32[1,128]{1,0:T(1,128)} %get-tuple-element.13.scale_ref, f32[1,128]{1,0:T(1,128)} %get-tuple-element.14.recip_ref, ...), custom_call_target="tpu_custom_call" | custom-call | tf_op jit(solution)/shard_map/pallas_call | solution.py:207
  (3 shorter events, 0.1 us)
Async XLA Ops:
  5.6 9.5 %copy-start.1 = (s32[4]{0:T(128)S(1)}, s32[4]{0:T(128)}, u32[]{:S(2)}) copy-start(s32[4]{0:T(128)} %constant.74.clone) | copy-start | bytes 52
  6.8 20.6 %collective-permute-start = (f32[10,4,32,128]{3,2,1,0:T(8,128)}, f32[10,4,32,128]{3,2,1,0:T(8,128)S(1)}, u32[]{:S(2)}, u32[]{:S(2)}) collective-permute-start(f32[10,4,32,128]{3,2,1,0:T(8,128)} %get-tuple-element.6), channel_id=1, source_target_pairs={{0,4},{1,5},{2,6},{3,7},{4,8},{5,9},{6,10},{7,11},{8,12},{9,13},{1... | collective-permute-start | bytes 1966088 | tf_op jit(solution)/shard_map/ppermute | solution.py:29
  13.2 29.4 %collective-permute-start.1 = (f32[10,4,32,128]{3,2,1,0:T(8,128)}, f32[10,4,32,128]{3,2,1,0:T(8,128)S(1)}, u32[]{:S(2)}, u32[]{:S(2)}) collective-permute-start(f32[10,4,32,128]{3,2,1,0:T(8,128)} %get-tuple-element.7), channel_id=1, source_target_pairs={{0,508},{1,509},{2,510},{3,511},{4,0},{5,1},{6,2},{7,3},{8,4},{9,5... | collective-permute-start | bytes 1966088 | tf_op jit(solution)/shard_map/ppermute | solution.py:29
  43.1 18.7 %copy-start = (f32[10,12,32,128]{3,2,1,0:T(8,128)}, f32[10,12,32,128]{3,2,1,0:T(8,128)S(1)}, u32[]{:S(2)}) copy-start(f32[10,12,32,128]{3,2,1,0:T(8,128)S(1)} %pad_maximum_fusion.c_ref) | copy-start | bytes 5898244
  44.1 4.9 %collective-permute-start.2 = (f32[2,3840]{1,0:T(2,128)S(1)}, f32[2,3840]{1,0:T(2,128)S(1)}, u32[]{:S(2)}, u32[]{:S(2)}) collective-permute-start(f32[2,3840]{1,0:T(2,128)S(1)} %get-tuple-element.11), channel_id=1, source_target_pairs={{1,0},{2,1},{3,2},{5,4},{6,5},{7,6},{9,8},{10,9},{11,10},{13,12},{... | collective-permute-start | bytes 92168 | tf_op jit(solution)/shard_map/ppermute | solution.py:29
  46.1 13.9 %collective-permute-start.3 = (f32[2,3840]{1,0:T(2,128)S(1)}, f32[2,3840]{1,0:T(2,128)S(1)}, u32[]{:S(2)}, u32[]{:S(2)}) collective-permute-start(f32[2,3840]{1,0:T(2,128)S(1)} %get-tuple-element.12), channel_id=1, source_target_pairs={{0,1},{1,2},{2,3},{4,5},{5,6},{6,7},{8,9},{9,10},{10,11},{12,13},{... | collective-permute-start | bytes 92168 | tf_op jit(solution)/shard_map/ppermute | solution.py:29

commit v11 on v10

--- a/solution.py
+++ b/solution.py
@@ -32,7 +32,12 @@
 
 
 def deposit(onehot, values):
-    out = jnp.einsum("ls,scn->lcn", onehot, values, precision=lax.Precision.HIGHEST)
+    hi = lax.reduce_precision(values, exponent_bits=8, mantissa_bits=7)
+    rest = values - hi
+    mid = lax.reduce_precision(rest, exponent_bits=8, mantissa_bits=7)
+    parts = jnp.concatenate([hi, mid, rest - mid], axis=0).astype(jnp.bfloat16)
+    lines = jnp.concatenate([onehot] * 3, axis=1).astype(jnp.bfloat16)
+    out = jnp.einsum("ls,scn->lcn", lines, parts, preferred_element_type=jnp.float32)
     return jnp.transpose(out, (1, 0, 2))
 
 

time: 69.7 us -> 70.6 us (1.013)
  other arithmetic: 2.55 us -> 5.29 us
  matrix products: 6.31 us -> 4.41 us
    another operation x1 -> x2, other arithmetic: 0.06 us -> 2.7 us
    dot_general x1, matrix products: 3.59 us -> 1.69 us  [deposit(): jnp.einsum('ls,scn->lcn', lines, parts, preferred_element_type=jnp.float32)]
where the time goes in v11:
time: 70.6 us; the launch traced here: 70.3 us
  waiting for transfers between devices  37.8 us (54%)
  starting transfers between devices  12.6 us (18%)
  Pallas kernels  7.61 us (11%)
  other arithmetic  5.29 us (7%)
  matrix products  4.41 us (6%)
  between operations  1.4 us (2%)
  local copies, waits for them, and re-layouts  1.24 us (2%)
    ppermute x4, waiting for transfers between devices, shifted(): return lax.ppermute(value, ('az', 'rad'), pairs)  37.8 us
    ppermute x4, starting transfers between devices, shifted(): return lax.ppermute(value, ('az', 'rad'), pairs)  12.6 us
    pallas_call x1, Pallas kernels, stencil(): pl.pallas_call(stencil_kernel, out_shape=(shape(channels), shape(3), shap...  7.61 us
    another operation x2, other arithmetic  2.7 us
    dot_general x1, matrix products, placed(): jnp.einsum('jm,jn->mn', parts, sel3, preferred_element_type=jnp.float32)  1.73 us
    dot_general x1, matrix products, deposit(): jnp.einsum('ls,scn->lcn', lines, parts, preferred_element_type=jnp.float32)  1.69 us
  transfers between devices with their start and end apart: 4, of which 3 were waited for; matrix products, arithmetic and copies ran while one was open for 2% of the time, Pallas kernels for 0%

profile of v11, /device:TPU:510, one launch (start us, length us, event | category | flops | bytes accessed | tf_op | source)
XLA Modules:
  0.0 70.3 jit_solution(8092681094727648303)
XLA Ops:
  1.3 0.7 %fusion.21 = s32[512]{0:T(512)S(1)} fusion(s32[512]{0:T(512)} %bitcast.22, s32[]{:T(128)S(6)} %mul.28), kind=kLoop, calls=%fused_computation.43 | loop fusion | flops 17408 | bytes 4100 | tf_op jit(solution)/shard_map/add | solution.py:46
  2.0 0.1 fusion.9
  2.1 2.6 %reduce-precision_convert_fusion.1 = (bf16[512,10,128]{2,0,1:T(8,128)(2,1)S(1)}, bf16[512,10,128]{2,0,1:T(8,128)(2,1)S(1)}, bf16[512,10,128]{2,0,1:T(8,128)(2,1)S(1)}) fusion(f32[512,9,128]{2,0,1:T(8,128)} %bitcast.20, f32[512,1,128]{2,0,1:T(8,128)} %bitcast.21), kind=kLoop, calls=%fused_computation.9 | loop fusion | flops 5242880 | bytes 6553600 | tf_op jit(solution)/shard_map/convert.7
  4.8 1.7 %fusion = f32[384,10,128]{2,0,1:T(8,128)S(1)} fusion(bf16[512,10,128]{2,0,1:T(8,128)(2,1)S(1)} %get-tuple-element.5, bf16[512,10,128]{2,0,1:T(8,128)(2,1)S(1)} %get-tuple-element.4, bf16[512,10,128]{2,0,1:T(8,128)(2,1)S(1)} %get-tuple-element.3, pred[384,512]{1,0:T(32,128)(4,1)S(1)} %fusion.9), kind=kOutput, calls=%fused_computation | convolution fusion | flops 1524105216 | bytes 6094848 | tf_op jit(solution)/shard_map/ls,scn->lcn/dot_general | solution.py:40
  6.5 0.0 copy-start.1
  6.5 1.2 %fusion.31 = (f32[10,4,32,128]{3,2,1,0:T(8,128)}, f32[10,4,32,128]{3,2,1,0:T(8,128)}) fusion(f32[10,12,32,128]{3,2,1,0:T(8,128)S(1)} %bitcast.18), kind=kLoop, calls=%fused_computation.62 | loop fusion | bytes 2621440 | tf_op jit(solution)/shard_map/slice | solution.py:78
  7.7 6.4 %collective-permute-start = (f32[10,4,32,128]{3,2,1,0:T(8,128)}, f32[10,4,32,128]{3,2,1,0:T(8,128)S(1)}, u32[]{:S(2)}, u32[]{:S(2)}) collective-permute-start(f32[10,4,32,128]{3,2,1,0:T(8,128)} %get-tuple-element.9), channel_id=1, source_target_pairs={{0,4},{1,5},{2,6},{3,7},{4,8},{5,9},{6,10},{7,11},{8,12},{9,13},{1... | collective-permute-start | bytes 1966088 | tf_op jit(solution)/shard_map/ppermute | solution.py:29
  14.1 1.9 %collective-permute-start.1 = (f32[10,4,32,128]{3,2,1,0:T(8,128)}, f32[10,4,32,128]{3,2,1,0:T(8,128)S(1)}, u32[]{:S(2)}, u32[]{:S(2)}) collective-permute-start(f32[10,4,32,128]{3,2,1,0:T(8,128)} %get-tuple-element.10), channel_id=1, source_target_pairs={{0,508},{1,509},{2,510},{3,511},{4,0},{5,1},{6,2},{7,3},{8,4},{9,5... | collective-permute-start | bytes 1966088 | tf_op jit(solution)/shard_map/ppermute | solution.py:29
  16.0 0.0 copy-done.1
  16.0 0.1 iota_compare_fusion.1
  16.1 0.5 fusion.24.xmask_ref
  16.6 11.7 %collective-permute-done = f32[10,4,32,128]{3,2,1,0:T(8,128)S(1)} collective-permute-done((f32[10,4,32,128]{3,2,1,0:T(8,128)}, f32[10,4,32,128]{3,2,1,0:T(8,128)S(1)}, u32[]{:S(2)}, u32[]{:S(2)}) %collective-permute-start) | collective-permute-done | bytes 655392 | tf_op jit(solution)/shard_map/ppermute | solution.py:29
  28.3 15.1 %collective-permute-done.1 = f32[10,4,32,128]{3,2,1,0:T(8,128)S(1)} collective-permute-done((f32[10,4,32,128]{3,2,1,0:T(8,128)}, f32[10,4,32,128]{3,2,1,0:T(8,128)S(1)}, u32[]{:S(2)}, u32[]{:S(2)}) %collective-permute-start.1) | collective-permute-done | bytes 655392 | tf_op jit(solution)/shard_map/ppermute | solution.py:29
  43.5 0.4 slice_add_fusion.1
  43.8 0.2 pad_maximum_fusion.1.c_ref
  44.0 0.0 copy-start
  44.0 1.0 %fusion.30 = f32[4,3840]{1,0:T(4,128)S(1)} fusion(f32[3840,128]{1,0:T(8,128)S(1)} %bitcast.16, s32[4]{0:T(128)S(1)} %copy-done.1), kind=kOutput, calls=%fused_computation.59 | convolution fusion | flops 23593472 | bytes 2027536 | tf_op jit(solution)/shard_map/jn,mn->jm/dot_general | solution.py:83
  45.0 1.9 %collective-permute-start.2 = (f32[2,3840]{1,0:T(2,128)S(1)}, f32[2,3840]{1,0:T(2,128)S(1)}, u32[]{:S(2)}, u32[]{:S(2)}) collective-permute-start(f32[2,3840]{1,0:T(2,128)S(1)} %get-tuple-element.14), channel_id=1, source_target_pairs={{1,0},{2,1},{3,2},{5,4},{6,5},{7,6},{9,8},{10,9},{11,10},{13,12},{... | collective-permute-start | bytes 92168 | tf_op jit(solution)/shard_map/ppermute | solution.py:29
  47.0 2.4 %collective-permute-start.3 = (f32[2,3840]{1,0:T(2,128)S(1)}, f32[2,3840]{1,0:T(2,128)S(1)}, u32[]{:S(2)}, u32[]{:S(2)}) collective-permute-start(f32[2,3840]{1,0:T(2,128)S(1)} %get-tuple-element.15), channel_id=1, source_target_pairs={{0,1},{1,2},{2,3},{4,5},{5,6},{6,7},{8,9},{9,10},{10,11},{12,13},{... | collective-permute-start | bytes 92168 | tf_op jit(solution)/shard_map/ppermute | solution.py:29
  49.4 0.6 multiply_divide_fusion
  50.0 0.0 collective-permute-done.2
  50.0 10.9 %collective-permute-done.3 = f32[2,3840]{1,0:T(2,128)S(1)} collective-permute-done((f32[2,3840]{1,0:T(2,128)S(1)}, f32[2,3840]{1,0:T(2,128)S(1)}, u32[]{:S(2)}, u32[]{:S(2)}) %collective-permute-start.3) | collective-permute-done | bytes 30752 | tf_op jit(solution)/shard_map/ppermute | solution.py:29
  60.9 0.1 reduce-precision_convert_fusion.3
  61.0 1.7 %fusion.10 = f32[3840,128]{1,0:T(8,128)} fusion(bf16[4,3840]{1,0:T(4,128)(2,1)S(1)} %get-tuple-element.13, bf16[4,3840]{1,0:T(4,128)(2,1)S(1)} %get-tuple-element.12, bf16[4,3840]{1,0:T(4,128)(2,1)S(1)} %get-tuple-element.11, pred[4,128]{1,0:T(4,128)(4,1)S(1)} %iota_compare_fusion.1), kind=kOutput, calls=%fused_computation.17 | convolution fusion | flops 12079104 | bytes 2058752 | tf_op jit(solution)/shard_map/jm,jn->mn/dot_general | solution.py:73
  62.7 0.0 copy-done
  62.7 7.6 %shard_map.85 = (f32[10,8,32,128]{3,2,1,0:T(8,128)}, f32[3,8,32,128]{3,2,1,0:T(8,128)}, f32[6,8,32,128]{3,2,1,0:T(8,128)}) custom-call(f32[10,12,32,128]{3,2,1,0:T(8,128)} %copy-done, f32[10,12,32,128]{3,2,1,0:T(8,128)} %bitcast.17, f32[1,128]{1,0:T(1,128)} %get-tuple-element.16.scale_ref, f32[1,128]{1,0:T(1,128)} %get-tuple-element.17.recip_ref, ...), custom_call_target="tpu_custom_call" | custom-call | tf_op jit(solution)/shard_map/pallas_call | solution.py:212
  (3 shorter events, 0.1 us)
Async XLA Ops:
  6.5 9.5 %copy-start.1 = (s32[4]{0:T(128)S(1)}, s32[4]{0:T(128)}, u32[]{:S(2)}) copy-start(s32[4]{0:T(128)} %constant.74.clone) | copy-start | bytes 52
  7.7 20.6 %collective-permute-start = (f32[10,4,32,128]{3,2,1,0:T(8,128)}, f32[10,4,32,128]{3,2,1,0:T(8,128)S(1)}, u32[]{:S(2)}, u32[]{:S(2)}) collective-permute-start(f32[10,4,32,128]{3,2,1,0:T(8,128)} %get-tuple-element.9), channel_id=1, source_target_pairs={{0,4},{1,5},{2,6},{3,7},{4,8},{5,9},{6,10},{7,11},{8,12},{9,13},{1... | collective-permute-start | bytes 1966088 | tf_op jit(solution)/shard_map/ppermute | solution.py:29
  14.1 29.4 %collective-permute-start.1 = (f32[10,4,32,128]{3,2,1,0:T(8,128)}, f32[10,4,32,128]{3,2,1,0:T(8,128)S(1)}, u32[]{:S(2)}, u32[]{:S(2)}) collective-permute-start(f32[10,4,32,128]{3,2,1,0:T(8,128)} %get-tuple-element.10), channel_id=1, source_target_pairs={{0,508},{1,509},{2,510},{3,511},{4,0},{5,1},{6,2},{7,3},{8,4},{9,5... | collective-permute-start | bytes 1966088 | tf_op jit(solution)/shard_map/ppermute | solution.py:29
  44.0 18.7 %copy-start = (f32[10,12,32,128]{3,2,1,0:T(8,128)}, f32[10,12,32,128]{3,2,1,0:T(8,128)S(1)}, u32[]{:S(2)}) copy-start(f32[10,12,32,128]{3,2,1,0:T(8,128)S(1)} %pad_maximum_fusion.1.c_ref) | copy-start | bytes 5898244
  45.0 4.9 %collective-permute-start.2 = (f32[2,3840]{1,0:T(2,128)S(1)}, f32[2,3840]{1,0:T(2,128)S(1)}, u32[]{:S(2)}, u32[]{:S(2)}) collective-permute-start(f32[2,3840]{1,0:T(2,128)S(1)} %get-tuple-element.14), channel_id=1, source_target_pairs={{1,0},{2,1},{3,2},{5,4},{6,5},{7,6},{9,8},{10,9},{11,10},{13,12},{... | collective-permute-start | bytes 92168 | tf_op jit(solution)/shard_map/ppermute | solution.py:29
  47.0 13.9 %collective-permute-start.3 = (f32[2,3840]{1,0:T(2,128)S(1)}, f32[2,3840]{1,0:T(2,128)S(1)}, u32[]{:S(2)}, u32[]{:S(2)}) collective-permute-start(f32[2,3840]{1,0:T(2,128)S(1)} %get-tuple-element.15), channel_id=1, source_target_pairs={{0,1},{1,2},{2,3},{4,5},{5,6},{6,7},{8,9},{9,10},{10,11},{12,13},{... | collective-permute-start | bytes 92168 | tf_op jit(solution)/shard_map/ppermute | solution.py:29

commit v12 on v10

--- a/solution.py
+++ b/solution.py
@@ -36,13 +36,11 @@
     return jnp.transpose(out, (1, 0, 2))
 
 
-def local_rows(values, dest, live, start, total_rows, width):
+def local_rows(values, dest, live, start, total_rows, width, lines):
     local_row = jnp.mod(dest // H - start + HALO, total_rows)
     line = local_row * H + dest % H
-    onehot = (
-        (jnp.arange((CA + 2 * HALO) * H, dtype=jnp.int32)[:, None] == line[None, :]) & live[None, :]
-    ).astype(jnp.float32)
-    return deposit(onehot, values).reshape(10, CA + 2 * HALO, H, width)
+    onehot = ((lines[:, None] == line[None, :]) & live[None, :]).astype(jnp.float32)
+    return deposit(onehot, values).reshape(10, -1, H, width)
 
 
 def add_rows(base, head, tail):
@@ -68,9 +66,8 @@
     return jnp.einsum("jm,jn->mn", parts, sel3, preferred_element_type=jnp.float32)
 
 
-def window(raw):
-    k = 2 * HALO
-    center = add_rows(raw, shifted(raw[:, -k:], 1, 0), shifted(raw[:, :k], -1, 0))
+def window(raw, top, bottom):
+    center = add_rows(raw, shifted(bottom, 1, 0), shifted(top, -1, 0))
     shape = center.shape
     cells = shape[3]
     flat = center.reshape(-1, cells)
@@ -226,8 +223,10 @@
     dest = block_dest[0, 0]
     slot_index = jnp.arange(slots, dtype=jnp.int32)
     live = slot_index < block_count[0, 0]
-    raw = local_rows(values, dest, live, start, total_rows, width)
-    center, edges = window(raw)
+    lines = jnp.arange((CA + 2 * HALO) * H, dtype=jnp.int32)
+    k = 2 * HALO * H
+    deposited = lambda part: local_rows(values, dest, live, start, total_rows, width, part)
+    center, edges = window(deposited(lines), deposited(lines[:k]), deposited(lines[-k:]))
     glob_cells = (band_index * width + jnp.arange(width, dtype=jnp.int32)).astype(jnp.float32)
     radius = width * n_rad + glob_cells + 0.5
     dtheta = 2.0 * math.pi / total_rows

time: 69.7 us -> 82.3 us (1.18)
  the two profiles are of different devices: /device:TPU:510 before, /device:TPU:1 now
where the time goes in v12:
time: 82.3 us; the launch traced here: 82 us
  starting transfers between devices  34.6 us (42%)
  waiting for transfers between devices  24.1 us (29%)
  matrix products  10.3 us (13%)
  Pallas kernels  7.61 us (9%)
  other arithmetic  3.64 us (4%)
  between operations  1.59 us (2%)
    ppermute x4, starting transfers between devices, shifted(): return lax.ppermute(value, ('az', 'rad'), pairs)  34.6 us
    ppermute x4, waiting for transfers between devices, shifted(): return lax.ppermute(value, ('az', 'rad'), pairs)  24.1 us
    pallas_call x1, Pallas kernels, stencil(): pl.pallas_call(stencil_kernel, out_shape=(shape(channels), shape(3), shap...  7.61 us
    dot_general x3, matrix products, deposit(): jnp.einsum('ls,scn->lcn', onehot, values, precision=lax.Precision.HIGHEST)  7.59 us
    dot_general x1, matrix products, placed(): jnp.einsum('jm,jn->mn', parts, sel3, preferred_element_type=jnp.float32)  1.73 us
  transfers between devices with their start and end apart: 4, of which 3 were waited for; matrix products, arithmetic and copies ran while one was open for 6% of the time, Pallas kernels for 0%

profile of v12, /device:TPU:1, one launch (start us, length us, event | category | flops | bytes accessed | tf_op | source)
XLA Modules:
  0.0 82.0 jit_solution(13011813295057688154)
XLA Ops:
  0.6 0.0 copy-start
  0.6 0.0 copy-start.2
  1.5 0.7 fusion.31
  2.2 3.6 %fusion = f32[128,10,128]{2,0,1:T(8,128)} fusion(f32[512,9,128]{2,0,1:T(8,128)} %bitcast.28, f32[512,1,128]{2,0,1:T(8,128)} %bitcast.34, s32[512]{0:T(512)S(1)} %fusion.31, s32[128]{0:T(128)S(1)} %slice.29, pred[512]{0:T(512)(128)(4,1)S(1)} %iota_compare_fusion.2), kind=kOutput, calls=%fused_computation.2 | convolution fusion | flops 1007419392 | bytes 3279872 | tf_op jit(solution)/shard_map/ls,scn->lcn/dot_general | solution.py:35
  5.8 0.0 copy-start.3
  5.8 18.5 %collective-permute-start.1 = (f32[10,4,32,128]{3,2,1,0:T(8,128)}, f32[10,4,32,128]{3,2,1,0:T(8,128)S(1)}, u32[]{:S(2)}, u32[]{:S(2)}) collective-permute-start(f32[10,4,32,128]{3,2,1,0:T(8,128)} %bitcast.13), channel_id=1, source_target_pairs={{0,508},{1,509},{2,510},{3,511},{4,0},{5,1},{6,2},{7,3},{8,4},{9,5... | collective-permute-start | bytes 1966088 | tf_op jit(solution)/shard_map/ppermute | solution.py:29
  24.3 0.0 copy-done
  24.3 0.0 copy-done.2
  24.3 2.0 %fusion.1 = f32[128,10,128]{2,0,1:T(8,128)} fusion(f32[512,9,128]{2,0,1:T(8,128)S(1)} %bitcast.29, f32[512,1,128]{2,0,1:T(8,128)S(1)} %bitcast.35, s32[512]{0:T(512)S(1)} %fusion.31, s32[128]{0:T(128)S(1)} %slice.26, pred[512]{0:T(512)(128)(4,1)S(1)} %iota_compare_fusion.2), kind=kOutput, calls=%fused_computation.3 | convolution fusion | flops 1007419392 | bytes 3279872 | tf_op jit(solution)/shard_map/ls,scn->lcn/dot_general | solution.py:35
  26.3 1.9 %collective-permute-start = (f32[10,4,32,128]{3,2,1,0:T(8,128)}, f32[10,4,32,128]{3,2,1,0:T(8,128)}, u32[]{:S(2)}, u32[]{:S(2)}) collective-permute-start(f32[10,4,32,128]{3,2,1,0:T(8,128)} %bitcast.9), channel_id=1, source_target_pairs={{0,4},{1,5},{2,6},{3,7},{4,8},{5,9},{6,10},{7,11},{8,12},{9,13},{1... | collective-permute-start | bytes 1966088 | tf_op jit(solution)/shard_map/ppermute | solution.py:29
  28.2 0.0 copy-done.3
  28.2 0.1 iota_compare_fusion.1
  28.3 0.6 fusion.34.xmask_ref
  28.9 2.0 %fusion.2 = f32[384,10,128]{2,0,1:T(8,128)S(1)} fusion(f32[512,9,128]{2,0,1:T(8,128)S(1)} %bitcast.30, f32[512,1,128]{2,0,1:T(8,128)S(1)} %bitcast.36, s32[512]{0:T(512)S(1)} %fusion.31, pred[512]{0:T(512)(128)(4,1)S(1)} %iota_compare_fusion.2), kind=kOutput, calls=%fused_computation.4 | convolution fusion | flops 3020947456 | bytes 4590080 | tf_op jit(solution)/shard_map/ls,scn->lcn/dot_general | solution.py:35
  30.9 7.1 %collective-permute-done.1 = f32[10,4,32,128]{3,2,1,0:T(8,128)S(1)} collective-permute-done((f32[10,4,32,128]{3,2,1,0:T(8,128)}, f32[10,4,32,128]{3,2,1,0:T(8,128)S(1)}, u32[]{:S(2)}, u32[]{:S(2)}) %collective-permute-start.1) | collective-permute-done | bytes 655392 | tf_op jit(solution)/shard_map/ppermute | solution.py:29
  38.0 16.7 %collective-permute-done = f32[10,4,32,128]{3,2,1,0:T(8,128)} collective-permute-done((f32[10,4,32,128]{3,2,1,0:T(8,128)}, f32[10,4,32,128]{3,2,1,0:T(8,128)}, u32[]{:S(2)}, u32[]{:S(2)}) %collective-permute-start) | collective-permute-done | bytes 655392 | tf_op jit(solution)/shard_map/ppermute | solution.py:29
  54.7 1.5 %slice_add_fusion.1 = (f32[10,4,32,128]{3,2,1,0:T(8,128)S(1)}, f32[10,4,32,128]{3,2,1,0:T(8,128)S(1)}, f32[10,4,32,128]{3,2,1,0:T(8,128)S(1)}) fusion(f32[10,4,32,128]{3,2,1,0:T(8,128)} %collective-permute-done, f32[10,12,32,128]{3,2,1,0:T(8,128)S(1)} %bitcast.33, f32[10,4,32,128]{3,2,1,0:T(8,128)S(1)} %collective-permute-done.1), kind=kLoop, calls=%fused_computation.9 | loop fusion | flops 327680 | bytes 5242880 | tf_op jit(solution)/shard_map/add | solution.py:50
  56.1 0.2 pad_maximum_fusion.1.c_ref
  56.3 0.0 copy-start.1
  56.3 1.0 %fusion.41 = f32[4,3840]{1,0:T(4,128)S(1)} fusion(f32[3840,128]{1,0:T(8,128)S(1)} %bitcast.31, s32[4]{0:T(128)S(1)} %copy-done.3), kind=kOutput, calls=%fused_computation.67 | convolution fusion | flops 23593472 | bytes 2027536 | tf_op jit(solution)/shard_map/jn,mn->jm/dot_general | solution.py:75
  57.3 3.7 %collective-permute-start.2 = (f32[2,3840]{1,0:T(2,128)S(1)}, f32[2,3840]{1,0:T(2,128)S(1)}, u32[]{:S(2)}, u32[]{:S(2)}) collective-permute-start(f32[2,3840]{1,0:T(2,128)S(1)} %get-tuple-element.9), channel_id=1, source_target_pairs={{1,0},{2,1},{3,2},{5,4},{6,5},{7,6},{9,8},{10,9},{11,10},{13,12},{... | collective-permute-start | bytes 92168 | tf_op jit(solution)/shard_map/ppermute | solution.py:29
  61.1 10.6 %collective-permute-start.3 = (f32[2,3840]{1,0:T(2,128)S(1)}, f32[2,3840]{1,0:T(2,128)S(1)}, u32[]{:S(2)}, u32[]{:S(2)}) collective-permute-start(f32[2,3840]{1,0:T(2,128)S(1)} %get-tuple-element.10), channel_id=1, source_target_pairs={{0,1},{1,2},{2,3},{4,5},{5,6},{6,7},{8,9},{9,10},{10,11},{12,13},{... | collective-permute-start | bytes 92168 | tf_op jit(solution)/shard_map/ppermute | solution.py:29
  71.6 0.6 multiply_divide_fusion
  72.2 0.0 collective-permute-done.2
  72.3 0.4 collective-permute-done.3
  72.6 0.1 reduce-precision_convert_fusion.1
  72.7 1.7 %fusion.20 = f32[3840,128]{1,0:T(8,128)} fusion(bf16[4,3840]{1,0:T(4,128)(2,1)S(1)} %get-tuple-element.8, bf16[4,3840]{1,0:T(4,128)(2,1)S(1)} %get-tuple-element.7, bf16[4,3840]{1,0:T(4,128)(2,1)S(1)} %get-tuple-element.6, pred[4,128]{1,0:T(4,128)(4,1)S(1)} %iota_compare_fusion.1), kind=kOutput, calls=%fused_computation.24 | convolution fusion | flops 12079104 | bytes 2058752 | tf_op jit(solution)/shard_map/jm,jn->mn/dot_general | solution.py:66
  74.4 0.0 copy-done.1
  74.4 7.6 %shard_map.85 = (f32[10,8,32,128]{3,2,1,0:T(8,128)}, f32[3,8,32,128]{3,2,1,0:T(8,128)}, f32[6,8,32,128]{3,2,1,0:T(8,128)}) custom-call(f32[10,12,32,128]{3,2,1,0:T(8,128)} %copy-done.1, f32[10,12,32,128]{3,2,1,0:T(8,128)} %bitcast.32, f32[1,128]{1,0:T(1,128)} %get-tuple-element.11.scale_ref, f32[1,128]{1,0:T(1,128)} %get-tuple-element.12.recip_ref, ...), custom_call_target="tpu_custom_call" | custom-call | tf_op jit(solution)/shard_map/pallas_call | solution.py:204
  (7 shorter events, 0.1 us)
Async XLA Ops:
  0.6 23.7 %copy-start = (f32[1,1,512,9,128]{4,2,3,1,0:T(8,128)S(1)}, f32[1,1,512,9,128]{4,2,3,1,0:T(8,128)}, u32[]{:S(2)}) copy-start(f32[1,1,512,9,128]{4,2,3,1,0:T(8,128)} %param.7) | copy-start | bytes 7077892
  0.6 23.7 %copy-start.2 = (f32[1,1,512,128]{3,2,1,0:T(8,128)S(1)}, f32[1,1,512,128]{3,2,1,0:T(8,128)}, u32[]{:S(2)}) copy-start(f32[1,1,512,128]{3,2,1,0:T(8,128)} %param.6) | copy-start | bytes 786436
  5.8 22.4 %copy-start.3 = (s32[4]{0:T(128)S(1)}, s32[4]{0:T(128)}, u32[]{:S(2)}) copy-start(s32[4]{0:T(128)} %constant.90.clone) | copy-start | bytes 52
  5.8 32.2 %collective-permute-start.1 = (f32[10,4,32,128]{3,2,1,0:T(8,128)}, f32[10,4,32,128]{3,2,1,0:T(8,128)S(1)}, u32[]{:S(2)}, u32[]{:S(2)}) collective-permute-start(f32[10,4,32,128]{3,2,1,0:T(8,128)} %bitcast.13), channel_id=1, source_target_pairs={{0,508},{1,509},{2,510},{3,511},{4,0},{5,1},{6,2},{7,3},{8,4},{9,5... | collective-permute-start | bytes 1966088 | tf_op jit(solution)/shard_map/ppermute | solution.py:29
  26.3 28.4 %collective-permute-start = (f32[10,4,32,128]{3,2,1,0:T(8,128)}, f32[10,4,32,128]{3,2,1,0:T(8,128)}, u32[]{:S(2)}, u32[]{:S(2)}) collective-permute-start(f32[10,4,32,128]{3,2,1,0:T(8,128)} %bitcast.9), channel_id=1, source_target_pairs={{0,4},{1,5},{2,6},{3,7},{4,8},{5,9},{6,10},{7,11},{8,12},{9,13},{1... | collective-permute-start | bytes 1966088 | tf_op jit(solution)/shard_map/ppermute | solution.py:29
  56.3 18.1 %copy-start.1 = (f32[10,12,32,128]{3,2,1,0:T(8,128)}, f32[10,12,32,128]{3,2,1,0:T(8,128)S(1)}, u32[]{:S(2)}) copy-start(f32[10,12,32,128]{3,2,1,0:T(8,128)S(1)} %pad_maximum_fusion.1.c_ref) | copy-start | bytes 5898244
  57.3 14.9 %collective-permute-start.2 = (f32[2,3840]{1,0:T(2,128)S(1)}, f32[2,3840]{1,0:T(2,128)S(1)}, u32[]{:S(2)}, u32[]{:S(2)}) collective-permute-start(f32[2,3840]{1,0:T(2,128)S(1)} %get-tuple-element.9), channel_id=1, source_target_pairs={{1,0},{2,1},{3,2},{5,4},{6,5},{7,6},{9,8},{10,9},{11,10},{13,12},{... | collective-permute-start | bytes 92168 | tf_op jit(solution)/shard_map/ppermute | solution.py:29
  61.1 11.5 %collective-permute-start.3 = (f32[2,3840]{1,0:T(2,128)S(1)}, f32[2,3840]{1,0:T(2,128)S(1)}, u32[]{:S(2)}, u32[]{:S(2)}) collective-permute-start(f32[2,3840]{1,0:T(2,128)S(1)} %get-tuple-element.10), channel_id=1, source_target_pairs={{0,1},{1,2},{2,3},{4,5},{5,6},{6,7},{8,9},{9,10},{10,11},{12,13},{... | collective-permute-start | bytes 92168 | tf_op jit(solution)/shard_map/ppermute | solution.py:29

commit v13 on v10

--- a/solution.py
+++ b/solution.py
@@ -157,7 +157,10 @@
             f1x = 0.25 * wx[j] + 0.5 * wx[j + 1] + 0.25 * wx[j + 2]
             pc, px = ring(f1c, f1x, 1, 0)
             nc, nx = ring(f1c, f1x, cells - 1, cells - 1)
-            sc_ref[c, j] = hsmooth(0.25 * pc + 0.5 * f1c + 0.25 * nc)
+            smooth_c = hsmooth(0.25 * pc + 0.5 * f1c + 0.25 * nc)
+            sc_ref[c, j] = smooth_c
+            if 0 < j < rows - 1:
+                sm_ref[c, j - 1] = smooth_c
             sx_ref[c, j] = hsmooth(0.25 * px + 0.5 * f1x + 0.25 * nx)
         return carry
 
@@ -172,8 +175,6 @@
         return ref[k + 1, j]
 
     def out_row(r, carry):
-        for c in range(sm_ref.shape[0]):
-            sm_ref[c, r] = sc_ref[c, r + 1]
         center = [comb(sc_ref, r + 1, k) for k in range(9)]
         grad_az = {}
         for k in (0, 1, 2, 3, 6, 7):

time: 69.7 us -> 69.6 us (level)
  no operation moved by 1% of the time
where the time goes in v13:
time: 69.6 us; the launch traced here: 69.3 us
  waiting for transfers between devices  37.7 us (54%)
  starting transfers between devices  12.6 us (18%)
  Pallas kernels  7.55 us (11%)
  matrix products  6.31 us (9%)
  other arithmetic  2.55 us (4%)
  between operations  1.39 us (2%)
  local copies, waits for them, and re-layouts  1.24 us (2%)
    ppermute x4, waiting for transfers between devices, shifted(): return lax.ppermute(value, ('az', 'rad'), pairs)  37.7 us
    ppermute x4, starting transfers between devices, shifted(): return lax.ppermute(value, ('az', 'rad'), pairs)  12.6 us
    pallas_call x1, Pallas kernels, stencil(): pl.pallas_call(stencil_kernel, out_shape=(shape(channels), shape(3), shap...  7.55 us
    dot_general x1, matrix products, deposit(): jnp.einsum('ls,scn->lcn', onehot, values, precision=lax.Precision.HIGHEST)  3.59 us
    dot_general x1, matrix products, placed(): jnp.einsum('jm,jn->mn', parts, sel3, preferred_element_type=jnp.float32)  1.74 us
  transfers between devices with their start and end apart: 4, of which 3 were waited for; matrix products, arithmetic and copies ran while one was open for 2% of the time, Pallas kernels for 0%

profile of v13, /device:TPU:510, one launch (start us, length us, event | category | flops | bytes accessed | tf_op | source)
XLA Modules:
  0.0 69.3 jit_solution(396379584767982687)
XLA Ops:
  1.3 0.7 %fusion.20 = s32[512]{0:T(512)S(1)} fusion(s32[512]{0:T(512)} %bitcast.22, s32[]{:T(128)S(6)} %mul.28), kind=kLoop, calls=%fused_computation.36 | loop fusion | flops 17408 | bytes 4100 | tf_op jit(solution)/shard_map/add | solution.py:41
  2.0 3.6 %fusion = f32[384,10,128]{2,0,1:T(8,128)S(1)} fusion(f32[512,9,128]{2,0,1:T(8,128)} %bitcast.20, f32[512,1,128]{2,0,1:T(8,128)} %bitcast.21, s32[512]{0:T(512)S(1)} %fusion.20, pred[512]{0:T(512)(128)(4,1)S(1)} %iota_compare_fusion.2), kind=kOutput, calls=%fused_computation | convolution fusion | flops 3020947456 | bytes 4590080 | tf_op jit(solution)/shard_map/ls,scn->lcn/dot_general | solution.py:35
  5.6 0.0 copy-start.1
  5.6 1.2 %fusion.29 = (f32[10,4,32,128]{3,2,1,0:T(8,128)}, f32[10,4,32,128]{3,2,1,0:T(8,128)}) fusion(f32[10,12,32,128]{3,2,1,0:T(8,128)S(1)} %bitcast.17), kind=kLoop, calls=%fused_computation.54 | loop fusion | bytes 2621440 | tf_op jit(solution)/shard_map/slice | solution.py:73
  6.8 6.4 %collective-permute-start = (f32[10,4,32,128]{3,2,1,0:T(8,128)}, f32[10,4,32,128]{3,2,1,0:T(8,128)S(1)}, u32[]{:S(2)}, u32[]{:S(2)}) collective-permute-start(f32[10,4,32,128]{3,2,1,0:T(8,128)} %get-tuple-element.6), channel_id=1, source_target_pairs={{0,4},{1,5},{2,6},{3,7},{4,8},{5,9},{6,10},{7,11},{8,12},{9,13},{1... | collective-permute-start | bytes 1966088 | tf_op jit(solution)/shard_map/ppermute | solution.py:29
  13.2 1.9 %collective-permute-start.1 = (f32[10,4,32,128]{3,2,1,0:T(8,128)}, f32[10,4,32,128]{3,2,1,0:T(8,128)S(1)}, u32[]{:S(2)}, u32[]{:S(2)}) collective-permute-start(f32[10,4,32,128]{3,2,1,0:T(8,128)} %get-tuple-element.7), channel_id=1, source_target_pairs={{0,508},{1,509},{2,510},{3,511},{4,0},{5,1},{6,2},{7,3},{8,4},{9,5... | collective-permute-start | bytes 1966088 | tf_op jit(solution)/shard_map/ppermute | solution.py:29
  15.1 0.0 copy-done.1
  15.1 0.1 iota_compare_fusion.1
  15.2 0.6 fusion.23.xmask_ref
  15.8 11.7 %collective-permute-done = f32[10,4,32,128]{3,2,1,0:T(8,128)S(1)} collective-permute-done((f32[10,4,32,128]{3,2,1,0:T(8,128)}, f32[10,4,32,128]{3,2,1,0:T(8,128)S(1)}, u32[]{:S(2)}, u32[]{:S(2)}) %collective-permute-start) | collective-permute-done | bytes 655392 | tf_op jit(solution)/shard_map/ppermute | solution.py:29
  27.4 15.1 %collective-permute-done.1 = f32[10,4,32,128]{3,2,1,0:T(8,128)S(1)} collective-permute-done((f32[10,4,32,128]{3,2,1,0:T(8,128)}, f32[10,4,32,128]{3,2,1,0:T(8,128)S(1)}, u32[]{:S(2)}, u32[]{:S(2)}) %collective-permute-start.1) | collective-permute-done | bytes 655392 | tf_op jit(solution)/shard_map/ppermute | solution.py:29
  42.6 0.4 slice_add_fusion.1
  42.9 0.2 pad_maximum_fusion.c_ref
  43.1 0.0 copy-start
  43.1 1.0 %fusion.28 = f32[4,3840]{1,0:T(4,128)S(1)} fusion(f32[3840,128]{1,0:T(8,128)S(1)} %bitcast.16, s32[4]{0:T(128)S(1)} %copy-done.1), kind=kOutput, calls=%fused_computation.51 | convolution fusion | flops 23593472 | bytes 2027536 | tf_op jit(solution)/shard_map/jn,mn->jm/dot_general | solution.py:78
  44.1 1.9 %collective-permute-start.2 = (f32[2,3840]{1,0:T(2,128)S(1)}, f32[2,3840]{1,0:T(2,128)S(1)}, u32[]{:S(2)}, u32[]{:S(2)}) collective-permute-start(f32[2,3840]{1,0:T(2,128)S(1)} %get-tuple-element.11), channel_id=1, source_target_pairs={{1,0},{2,1},{3,2},{5,4},{6,5},{7,6},{9,8},{10,9},{11,10},{13,12},{... | collective-permute-start | bytes 92168 | tf_op jit(solution)/shard_map/ppermute | solution.py:29
  46.1 2.4 %collective-permute-start.3 = (f32[2,3840]{1,0:T(2,128)S(1)}, f32[2,3840]{1,0:T(2,128)S(1)}, u32[]{:S(2)}, u32[]{:S(2)}) collective-permute-start(f32[2,3840]{1,0:T(2,128)S(1)} %get-tuple-element.12), channel_id=1, source_target_pairs={{0,1},{1,2},{2,3},{4,5},{5,6},{6,7},{8,9},{9,10},{10,11},{12,13},{... | collective-permute-start | bytes 92168 | tf_op jit(solution)/shard_map/ppermute | solution.py:29
  48.5 0.6 multiply_divide_fusion
  49.1 0.0 collective-permute-done.2
  49.1 10.9 %collective-permute-done.3 = f32[2,3840]{1,0:T(2,128)S(1)} collective-permute-done((f32[2,3840]{1,0:T(2,128)S(1)}, f32[2,3840]{1,0:T(2,128)S(1)}, u32[]{:S(2)}, u32[]{:S(2)}) %collective-permute-start.3) | collective-permute-done | bytes 30752 | tf_op jit(solution)/shard_map/ppermute | solution.py:29
  60.0 0.1 reduce-precision_convert_fusion.1
  60.1 1.7 %fusion.9 = f32[3840,128]{1,0:T(8,128)} fusion(bf16[4,3840]{1,0:T(4,128)(2,1)S(1)} %get-tuple-element.10, bf16[4,3840]{1,0:T(4,128)(2,1)S(1)} %get-tuple-element.9, bf16[4,3840]{1,0:T(4,128)(2,1)S(1)} %get-tuple-element.8, pred[4,128]{1,0:T(4,128)(4,1)S(1)} %iota_compare_fusion.1), kind=kOutput, calls=%fused_computation.10 | convolution fusion | flops 12079104 | bytes 2058752 | tf_op jit(solution)/shard_map/jm,jn->mn/dot_general | solution.py:68
  61.8 0.0 copy-done
  61.8 7.5 %shard_map.85 = (f32[10,8,32,128]{3,2,1,0:T(8,128)}, f32[3,8,32,128]{3,2,1,0:T(8,128)}, f32[6,8,32,128]{3,2,1,0:T(8,128)}) custom-call(f32[10,12,32,128]{3,2,1,0:T(8,128)} %copy-done, f32[10,12,32,128]{3,2,1,0:T(8,128)} %bitcast.19, f32[1,128]{1,0:T(1,128)} %get-tuple-element.13.scale_ref, f32[1,128]{1,0:T(1,128)} %get-tuple-element.14.recip_ref, ...), custom_call_target="tpu_custom_call" | custom-call | tf_op jit(solution)/shard_map/pallas_call | solution.py:208
  (3 shorter events, 0.1 us)
Async XLA Ops:
  5.6 9.5 %copy-start.1 = (s32[4]{0:T(128)S(1)}, s32[4]{0:T(128)}, u32[]{:S(2)}) copy-start(s32[4]{0:T(128)} %constant.74.clone) | copy-start | bytes 52
  6.8 20.6 %collective-permute-start = (f32[10,4,32,128]{3,2,1,0:T(8,128)}, f32[10,4,32,128]{3,2,1,0:T(8,128)S(1)}, u32[]{:S(2)}, u32[]{:S(2)}) collective-permute-start(f32[10,4,32,128]{3,2,1,0:T(8,128)} %get-tuple-element.6), channel_id=1, source_target_pairs={{0,4},{1,5},{2,6},{3,7},{4,8},{5,9},{6,10},{7,11},{8,12},{9,13},{1... | collective-permute-start | bytes 1966088 | tf_op jit(solution)/shard_map/ppermute | solution.py:29
  13.2 29.4 %collective-permute-start.1 = (f32[10,4,32,128]{3,2,1,0:T(8,128)}, f32[10,4,32,128]{3,2,1,0:T(8,128)S(1)}, u32[]{:S(2)}, u32[]{:S(2)}) collective-permute-start(f32[10,4,32,128]{3,2,1,0:T(8,128)} %get-tuple-element.7), channel_id=1, source_target_pairs={{0,508},{1,509},{2,510},{3,511},{4,0},{5,1},{6,2},{7,3},{8,4},{9,5... | collective-permute-start | bytes 1966088 | tf_op jit(solution)/shard_map/ppermute | solution.py:29
  43.1 18.7 %copy-start = (f32[10,12,32,128]{3,2,1,0:T(8,128)}, f32[10,12,32,128]{3,2,1,0:T(8,128)S(1)}, u32[]{:S(2)}) copy-start(f32[10,12,32,128]{3,2,1,0:T(8,128)S(1)} %pad_maximum_fusion.c_ref) | copy-start | bytes 5898244
  44.1 4.9 %collective-permute-start.2 = (f32[2,3840]{1,0:T(2,128)S(1)}, f32[2,3840]{1,0:T(2,128)S(1)}, u32[]{:S(2)}, u32[]{:S(2)}) collective-permute-start(f32[2,3840]{1,0:T(2,128)S(1)} %get-tuple-element.11), channel_id=1, source_target_pairs={{1,0},{2,1},{3,2},{5,4},{6,5},{7,6},{9,8},{10,9},{11,10},{13,12},{... | collective-permute-start | bytes 92168 | tf_op jit(solution)/shard_map/ppermute | solution.py:29
  46.1 13.9 %collective-permute-start.3 = (f32[2,3840]{1,0:T(2,128)S(1)}, f32[2,3840]{1,0:T(2,128)S(1)}, u32[]{:S(2)}, u32[]{:S(2)}) collective-permute-start(f32[2,3840]{1,0:T(2,128)S(1)} %get-tuple-element.12), channel_id=1, source_target_pairs={{0,1},{1,2},{2,3},{4,5},{5,6},{6,7},{8,9},{9,10},{10,11},{12,13},{... | collective-permute-start | bytes 92168 | tf_op jit(solution)/shard_map/ppermute | solution.py:29
